TPU v7x, 128 devices: a whole 4x4x4 slice. The times are simulated.
128 devices in a mesh: dp: 4 (over z_lo, core), tensor: 32 (over y, x, z_hi).
Axes of the slice: x: 4, y: 4, z: 4 (z_hi: 2, z_lo: 2; z = z_hi * 2 + z_lo), core: 2. Of those that a mesh axis runs over, the one named last changes fastest.
Arguments:
- stream: bfloat16 [6144, 2560], P(('dp', 'tensor')), may hold values from -26 to 26
- lengths: int32 [4, 6], P('dp'), may hold values from 16 to 768, as said below
- page_table: int32 [384], P('dp'), may hold values from 0 to 383, as said below
- request_prompt: int32 [64], P('dp'), may hold values from 0 to 23
- attn_gain: bfloat16 [2560], replicated, may hold values from 0.099609375 to 1.8984375
- query_gain: bfloat16 [128], replicated, may hold values from 0.5 to 10, as said below
- key_gain: bfloat16 [128], replicated, may hold values from 0.5 to 10, as said below
- mlp_gain: bfloat16 [2560], replicated, may hold values from 0.099609375 to 1.8984375
- w_query: bfloat16 [2560, 4096], P(None, 'tensor'), may hold values from -0.125 to 0.125
- key_value_weight: bfloat16 [2560, 2048], P(None, 'tensor'), may hold values from -0.125 to 0.125
- w_out: bfloat16 [4096, 2560], P('tensor'), may hold values from -0.5 to 0.5
- w_gate: bfloat16 [2560, 9728], P(None, 'tensor'), may hold values from -0.125 to 0.125
- w_up: bfloat16 [2560, 9728], P(None, 'tensor'), may hold values from -0.125 to 0.125
- w_down: bfloat16 [9728, 2560], P('tensor'), may hold values from -0.0625 to 0.0625
Outputs:
- layer_out: bfloat16 [6144, 2560], P(('dp', 'tensor'))
- paged_key_value_cache: bfloat16 [384, 16, 2048], P('dp', None, 'tensor')
- request_state: bfloat16 [64, 2560], P('dp', 'tensor')
Inputs may be any that keep to these rules, and one draw needn't show every extreme that they name: Every length is a multiple of 16; each batch's lengths add up to 1536, and the largest length of each batch is exactly 768. page_table is a permutation of all global slots; slot v belongs to owner v // 96, and each batch writes exactly 24 pages to each owner. `query_gain`: positive gains. `key_gain`: positive gains.
All inputs are finite; a program needn't handle non-finite values.
Results may differ from a plain program's by a relative error of at most 0.02.
The roundings to bfloat16 on the way count: a program that leaves them out, or rounds other values in their place, can miss the bound.
Values may be sent and summed in bfloat16 or wider, within the bound.
No kernel may reach another device: no remote copies, remote signals or barrier semaphores. Data moves between devices by JAX's collectives and lax.ppermute only.
A program may use at most 128 MiB of HBM per device.

v0:
```python
import math

import jax
import jax.numpy as jnp
from jax import lax
from jax.sharding import PartitionSpec as P

KEY_VALUE_HEADS = 8
HEAD_SIZE = 128
PAGE_TOKENS = 16


epsilon = 1e-06
rope_base = 1000000.0


def partner_2(value, axis, bit):
    mask = 2**bit
    pairs = [(source, source ^ mask) for source in range(lax.axis_size(axis))]
    return lax.ppermute(value, axis, pairs)


def row_norm(inputs, gain):
    inputs = inputs.astype(jnp.float32)
    scale = lax.rsqrt(jnp.mean(inputs * inputs, axis=-1, keepdims=True) + epsilon)
    return inputs * scale * gain.astype(jnp.float32)


def rotate(inputs, position):
    half_dim = inputs.shape[-1] // 2
    frequency = rope_base ** (-2.0 * jnp.arange(half_dim, dtype=jnp.float32) / inputs.shape[-1])
    angles = position.astype(jnp.float32)[:, None] * frequency[None, :]
    cosine = jnp.cos(angles)[:, None, :]
    sine_part = jnp.sin(angles)[:, None, :]
    front = inputs[..., :half_dim]
    second = inputs[..., half_dim:]
    return jnp.concatenate(
        [front * cosine - second * sine_part, second * cosine + front * sine_part], axis=-1
    )


def prompt_layout(lengths_row, token_count):
    prompt_ends = jnp.cumsum(lengths_row)
    prompt_starts = prompt_ends - lengths_row
    row_ids = jnp.arange(token_count, dtype=jnp.int32)
    prompt = jnp.sum((row_ids[:, None] >= prompt_ends[None, :]).astype(jnp.int32), axis=1)
    inside = (row_ids[:, None] >= prompt_starts[None, :]) & (
        row_ids[:, None] < prompt_ends[None, :]
    )
    offset = jnp.sum(jnp.where(inside, prompt_starts[None, :], 0), axis=1)
    return (prompt, row_ids - offset, prompt_starts, prompt_ends)


def per_device(
    stream,
    lengths,
    page_table,
    request_prompt,
    attn_gain,
    query_gain,
    key_gain,
    mlp_gain,
    w_query,
    key_value_weight,
    w_out,
    w_gate,
    w_up,
    w_down,
):
    tok_dev = stream.shape[0]
    tensor_element_count = lax.axis_size("tensor")
    token_count = tok_dev * tensor_element_count
    my_index = lax.axis_index("tensor")
    heads_dev = w_query.shape[1] // HEAD_SIZE
    query_cols = heads_dev * HEAD_SIZE
    prompt, position, prompt_starts, prompt_ends = prompt_layout(lengths[0], token_count)
    portion = lax.all_gather(
        row_norm(stream, attn_gain).astype(jnp.bfloat16), "tensor", axis=0, tiled=True
    )
    joined = jnp.concatenate(
        [
            jnp.dot(portion, w_query, preferred_element_type=jnp.float32),
            jnp.dot(portion, key_value_weight, preferred_element_type=jnp.float32),
        ],
        axis=1,
    )
    queries = joined[:, :query_cols].reshape(token_count, heads_dev, HEAD_SIZE)
    kv_part = joined[:, query_cols:].astype(jnp.bfloat16)
    key_value_group = tensor_element_count // KEY_VALUE_HEADS
    for bit_id in range(key_value_group.bit_length() - 1):
        partner = partner_2(kv_part, "tensor", bit_id)
        upper_half = my_index // 2**bit_id % 2
        kv_part = jnp.where(
            upper_half == 1,
            jnp.concatenate([partner, kv_part], axis=1),
            jnp.concatenate([kv_part, partner], axis=1),
        )
    key_flat = rotate(row_norm(kv_part[:, None, :HEAD_SIZE], key_gain), position).astype(
        jnp.bfloat16
    )[:, 0, :]
    value_matrix_rows = kv_part[:, HEAD_SIZE:]
    q_rot = rotate(row_norm(queries, query_gain), position).astype(jnp.bfloat16)
    piece_cols = key_value_weight.shape[1]
    head_rows = jnp.concatenate([key_flat, value_matrix_rows], axis=1)
    own_cols = lax.dynamic_slice_in_dim(
        head_rows, my_index % key_value_group * piece_cols, piece_cols, 1
    )
    page_count = token_count // PAGE_TOKENS
    page_rows = own_cols.reshape(page_count, PAGE_TOKENS, piece_cols)
    group_count = lax.axis_size("dp")
    capacity = page_count // group_count
    owners = page_table // page_count
    slot_ids = page_table % page_count
    hits = (owners[:, None] == jnp.arange(group_count, dtype=jnp.int32)[None, :]).astype(jnp.int32)
    order_in = jnp.sum((jnp.cumsum(hits, axis=0) - hits) * hits, axis=1)
    buffer_pos = owners * capacity + order_in
    source = (
        jnp.zeros((page_count,), jnp.int32)
        .at[buffer_pos]
        .set(jnp.arange(page_count, dtype=jnp.int32))
    )
    send_pages = page_rows[source].reshape(group_count, capacity, PAGE_TOKENS, piece_cols)
    send_slots = slot_ids[source].reshape(group_count, capacity)
    got_pages, got_slots = (
        lax.all_to_all(send_pages, "dp", split_axis=0, concat_axis=0, tiled=True),
        lax.all_to_all(send_slots, "dp", split_axis=0, concat_axis=0, tiled=True),
    )
    paged_key_value_cache = (
        jnp.zeros((page_count, PAGE_TOKENS, piece_cols), jnp.bfloat16)
        .at[got_slots.reshape(-1)]
        .set(got_pages.reshape(page_count, PAGE_TOKENS, piece_cols))
    )
    block_rows = min(512, token_count)
    block_total = token_count // block_rows
    score_scale = math.sqrt(HEAD_SIZE)
    all_ids = jnp.arange(token_count, dtype=jnp.int32)
    local_ids = jnp.arange(block_rows, dtype=jnp.int32)

    def dense_block(block_index):
        first_row = block_index * block_rows
        q_block = lax.dynamic_slice_in_dim(q_rot, first_row, block_rows, 0)
        q_prompt = lax.dynamic_slice_in_dim(prompt, first_row, block_rows, 0)
        row_ids = first_row + local_ids
        scores = (
            jnp.einsum("qhd,kd->hqk", q_block, key_flat, preferred_element_type=jnp.float32)
            / score_scale
        )
        allowed = ((q_prompt[:, None] == prompt[None, :]) & (row_ids[:, None] >= all_ids[None, :]))[
            None
        ]
        peak = jnp.max(jnp.where(allowed, scores, -jnp.inf), axis=2, keepdims=True)
        weight = jnp.where(allowed, jnp.exp(scores - peak), 0.0)
        total_weight = jnp.sum(weight, axis=2, keepdims=True)
        running = jnp.einsum(
            "hqk,kd->hqd",
            weight.astype(jnp.bfloat16),
            value_matrix_rows,
            preferred_element_type=jnp.float32,
        )
        return (running / total_weight).astype(jnp.bfloat16)

    block_ids = jnp.arange(block_total, dtype=jnp.int32)
    blocks_out = lax.map(dense_block, block_ids)
    attn = jnp.transpose(blocks_out, (0, 2, 1, 3)).reshape(token_count, query_cols)
    attn_sum = lax.psum_scatter(
        jnp.dot(attn, w_out, preferred_element_type=jnp.float32).astype(jnp.bfloat16),
        "tensor",
        scatter_dimension=0,
        tiled=True,
    ).astype(jnp.float32)
    resid = (stream.astype(jnp.float32) + attn_sum).astype(jnp.bfloat16)
    portion = lax.all_gather(
        row_norm(resid, mlp_gain).astype(jnp.bfloat16), "tensor", axis=0, tiled=True
    )
    gate_rows = jnp.dot(portion, w_gate, preferred_element_type=jnp.float32)
    upward = jnp.dot(portion, w_up, preferred_element_type=jnp.float32)
    hidden = (jax.nn.silu(gate_rows) * upward).astype(jnp.bfloat16)
    mlp_sum = lax.psum_scatter(
        jnp.dot(hidden, w_down, preferred_element_type=jnp.float32).astype(jnp.bfloat16),
        "tensor",
        scatter_dimension=0,
        tiled=True,
    ).astype(jnp.float32)
    layer_out = (resid.astype(jnp.float32) + mlp_sum).astype(jnp.bfloat16)
    my_rows = my_index * tok_dev + jnp.arange(tok_dev, dtype=jnp.int32)
    select = ((prompt_ends - 1)[:, None] == my_rows[None, :]).astype(jnp.bfloat16)
    end_terms = jnp.dot(select, layer_out, preferred_element_type=jnp.float32)
    end_rows = lax.psum_scatter(
        end_terms.astype(jnp.bfloat16), "tensor", scatter_dimension=1, tiled=True
    )
    table = lax.all_gather(end_rows, "dp", axis=0, tiled=True)
    pick = (request_prompt[:, None] == jnp.arange(table.shape[0], dtype=jnp.int32)[None, :]).astype(
        jnp.bfloat16
    )
    request_state = jnp.dot(pick, table, preferred_element_type=jnp.float32).astype(jnp.bfloat16)
    return (layer_out, paged_key_value_cache, request_state)


def solution(mesh):
    placed = (
        P(("dp", "tensor"), None),
        P("dp", None),
        P("dp"),
        P("dp"),
        P(),
        P(),
        P(),
        P(),
        P(None, "tensor"),
        P(None, "tensor"),
        P("tensor", None),
        P(None, "tensor"),
        P(None, "tensor"),
        P("tensor", None),
    )
    return jax.shard_map(
        per_device,
        mesh=mesh,
        in_specs=placed,
        out_specs=(P(("dp", "tensor"), None), P("dp", None, "tensor"), P("dp", "tensor")),
        check_vma=False,
    )
```

profile of v0, /device:TPU:27, one launch (start us, length us, event | category | flops | bytes accessed | tf_op | source)
XLA Modules:
  0.0 961.0 jit_solution(15160185584792332749)
XLA Ops:
  7.2 1.2 fusion.39
  9.1 1.8 fusion.41
  14.5 98.5 %all-gather.4.cloned.1.call-done = bf16[1536,2560]{1,0:T(8,128)(2,1)} async-done(((bf16[48,2560]{1,0:T(8,128)(2,1)}), bf16[1536,2560]{1,0:T(8,128)(2,1)}) %all-gather.4.cloned.1.call-update) | async-done | bytes 7864336 | tf_op jit(solution)/shard_map/all_gather | solution.py:77
  113.0 5.9 convolution_convert_fusion.3
  119.0 2.7 multiply_reduce_fusion
  121.8 3.7 collective-permute-done
  125.5 1.6 collective-permute-start.1
  127.3 6.8 collective-permute-done.1
  135.5 3.0 fusion.58
  139.5 1.8 pad_maximum_fusion
  141.3 18.3 %while.11 = (s32[]{:T(128)}, bf16[3,1,512,128]{3,2,1,0:T(8,128)(2,1)S(1)}, s32[3]{0:T(128)S(1)}, s32[1536]{0:T(1024)S(1)}, bf16[1536,1,128]{0,2,1:T(8,128)(2,1)}...) while((s32[]{:T(128)}, ...), condition=%wide.region_9.10_spmd.clone, body=%wide.region_6.9_spmd.clone.sunk | while | flops 416939520 | bytes 12107995 | solution.py:163
  142.6 2.2 select_reduce_fusion.4
  145.9 1.5 fusion.95
  148.7 2.2 select_reduce_fusion.4
  151.9 1.5 fusion.95
  154.8 2.2 select_reduce_fusion.4
  158.0 1.5 fusion.95
  159.5 5.3 convolution_convert_fusion.1
  165.5 239.6 %reduce-scatter.6.cloned.1.call-done = bf16[48,2560]{1,0:T(8,128)(2,1)} async-done(((bf16[1536,2560]{1,0:T(8,128)(2,1)}), bf16[48,2560]{1,0:T(8,128)(2,1)}) %reduce-scatter.6.cloned.1.call-update) | async-done | bytes 245776 | tf_op jit(solution)/shard_map/reduce_scatter | solution.py:165
  406.2 1.8 fusion.45
  408.2 100.7 %all-gather.6.cloned.1.call-done = bf16[1536,2560]{1,0:T(8,128)(2,1)} async-done(((bf16[48,2560]{1,0:T(8,128)(2,1)}), bf16[1536,2560]{1,0:T(8,128)(2,1)}) %all-gather.6.cloned.1.call-update) | async-done | bytes 7864336 | tf_op jit(solution)/shard_map/all_gather | solution.py:172
  509.0 7.5 fusion.70
  516.4 13.4 %convolution_convert_fusion = bf16[1536,2560]{1,0:T(8,128)(2,1)} fusion(bf16[304,2560]{1,0:T(8,128)(2,1)S(1)} %copy-done, bf16[1536,2560]{1,0:T(8,128)(2,1)} %all-gather.6.cloned.1.call-done, bf16[2560,304]{0,1:T(8,128)(2,1)} %param.28, f32[1536,304]{0,1:T(8,128)} %fusion.70), kind=kOutput, calls=%fused_computation.25 | convolution fusion | flops 4788240384 | bytes 20709376 | tf_op jit(solution)/shard_map/dot_general | solution.py:179
  531.8 1.2 gather_fusion
  533.7 4.6 all-to-all-start
  538.3 3.4 all-to-all-done
  545.0 3.6 all-to-all-start.1
  548.6 219.8 %reduce-scatter.8.cloned.1.call-done = bf16[48,2560]{1,0:T(8,128)(2,1)} async-done(((bf16[1536,2560]{1,0:T(8,128)(2,1)}), bf16[48,2560]{1,0:T(8,128)(2,1)}) %reduce-scatter.8.cloned.1.call-update) | async-done | bytes 245776 | tf_op jit(solution)/shard_map/reduce_scatter | solution.py:178
  769.6 1.2 copy.37
  771.2 3.5 scatter_fusion
  775.7 146.6 %reduce-scatter.10.cloned.1.call-done = bf16[80,6]{1,0:T(8,128)(2,1)} async-done(((bf16[2560,6]{1,0:T(8,128)(2,1)}), bf16[80,6]{1,0:T(8,128)(2,1)}) %reduce-scatter.10.cloned.1.call-update) | async-done | bytes 976
  923.1 30.6 %all-gather = bf16[4,6,80]{2,1,0:T(8,128)(2,1)S(1)} all-gather(bf16[1,6,80]{2,1,0:T(8,128)(2,1)S(1)} %bitcast.90), channel_id=1, replica_groups=mesh['dp'=4,'tensor'=32] {'dp'}, dimensions={0}, use_global_device_ids=true | all-gather | bytes 4800 | tf_op jit(solution)/shard_map/all_gather | solution.py:191
  (105 shorter events, 24.4 us)
Async XLA Ops:
  7.2 509.3 %copy-start = (bf16[304,2560]{1,0:T(8,128)(2,1)S(1)}, bf16[304,2560]{1,0:T(8,128)(2,1)}, u32[]{:S(2)}) copy-start(bf16[304,2560]{1,0:T(8,128)(2,1)} %param.29) | copy-start | bytes 4669444
  7.2 105.8 %all-gather.4.cloned.1.call-start = ((), (), s32[]{:S(2)}) async-start(), calls=%async_computation.5 | async-start | bytes 8110080 | tf_op jit(solution)/shard_map/all_gather | solution.py:77
  10.9 394.1 %reduce-scatter.6.cloned.1.call-start = ((), (), s32[]{:S(2)}) async-start(), calls=%async_computation.6 | async-start | bytes 8110080 | tf_op jit(solution)/shard_map/reduce_scatter | solution.py:165
  14.5 104.5 %copy-start.6 = (bf16[2560,128]{1,0:T(8,128)(2,1)S(1)}, bf16[2560,128]{1,0:T(8,128)(2,1)}, u32[]{:S(2)}) copy-start(bf16[2560,128]{1,0:T(8,128)(2,1)} %param.24) | copy-start | bytes 1966084
  113.0 6.0 copy-start.1
  118.8 6.6 collective-permute-start
  125.5 8.5 collective-permute-start.1
  135.5 5.8 copy-start.5
  141.3 18.3 %copy-start.7 = (bf16[128,2560]{1,0:T(8,128)(2,1)S(1)}, bf16[128,2560]{1,0:T(8,128)(2,1)}, u32[]{:S(2)}) copy-start(bf16[128,2560]{1,0:T(8,128)(2,1)} %param.26) | copy-start | bytes 1966084
  142.6 3.2 copy-start.8
  148.7 3.2 copy-start.8
  154.8 3.2 copy-start.8
  164.8 0.7 copy-start.9
  164.8 240.3 %copy-start.2 = (bf16[48,2560]{1,0:T(8,128)(2,1)S(1)}, bf16[48,2560]{1,0:T(8,128)(2,1)}, u32[]{:S(2)}) copy-start(bf16[48,2560]{1,0:T(8,128)(2,1)} %param.16) | copy-start | bytes 737284
  164.8 344.1 %all-gather.6.cloned.1.call-start = ((), (), s32[]{:S(2)}) async-start(), calls=%async_computation.7 | async-start | bytes 8110080 | tf_op jit(solution)/shard_map/all_gather | solution.py:172
  408.0 360.4 %reduce-scatter.8.cloned.1.call-start = ((), (), s32[]{:S(2)}) async-start(), calls=%async_computation.8 | async-start | bytes 8110080 | tf_op jit(solution)/shard_map/reduce_scatter | solution.py:178
  529.8 0.7 copy-start.10
  530.4 237.9 %copy-start.3 = (bf16[48,2560]{1,0:T(8,128)(2,1)S(1)}, bf16[48,2560]{1,0:T(8,128)(2,1)}, u32[]{:S(2)}) copy-start(bf16[48,2560]{1,0:T(8,128)(2,1)} %reduce-scatter.6.cloned.1.call-done) | copy-start | bytes 737284
  533.7 8.0 all-to-all-start
  544.0 409.8 %copy-start.11 = (s32[16]{0:T(128)S(1)}, s32[16]{0:T(128)}, u32[]{:S(2)}) copy-start(s32[16]{0:T(128)} %param.19) | copy-start | bytes 196
  545.0 225.8 %all-to-all-start.1 = ((bf16[4,2,12288]{2,1,0:T(2,128)(2,1)}), bf16[4,2,12288]{2,1,0:T(2,128)(2,1)S(1)}, u32[]{:S(2)}, u32[]{:S(2)}) async-start(bf16[4,2,12288]{2,1,0:T(2,128)(2,1)} %reshape.438), calls=%async_computation.3 | async-start | bytes 393216 | tf_op jit(solution)/shard_map/all_to_all | solution.py:125
  548.6 373.7 %reduce-scatter.10.cloned.1.call-start = ((), (), s32[]{:S(2)}) async-start(), calls=%async_computation.9 | async-start | bytes 675840
  769.4 185.1 %copy-start.4 = (bf16[48,2560]{1,0:T(8,128)(2,1)}, bf16[48,2560]{1,0:T(8,128)(2,1)S(1)}, u32[]{:S(2)}) copy-start(bf16[48,2560]{1,0:T(8,128)(2,1)S(1)} %fusion.46) | copy-start | bytes 737284
Sparse Core Ops, SparseCore 0:
  11.6 101.3 all-gather.3
  165.0 240.0 reduce-scatter.5
  408.7 100.1 all-gather.5
  529.9 238.3 reduce-scatter.7
  770.9 151.3 reduce-scatter.9
where the time goes:
time: 974 us; the launch traced here: 961 us
  waiting for transfers between devices  819 us (84%)
  matrix products  46.6 us (5%)
  blocking collectives  30.6 us (3%)
  other arithmetic  20.9 us (2%)
  local copies, waits for them, and re-layouts  17.2 us (2%)
  between operations  14.1 us (1%)
  starting transfers between devices  10.3 us (1%)
    reduce_scatter x1, waiting for transfers between devices, per_device(): lax.psum_scatter(jnp.dot(attn, w_out, preferred_element_type=jnp.float32)...  240 us
    reduce_scatter x1, waiting for transfers between devices, per_device(): lax.psum_scatter(jnp.dot(hidden, w_down, preferred_element_type=jnp.float...  220 us
    unnamed x6, waiting for transfers between devices  147 us
    all_gather x1, waiting for transfers between devices, per_device(): lax.all_gather(row_norm(resid, mlp_gain).astype(jnp.bfloat16), 'tensor',...  101 us
    all_gather x1, waiting for transfers between devices, per_device(): lax.all_gather(row_norm(stream, attn_gain).astype(jnp.bfloat16), 'tensor'...  98.5 us
    all_gather x1, blocking collectives, per_device(): table = lax.all_gather(end_rows, 'dp', axis=0, tiled=True)  30.6 us
  transfers between devices with their start and end apart: 9, of which 8 were waited for; matrix products, arithmetic and copies ran while one was open for 2% of the time, Pallas kernels for 0%

commit v1 on v0

--- a/solution.py
+++ b/solution.py
@@ -18,6 +18,12 @@
     mask = 2**bit
     pairs = [(source, source ^ mask) for source in range(lax.axis_size(axis))]
     return lax.ppermute(value, axis, pairs)
+
+
+def scatter_sum(partial, parts):
+    pieces = partial.reshape((parts, partial.shape[0] // parts) + partial.shape[1:])
+    got = lax.all_to_all(pieces, "tensor", 0, 0, tiled=True)
+    return jnp.sum(got.astype(jnp.float32), axis=0)
 
 
 def row_norm(inputs, gain):
@@ -162,12 +168,10 @@
     block_ids = jnp.arange(block_total, dtype=jnp.int32)
     blocks_out = lax.map(dense_block, block_ids)
     attn = jnp.transpose(blocks_out, (0, 2, 1, 3)).reshape(token_count, query_cols)
-    attn_sum = lax.psum_scatter(
+    attn_sum = scatter_sum(
         jnp.dot(attn, w_out, preferred_element_type=jnp.float32).astype(jnp.bfloat16),
-        "tensor",
-        scatter_dimension=0,
-        tiled=True,
-    ).astype(jnp.float32)
+        tensor_element_count,
+    )
     resid = (stream.astype(jnp.float32) + attn_sum).astype(jnp.bfloat16)
     portion = lax.all_gather(
         row_norm(resid, mlp_gain).astype(jnp.bfloat16), "tensor", axis=0, tiled=True
@@ -175,18 +179,19 @@
     gate_rows = jnp.dot(portion, w_gate, preferred_element_type=jnp.float32)
     upward = jnp.dot(portion, w_up, preferred_element_type=jnp.float32)
     hidden = (jax.nn.silu(gate_rows) * upward).astype(jnp.bfloat16)
-    mlp_sum = lax.psum_scatter(
+    mlp_sum = scatter_sum(
         jnp.dot(hidden, w_down, preferred_element_type=jnp.float32).astype(jnp.bfloat16),
-        "tensor",
-        scatter_dimension=0,
-        tiled=True,
-    ).astype(jnp.float32)
+        tensor_element_count,
+    )
     layer_out = (resid.astype(jnp.float32) + mlp_sum).astype(jnp.bfloat16)
     my_rows = my_index * tok_dev + jnp.arange(tok_dev, dtype=jnp.int32)
     select = ((prompt_ends - 1)[:, None] == my_rows[None, :]).astype(jnp.bfloat16)
     end_terms = jnp.dot(select, layer_out, preferred_element_type=jnp.float32)
-    end_rows = lax.psum_scatter(
-        end_terms.astype(jnp.bfloat16), "tensor", scatter_dimension=1, tiled=True
+    end_blocks = end_terms.astype(jnp.bfloat16).reshape(
+        end_terms.shape[0], tensor_element_count, -1
+    )
+    end_rows = scatter_sum(jnp.transpose(end_blocks, (1, 0, 2)), tensor_element_count)[0].astype(
+        jnp.bfloat16
     )
     table = lax.all_gather(end_rows, "dp", axis=0, tiled=True)
     pick = (request_prompt[:, None] == jnp.arange(table.shape[0], dtype=jnp.int32)[None, :]).astype(

time: 974 us -> 581 us (0.60)
  waiting for transfers between devices: 819 us -> 427 us
  starting transfers between devices: 10.3 us -> 35.2 us
  blocking collectives: 30.6 us -> 6.49 us
    reduce_scatter x2 -> x0, waiting for transfers between devices: 459 us -> none  [the longest x1 240 us: per_device(): lax.psum_scatter(jnp.dot(attn, w_out, preferred_element_type=jnp.float32)...]
    all_to_all x0 -> x3, waiting for transfers between devices: none -> 224 us  [scatter_sum(): got = lax.all_to_all(pieces, 'tensor', 0, 0, tiled=True)]
    unnamed x6 -> x2, waiting for transfers between devices: 147 us -> 0.03 us
    all_gather x1, blocking collectives: 30.6 us -> 6.49 us  [per_device(): table = lax.all_gather(end_rows, 'dp', axis=0, tiled=True)]
    all_to_all x0 -> x3, starting transfers between devices: none -> 22.2 us  [scatter_sum(): got = lax.all_to_all(pieces, 'tensor', 0, 0, tiled=True)]
  transfers between devices with their start and end apart: 9 -> 9, of which waited for: 8 -> 7; matrix products, arithmetic and copies ran while one was open for 2% -> 8% of each run, Pallas kernels for 0% -> 0%
where the time goes in v1:
time: 581 us; the launch traced here: 576 us
  waiting for transfers between devices  427 us (73%)
  matrix products  49.1 us (8%)
  starting transfers between devices  35.2 us (6%)
  other arithmetic  26.4 us (5%)
  local copies, waits for them, and re-layouts  15.7 us (3%)
  between operations  14.5 us (2%)
  blocking collectives  6.49 us (1%)
    all_to_all x3, waiting for transfers between devices, scatter_sum(): got = lax.all_to_all(pieces, 'tensor', 0, 0, tiled=True)  224 us
    all_gather x1, waiting for transfers between devices, per_device(): lax.all_gather(row_norm(stream, attn_gain).astype(jnp.bfloat16), 'tensor'...  98.5 us
    all_gather x1, waiting for transfers between devices, per_device(): lax.all_gather(row_norm(resid, mlp_gain).astype(jnp.bfloat16), 'tensor',...  93.8 us
    all_to_all x3, starting transfers between devices, scatter_sum(): got = lax.all_to_all(pieces, 'tensor', 0, 0, tiled=True)  22.2 us
    dot_general x1, matrix products, per_device(): jnp.dot(hidden, w_down, preferred_element_type=jnp.float32)  13.4 us
  transfers between devices with their start and end apart: 9, of which 7 were waited for; matrix products, arithmetic and copies ran while one was open for 8% of the time, Pallas kernels for 0%

profile of v1, /device:TPU:27, one launch (start us, length us, event | category | flops | bytes accessed | tf_op | source)
XLA Modules:
  0.0 576.3 jit_solution(15585873226970098460)
XLA Ops:
  9.1 1.8 fusion.41
  14.4 98.5 %all-gather.4.cloned.1.call-done = bf16[1536,2560]{1,0:T(8,128)(2,1)} async-done(((bf16[48,2560]{1,0:T(8,128)(2,1)}), bf16[1536,2560]{1,0:T(8,128)(2,1)}) %all-gather.4.cloned.1.call-update) | async-done | bytes 7864336 | tf_op jit(solution)/shard_map/all_gather | solution.py:83
  113.0 5.9 %convolution_convert_fusion.3 = bf16[1536,64]{0,1:T(8,128)(2,1)S(1)} fusion(bf16[1536,2560]{1,0:T(8,128)(2,1)} %all-gather.4.cloned.1.call-done, bf16[2560,64]{0,1:T(8,128)(2,1)} %param.25), kind=kOutput, calls=%fused_computation.32 | convolution fusion | flops 503414784 | bytes 8388608 | tf_op jit(solution)/shard_map/dot_general | solution.py:89
  119.0 2.7 multiply_reduce_fusion
  121.8 3.7 collective-permute-done
  125.5 1.6 collective-permute-start.1
  127.2 6.8 %collective-permute-done.1 = bf16[1536,128]{0,1:T(8,128)(2,1)S(1)} collective-permute-done((bf16[1536,128]{0,1:T(8,128)(2,1)S(1)}, bf16[1536,128]{0,1:T(8,128)(2,1)S(1)}, u32[]{:S(2)}, u32[]{:S(2)}) %collective-permute-start.1) | collective-permute-done | bytes 393248 | tf_op jit(solution)/shard_map/ppermute | solution.py:20
  135.5 3.0 fusion.58
  141.2 19.7 %while.11 = (s32[]{:T(128)}, bf16[3,1,512,128]{3,2,1,0:T(8,128)(2,1)}, s32[3]{0:T(128)S(1)}, s32[1536]{0:T(1024)S(1)}, bf16[1536,1,128]{0,2,1:T(8,128)(2,1)S(1)}...) while((s32[]{:T(128)}, ...), condition=%wide.region_9.10_spmd.clone, body=%wide.region_6.9_spmd.clone.sunk | while | flops 416939520 | bytes 12107995 | solution.py:169
  142.5 2.1 select_reduce_fusion.4
  145.7 2.0 fusion.96
  149.1 2.1 select_reduce_fusion.4
  152.3 2.0 fusion.96
  155.6 2.1 select_reduce_fusion.4
  158.8 2.0 fusion.96
  160.9 6.3 %convolution_convert_fusion.1 = bf16[1536,2560]{1,0:T(8,128)(2,1)} fusion(bf16[1536,128]{1,0:T(8,128)(2,1)} %bitcast.8, bf16[128,2560]{1,0:T(8,128)(2,1)S(1)} %copy-done.7), kind=kOutput, calls=%fused_computation.28 | convolution fusion | flops 1010565120 | bytes 8912896 | tf_op jit(solution)/shard_map/dot_general | solution.py:172
  167.1 6.7 %all-to-all-start = ((bf16[32,48,2560]{2,1,0:T(8,128)(2,1)}), bf16[32,48,2560]{2,1,0:T(8,128)(2,1)}, u32[]{:S(2)}, u32[]{:S(2)}) async-start(bf16[32,48,2560]{2,1,0:T(8,128)(2,1)} %bitcast.89), calls=%async_computation | async-start | bytes 15728640 | tf_op jit(solution)/shard_map/all_to_all | solution.py:25
  174.1 111.3 %all-to-all-done = bf16[32,48,2560]{2,1,0:T(8,128)(2,1)} async-done(((bf16[32,48,2560]{2,1,0:T(8,128)(2,1)}), bf16[32,48,2560]{2,1,0:T(8,128)(2,1)}, u32[]{:S(2)}, u32[]{:S(2)}) %all-to-all-start) | async-done | bytes 7864352 | tf_op jit(solution)/shard_map/all_to_all | solution.py:25
  285.4 4.5 convert_reduce_fusion.1
  292.4 1.2 gather_fusion
  294.3 5.8 %all-to-all-start.2 = ((s32[4,1,24]{2,1,0:T(1,128)}), s32[4,1,24]{2,1,0:T(1,128)S(1)}, u32[]{:S(2)}, u32[]{:S(2)}) async-start(s32[4,1,24]{2,1,0:T(1,128)} %bitcast.11), calls=%async_computation.2 | async-start | bytes 4096 | tf_op jit(solution)/shard_map/all_to_all | solution.py:132
  300.1 93.8 %all-gather.6.cloned.1.call-done = bf16[1536,2560]{1,0:T(8,128)(2,1)} async-done(((bf16[48,2560]{1,0:T(8,128)(2,1)}), bf16[1536,2560]{1,0:T(8,128)(2,1)}) %all-gather.6.cloned.1.call-update) | async-done | bytes 7864336 | tf_op jit(solution)/shard_map/all_gather | solution.py:176
  393.9 7.5 %fusion.71 = f32[1536,304]{0,1:T(8,128)} fusion(bf16[1536,2560]{1,0:T(8,128)(2,1)} %all-gather.6.cloned.1.call-done, bf16[2560,304]{0,1:T(8,128)(2,1)} %param.27), kind=kOutput, calls=%fused_computation.119 | convolution fusion | flops 2390753280 | bytes 11288576 | tf_op jit(solution)/shard_map/dot_general | solution.py:179
  401.3 13.4 %convolution_convert_fusion = bf16[1536,2560]{1,0:T(8,128)(2,1)} fusion(bf16[304,2560]{1,0:T(8,128)(2,1)S(1)} %copy-done, bf16[1536,2560]{1,0:T(8,128)(2,1)} %all-gather.6.cloned.1.call-done, bf16[2560,304]{0,1:T(8,128)(2,1)} %param.28, f32[1536,304]{0,1:T(8,128)} %fusion.71), kind=kOutput, calls=%fused_computation.27 | convolution fusion | flops 4788240384 | bytes 20709376 | tf_op jit(solution)/shard_map/dot_general | solution.py:183
  414.7 6.8 %all-to-all-start.1 = ((bf16[32,48,2560]{2,1,0:T(8,128)(2,1)}), bf16[32,48,2560]{2,1,0:T(8,128)(2,1)}, u32[]{:S(2)}, u32[]{:S(2)}) async-start(bf16[32,48,2560]{2,1,0:T(8,128)(2,1)} %bitcast.90), calls=%async_computation.1 | async-start | bytes 15728640 | tf_op jit(solution)/shard_map/all_to_all | solution.py:25
  424.8 111.4 %all-to-all-done.1 = bf16[32,48,2560]{2,1,0:T(8,128)(2,1)} async-done(((bf16[32,48,2560]{2,1,0:T(8,128)(2,1)}), bf16[32,48,2560]{2,1,0:T(8,128)(2,1)}, u32[]{:S(2)}, u32[]{:S(2)}) %all-to-all-start.1) | async-done | bytes 7864352 | tf_op jit(solution)/shard_map/all_to_all | solution.py:25
  536.2 5.2 all-to-all-start.3
  541.4 4.5 convert_reduce_fusion
  547.1 8.7 %all-to-all-start.4 = ((bf16[32,2,240]{2,1,0:T(2,128)(2,1)}), bf16[32,2,240]{2,1,0:T(2,128)(2,1)S(1)}, u32[]{:S(2)}, u32[]{:S(2)}) async-start(bf16[32,2,240]{2,1,0:T(2,128)(2,1)} %reshape.456), calls=%async_computation.4 | async-start | bytes 65536 | tf_op jit(solution)/shard_map/all_to_all | solution.py:25
  556.2 3.5 scatter_fusion
  560.8 1.2 all-to-all-done.4
  562.1 6.5 %all-gather = bf16[4,6,80]{2,1,0:T(8,128)(2,1)S(1)} all-gather(bf16[1,6,80]{2,1,0:T(8,128)(2,1)S(1)} %bitcast.95), channel_id=1, replica_groups=mesh['dp'=4,'tensor'=32] {'dp'}, dimensions={0}, use_global_device_ids=true | all-gather | bytes 4800 | tf_op jit(solution)/shard_map/all_gather | solution.py:196
  (107 shorter events, 25.1 us)
Async XLA Ops:
  7.2 394.2 %copy-start = (bf16[304,2560]{1,0:T(8,128)(2,1)S(1)}, bf16[304,2560]{1,0:T(8,128)(2,1)}, u32[]{:S(2)}) copy-start(bf16[304,2560]{1,0:T(8,128)(2,1)} %param.29) | copy-start | bytes 4669444
  7.2 105.8 %all-gather.4.cloned.1.call-start = ((), (), s32[]{:S(2)}) async-start(), calls=%async_computation.5 | async-start | bytes 8110080 | tf_op jit(solution)/shard_map/all_gather | solution.py:83
  14.4 104.6 %copy-start.6 = (bf16[2560,128]{1,0:T(8,128)(2,1)S(1)}, bf16[2560,128]{1,0:T(8,128)(2,1)}, u32[]{:S(2)}) copy-start(bf16[2560,128]{1,0:T(8,128)(2,1)} %param.24) | copy-start | bytes 1966084
  113.0 6.0 %copy-start.1 = (bf16[1536,2560]{1,0:T(8,128)(2,1)S(1)}, bf16[1536,2560]{1,0:T(8,128)(2,1)}, u32[]{:S(2)}) copy-start(bf16[1536,2560]{1,0:T(8,128)(2,1)} %all-gather.4.cloned.1.call-done) | copy-start | bytes 23592964
  118.8 6.6 %collective-permute-start = (bf16[1536,64]{0,1:T(8,128)(2,1)S(1)}, bf16[1536,64]{0,1:T(8,128)(2,1)S(1)}, u32[]{:S(2)}, u32[]{:S(2)}) collective-permute-start(bf16[1536,64]{0,1:T(8,128)(2,1)S(1)} %convolution_convert_fusion.3), channel_id=1, source_target_pairs={{0,1},{1,0},{2,3},{3,2},{4,5},{5,4},{6,7},{7,6},{8,9},{9,8},{10,11... | collective-permute-start | bytes 589832 | tf_op jit(solution)/shard_map/ppermute | solution.py:20
  125.5 8.5 %collective-permute-start.1 = (bf16[1536,128]{0,1:T(8,128)(2,1)S(1)}, bf16[1536,128]{0,1:T(8,128)(2,1)S(1)}, u32[]{:S(2)}, u32[]{:S(2)}) collective-permute-start(bf16[1536,128]{0,1:T(8,128)(2,1)S(1)} %maximum_select_fusion.1), channel_id=1, source_target_pairs={{0,2},{1,3},{2,0},{3,1},{4,6},{5,7},{6,4},{7,5},{8,10},{9,11},{10,... | collective-permute-start | bytes 1179656 | tf_op jit(solution)/shard_map/ppermute | solution.py:20
  138.5 0.7 copy-start.3
  141.2 19.7 %copy-start.7 = (bf16[128,2560]{1,0:T(8,128)(2,1)S(1)}, bf16[128,2560]{1,0:T(8,128)(2,1)}, u32[]{:S(2)}) copy-start(bf16[128,2560]{1,0:T(8,128)(2,1)} %param.26) | copy-start | bytes 1966084
  142.5 3.2 copy-start.8
  149.1 3.2 copy-start.8
  155.6 3.2 copy-start.8
  167.1 7.0 %copy-start.9 = (bf16[2560]{0:T(1024)(128)(2,1)S(1)}, bf16[2560]{0:T(1024)(128)(2,1)}, u32[]{:S(2)}) copy-start(bf16[2560]{0:T(1024)(128)(2,1)} %param.23) | copy-start | bytes 15364
  167.1 118.3 %all-to-all-start = ((bf16[32,48,2560]{2,1,0:T(8,128)(2,1)}), bf16[32,48,2560]{2,1,0:T(8,128)(2,1)}, u32[]{:S(2)}, u32[]{:S(2)}) async-start(bf16[32,48,2560]{2,1,0:T(8,128)(2,1)} %bitcast.89), calls=%async_computation | async-start | bytes 15728640 | tf_op jit(solution)/shard_map/all_to_all | solution.py:25
  173.9 220.0 %all-gather.6.cloned.1.call-start = ((), (), s32[]{:S(2)}) async-start(), calls=%async_computation.6 | async-start | bytes 8110080 | tf_op jit(solution)/shard_map/all_gather | solution.py:176
  174.1 115.8 %copy-start.2 = (bf16[48,2560]{1,0:T(8,128)(2,1)S(1)}, bf16[48,2560]{1,0:T(8,128)(2,1)}, u32[]{:S(2)}) copy-start(bf16[48,2560]{1,0:T(8,128)(2,1)} %param.16) | copy-start | bytes 737284
  174.1 116.9 %copy-start.10 = (s32[96]{0:T(128)S(1)}, s32[96]{0:T(128)}, u32[]{:S(2)}) copy-start(s32[96]{0:T(128)} %param.18) | copy-start | bytes 1156
  294.3 120.4 %all-to-all-start.2 = ((s32[4,1,24]{2,1,0:T(1,128)}), s32[4,1,24]{2,1,0:T(1,128)S(1)}, u32[]{:S(2)}, u32[]{:S(2)}) async-start(s32[4,1,24]{2,1,0:T(1,128)} %bitcast.11), calls=%async_computation.2 | async-start | bytes 4096 | tf_op jit(solution)/shard_map/all_to_all | solution.py:132
  414.7 8.1 %copy-start.4 = (bf16[1536,64]{0,1:T(8,128)(2,1)S(1)}, bf16[1536,64]{0,1:T(8,128)(2,1)}, u32[]{:S(2)}) copy-start(bf16[1536,64]{0,1:T(8,128)(2,1)} %copy-done.3) | copy-start | bytes 589828
  414.7 121.5 %all-to-all-start.1 = ((bf16[32,48,2560]{2,1,0:T(8,128)(2,1)}), bf16[32,48,2560]{2,1,0:T(8,128)(2,1)}, u32[]{:S(2)}, u32[]{:S(2)}) async-start(bf16[32,48,2560]{2,1,0:T(8,128)(2,1)} %bitcast.90), calls=%async_computation.1 | async-start | bytes 15728640 | tf_op jit(solution)/shard_map/all_to_all | solution.py:25
  536.2 10.9 %all-to-all-start.3 = ((bf16[4,2,12288]{2,1,0:T(2,128)(2,1)}), bf16[4,2,12288]{2,1,0:T(2,128)(2,1)S(1)}, u32[]{:S(2)}, u32[]{:S(2)}) async-start(bf16[4,2,12288]{2,1,0:T(2,128)(2,1)} %reshape.454), calls=%async_computation.3 | async-start | bytes 393216 | tf_op jit(solution)/shard_map/all_to_all | solution.py:131
  545.9 22.7 %copy-start.11 = (s32[16]{0:T(128)S(1)}, s32[16]{0:T(128)}, u32[]{:S(2)}) copy-start(s32[16]{0:T(128)} %param.19) | copy-start | bytes 196
  546.0 23.4 %copy-start.5 = (bf16[48,2560]{1,0:T(8,128)(2,1)}, bf16[48,2560]{1,0:T(8,128)(2,1)S(1)}, u32[]{:S(2)}) copy-start(bf16[48,2560]{1,0:T(8,128)(2,1)S(1)} %fusion.46) | copy-start | bytes 737284
  547.1 14.8 %all-to-all-start.4 = ((bf16[32,2,240]{2,1,0:T(2,128)(2,1)}), bf16[32,2,240]{2,1,0:T(2,128)(2,1)S(1)}, u32[]{:S(2)}, u32[]{:S(2)}) async-start(bf16[32,2,240]{2,1,0:T(2,128)(2,1)} %reshape.456), calls=%async_computation.4 | async-start | bytes 65536 | tf_op jit(solution)/shard_map/all_to_all | solution.py:25
Sparse Core Ops, SparseCore 0:
  11.6 101.3 all-gather.3
  291.1 102.6 all-gather.5

commit v2 on v1

--- a/solution.py
+++ b/solution.py
@@ -8,6 +8,8 @@
 KEY_VALUE_HEADS = 8
 HEAD_SIZE = 128
 PAGE_TOKENS = 16
+TENSOR = ("ty", "tx", "tz")
+TENSOR_SHAPE = (4, 4, 2)
 
 
 epsilon = 1e-06
@@ -22,8 +24,13 @@
 
 def scatter_sum(partial, parts):
     pieces = partial.reshape((parts, partial.shape[0] // parts) + partial.shape[1:])
-    got = lax.all_to_all(pieces, "tensor", 0, 0, tiled=True)
+    got = lax.all_to_all(pieces, TENSOR, 0, 0, tiled=True)
     return jnp.sum(got.astype(jnp.float32), axis=0)
+
+
+def gather_rows(rows):
+    rows = lax.all_gather(rows, "tz", axis=0, tiled=True)
+    return lax.all_gather(rows, ("ty", "tx"), axis=0, tiled=True)
 
 
 def row_norm(inputs, gain):
@@ -74,15 +81,13 @@
     w_down,
 ):
     tok_dev = stream.shape[0]
-    tensor_element_count = lax.axis_size("tensor")
+    tensor_element_count = lax.axis_size(TENSOR)
     token_count = tok_dev * tensor_element_count
-    my_index = lax.axis_index("tensor")
+    my_index = lax.axis_index(TENSOR)
     heads_dev = w_query.shape[1] // HEAD_SIZE
     query_cols = heads_dev * HEAD_SIZE
     prompt, position, prompt_starts, prompt_ends = prompt_layout(lengths[0], token_count)
-    portion = lax.all_gather(
-        row_norm(stream, attn_gain).astype(jnp.bfloat16), "tensor", axis=0, tiled=True
-    )
+    portion = gather_rows(row_norm(stream, attn_gain).astype(jnp.bfloat16))
     joined = jnp.concatenate(
         [
             jnp.dot(portion, w_query, preferred_element_type=jnp.float32),
@@ -94,7 +99,7 @@
     kv_part = joined[:, query_cols:].astype(jnp.bfloat16)
     key_value_group = tensor_element_count // KEY_VALUE_HEADS
     for bit_id in range(key_value_group.bit_length() - 1):
-        partner = partner_2(kv_part, "tensor", bit_id)
+        partner = partner_2(kv_part, TENSOR, bit_id)
         upper_half = my_index // 2**bit_id % 2
         kv_part = jnp.where(
             upper_half == 1,
@@ -173,9 +178,7 @@
         tensor_element_count,
     )
     resid = (stream.astype(jnp.float32) + attn_sum).astype(jnp.bfloat16)
-    portion = lax.all_gather(
-        row_norm(resid, mlp_gain).astype(jnp.bfloat16), "tensor", axis=0, tiled=True
-    )
+    portion = gather_rows(row_norm(resid, mlp_gain).astype(jnp.bfloat16))
     gate_rows = jnp.dot(portion, w_gate, preferred_element_type=jnp.float32)
     upward = jnp.dot(portion, w_up, preferred_element_type=jnp.float32)
     hidden = (jax.nn.silu(gate_rows) * upward).astype(jnp.bfloat16)
@@ -203,7 +206,7 @@
 
 def solution(mesh):
     placed = (
-        P(("dp", "tensor"), None),
+        P(("dp",) + TENSOR, None),
         P("dp", None),
         P("dp"),
         P("dp"),
@@ -211,17 +214,21 @@
         P(),
         P(),
         P(),
-        P(None, "tensor"),
-        P(None, "tensor"),
-        P("tensor", None),
-        P(None, "tensor"),
-        P(None, "tensor"),
-        P("tensor", None),
+        P(None, TENSOR),
+        P(None, TENSOR),
+        P(TENSOR, None),
+        P(None, TENSOR),
+        P(None, TENSOR),
+        P(TENSOR, None),
+    )
+    dp_size = mesh.shape["dp"]
+    fine = jax.sharding.Mesh(
+        mesh.devices.reshape((dp_size,) + TENSOR_SHAPE), ("dp",) + TENSOR
     )
     return jax.shard_map(
         per_device,
-        mesh=mesh,
+        mesh=fine,
         in_specs=placed,
-        out_specs=(P(("dp", "tensor"), None), P("dp", None, "tensor"), P("dp", "tensor")),
+        out_specs=(P(("dp",) + TENSOR, None), P("dp", None, TENSOR), P("dp", TENSOR)),
         check_vma=False,
     )

time: 581 us -> 546 us (0.940)
  waiting for transfers between devices: 427 us -> 370 us
  blocking collectives: 6.49 us -> 23.8 us
  starting transfers between devices: 35.2 us -> 41.9 us
    all_gather x2, waiting for transfers between devices: 192 us -> 129 us  [gather_rows(): return lax.all_gather(rows, ('ty', 'tx'), axis=0, tiled=True)]
    all_gather x0 -> x2, blocking collectives: none -> 17.3 us  [gather_rows(): rows = lax.all_gather(rows, 'tz', axis=0, tiled=True)]
    all_to_all x3, waiting for transfers between devices: 224 us -> 232 us  [scatter_sum(): got = lax.all_to_all(pieces, TENSOR, 0, 0, tiled=True)]
where the time goes in v2:
time: 546 us; the launch traced here: 542 us
  waiting for transfers between devices  370 us (68%)
  matrix products  49.2 us (9%)
  starting transfers between devices  41.9 us (8%)
  other arithmetic  25.1 us (5%)
  blocking collectives  23.8 us (4%)
  local copies, waits for them, and re-layouts  15.7 us (3%)
  between operations  14.5 us (3%)
    all_to_all x3, waiting for transfers between devices, scatter_sum(): got = lax.all_to_all(pieces, TENSOR, 0, 0, tiled=True)  232 us
    all_gather x2, waiting for transfers between devices, gather_rows(): return lax.all_gather(rows, ('ty', 'tx'), axis=0, tiled=True)  129 us
    all_to_all x3, starting transfers between devices, scatter_sum(): got = lax.all_to_all(pieces, TENSOR, 0, 0, tiled=True)  25.4 us
    all_gather x2, blocking collectives, gather_rows(): rows = lax.all_gather(rows, 'tz', axis=0, tiled=True)  17.3 us
    dot_general x1, matrix products, per_device(): jnp.dot(hidden, w_down, preferred_element_type=jnp.float32)  13.3 us
  transfers between devices with their start and end apart: 9, of which 7 were waited for; matrix products, arithmetic and copies ran while one was open for 8% of the time, Pallas kernels for 0%

profile of v2, /device:TPU:27, one launch (start us, length us, event | category | flops | bytes accessed | tf_op | source)
XLA Modules:
  0.0 542.0 jit_solution(2696355523527510961)
XLA Ops:
  10.2 10.0 %all_gather.15 = bf16[96,2560]{1,0:T(8,128)(2,1)} all-gather(bf16[48,2560]{1,0:T(8,128)(2,1)S(1)} %fusion.41), channel_id=1, replica_groups=mesh['dp'=4,'ty'=4,'tx'=4,'tz'=2] {'tz'}, dimensions={0}, use_global_device_ids=true | all-gather | bytes 737280 | tf_op jit(solution)/shard_map/all_gather | solution.py:32
  23.9 65.5 %all-gather.4.cloned.1.call-done = bf16[1536,2560]{1,0:T(8,128)(2,1)} async-done(((bf16[96,2560]{1,0:T(8,128)(2,1)}), bf16[1536,2560]{1,0:T(8,128)(2,1)}) %all-gather.4.cloned.1.call-update) | async-done | bytes 7864336 | tf_op jit(solution)/shard_map/all_gather | solution.py:33
  89.4 5.9 %convolution_convert_fusion.3 = bf16[1536,64]{0,1:T(8,128)(2,1)S(1)} fusion(bf16[1536,2560]{1,0:T(8,128)(2,1)} %all-gather.4.cloned.1.call-done, bf16[2560,64]{0,1:T(8,128)(2,1)} %param.25), kind=kOutput, calls=%fused_computation.32 | convolution fusion | flops 503414784 | bytes 8388608 | tf_op jit(solution)/shard_map/dot_general | solution.py:94
  95.2 2.9 collective-permute-start
  98.2 2.7 multiply_reduce_fusion
  100.9 1.5 collective-permute-done
  102.5 1.6 collective-permute-start.1
  104.2 7.4 %collective-permute-done.1 = bf16[1536,128]{0,1:T(8,128)(2,1)S(1)} collective-permute-done((bf16[1536,128]{0,1:T(8,128)(2,1)S(1)}, bf16[1536,128]{0,1:T(8,128)(2,1)S(1)}, u32[]{:S(2)}, u32[]{:S(2)}) %collective-permute-start.1) | collective-permute-done | bytes 393248 | tf_op jit(solution)/shard_map/ppermute | solution.py:22
  113.0 3.1 fusion.58
  118.8 19.7 %while.11 = (s32[]{:T(128)}, bf16[3,1,512,128]{3,2,1,0:T(8,128)(2,1)}, s32[3]{0:T(128)S(1)}, s32[1536]{0:T(1024)S(1)}, bf16[1536,1,128]{0,2,1:T(8,128)(2,1)S(1)}...) while((s32[]{:T(128)}, ...), condition=%wide.region_9.10_spmd.clone, body=%wide.region_6.9_spmd.clone.sunk | while | flops 416939520 | bytes 12107995 | solution.py:174
  120.1 2.1 select_reduce_fusion.4
  123.3 2.1 fusion.96
  126.7 2.1 select_reduce_fusion.4
  129.9 2.0 fusion.96
  133.3 2.1 select_reduce_fusion.4
  136.5 2.0 fusion.96
  138.5 6.3 %convolution_convert_fusion.1 = bf16[1536,2560]{1,0:T(8,128)(2,1)} fusion(bf16[1536,128]{1,0:T(8,128)(2,1)} %bitcast.8, bf16[128,2560]{1,0:T(8,128)(2,1)S(1)} %copy-done.7), kind=kOutput, calls=%fused_computation.28 | convolution fusion | flops 1010565120 | bytes 8912896 | tf_op jit(solution)/shard_map/dot_general | solution.py:177
  144.8 9.2 %all-to-all-start = ((bf16[32,48,2560]{2,1,0:T(8,128)(2,1)}), bf16[32,48,2560]{2,1,0:T(8,128)(2,1)}, u32[]{:S(2)}, u32[]{:S(2)}) async-start(bf16[32,48,2560]{2,1,0:T(8,128)(2,1)} %bitcast.89), calls=%async_computation | async-start | bytes 15728640 | tf_op jit(solution)/shard_map/all_to_all | solution.py:27
  154.3 112.6 %all-to-all-done = bf16[32,48,2560]{2,1,0:T(8,128)(2,1)} async-done(((bf16[32,48,2560]{2,1,0:T(8,128)(2,1)}), bf16[32,48,2560]{2,1,0:T(8,128)(2,1)}, u32[]{:S(2)}, u32[]{:S(2)}) %all-to-all-start) | async-done | bytes 7864352 | tf_op jit(solution)/shard_map/all_to_all | solution.py:27
  266.9 4.5 convert_reduce_fusion.1
  271.7 7.3 %all_gather.17 = bf16[96,2560]{1,0:T(8,128)(2,1)} all-gather(bf16[48,2560]{1,0:T(8,128)(2,1)S(1)} %fusion.45), channel_id=1, replica_groups=mesh['dp'=4,'ty'=4,'tx'=4,'tz'=2] {'tz'}, dimensions={0}, use_global_device_ids=true | all-gather | bytes 737280 | tf_op jit(solution)/shard_map/all_gather | solution.py:32
  282.3 6.7 %all-to-all-start.2 = ((s32[4,1,24]{2,1,0:T(1,128)}), s32[4,1,24]{2,1,0:T(1,128)S(1)}, u32[]{:S(2)}, u32[]{:S(2)}) async-start(s32[4,1,24]{2,1,0:T(1,128)} %bitcast.11), calls=%async_computation.2 | async-start | bytes 4096 | tf_op jit(solution)/shard_map/all_to_all | solution.py:137
  289.1 63.4 %all-gather.6.cloned.1.call-done = bf16[1536,2560]{1,0:T(8,128)(2,1)} async-done(((bf16[96,2560]{1,0:T(8,128)(2,1)}), bf16[1536,2560]{1,0:T(8,128)(2,1)}) %all-gather.6.cloned.1.call-update) | async-done | bytes 7864336 | tf_op jit(solution)/shard_map/all_gather | solution.py:33
  352.5 7.5 %fusion.71 = f32[1536,304]{0,1:T(8,128)} fusion(bf16[1536,2560]{1,0:T(8,128)(2,1)} %all-gather.6.cloned.1.call-done, bf16[2560,304]{0,1:T(8,128)(2,1)} %param.27), kind=kOutput, calls=%fused_computation.119 | convolution fusion | flops 2390753280 | bytes 11288576 | tf_op jit(solution)/shard_map/dot_general | solution.py:182
  360.0 13.3 %convolution_convert_fusion = bf16[1536,2560]{1,0:T(8,128)(2,1)} fusion(bf16[304,2560]{1,0:T(8,128)(2,1)S(1)} %copy-done, bf16[1536,2560]{1,0:T(8,128)(2,1)} %all-gather.6.cloned.1.call-done, bf16[2560,304]{0,1:T(8,128)(2,1)} %param.28, f32[1536,304]{0,1:T(8,128)} %fusion.71), kind=kOutput, calls=%fused_computation.27 | convolution fusion | flops 4788240384 | bytes 20709376 | tf_op jit(solution)/shard_map/dot_general | solution.py:186
  373.3 9.4 %all-to-all-start.1 = ((bf16[32,48,2560]{2,1,0:T(8,128)(2,1)}), bf16[32,48,2560]{2,1,0:T(8,128)(2,1)}, u32[]{:S(2)}, u32[]{:S(2)}) async-start(bf16[32,48,2560]{2,1,0:T(8,128)(2,1)} %bitcast.90), calls=%async_computation.1 | async-start | bytes 15728640 | tf_op jit(solution)/shard_map/all_to_all | solution.py:27
  386.0 118.0 %all-to-all-done.1 = bf16[32,48,2560]{2,1,0:T(8,128)(2,1)} async-done(((bf16[32,48,2560]{2,1,0:T(8,128)(2,1)}), bf16[32,48,2560]{2,1,0:T(8,128)(2,1)}, u32[]{:S(2)}, u32[]{:S(2)}) %all-to-all-start.1) | async-done | bytes 7864352 | tf_op jit(solution)/shard_map/all_to_all | solution.py:27
  504.1 5.0 all-to-all-start.3
  509.1 4.5 convert_reduce_fusion
  514.8 6.8 %all-to-all-start.4 = ((bf16[32,2,240]{2,1,0:T(2,128)(2,1)}), bf16[32,2,240]{2,1,0:T(2,128)(2,1)S(1)}, u32[]{:S(2)}, u32[]{:S(2)}) async-start(bf16[32,2,240]{2,1,0:T(2,128)(2,1)} %reshape.456), calls=%async_computation.4 | async-start | bytes 65536 | tf_op jit(solution)/shard_map/all_to_all | solution.py:27
  521.9 3.5 scatter_fusion
  527.8 6.5 %all-gather = bf16[4,6,80]{2,1,0:T(8,128)(2,1)S(1)} all-gather(bf16[1,6,80]{2,1,0:T(8,128)(2,1)S(1)} %bitcast.95), channel_id=1, replica_groups=mesh['dp'=4,'ty'=4,'tx'=4,'tz'=2] {'dp'}, dimensions={0}, use_global_device_ids=true | all-gather | bytes 4800 | tf_op jit(solution)/shard_map/all_gather | solution.py:199
  (109 shorter events, 27.8 us)
Async XLA Ops:
  7.2 352.8 %copy-start = (bf16[304,2560]{1,0:T(8,128)(2,1)S(1)}, bf16[304,2560]{1,0:T(8,128)(2,1)}, u32[]{:S(2)}) copy-start(bf16[304,2560]{1,0:T(8,128)(2,1)} %param.29) | copy-start | bytes 4669444
  7.2 82.2 %all-gather.4.cloned.1.call-start = ((), (), s32[]{:S(2)}) async-start(), calls=%async_computation.5 | async-start | bytes 8355840 | tf_op jit(solution)/shard_map/all_gather | solution.py:33
  23.8 74.3 %copy-start.6 = (bf16[2560,128]{1,0:T(8,128)(2,1)S(1)}, bf16[2560,128]{1,0:T(8,128)(2,1)}, u32[]{:S(2)}) copy-start(bf16[2560,128]{1,0:T(8,128)(2,1)} %param.24) | copy-start | bytes 1966084
  89.4 8.8 %copy-start.1 = (bf16[1536,2560]{1,0:T(8,128)(2,1)S(1)}, bf16[1536,2560]{1,0:T(8,128)(2,1)}, u32[]{:S(2)}) copy-start(bf16[1536,2560]{1,0:T(8,128)(2,1)} %all-gather.4.cloned.1.call-done) | copy-start | bytes 23592964
  95.2 7.2 %collective-permute-start = (bf16[1536,64]{0,1:T(8,128)(2,1)S(1)}, bf16[1536,64]{0,1:T(8,128)(2,1)S(1)}, u32[]{:S(2)}, u32[]{:S(2)}) collective-permute-start(bf16[1536,64]{0,1:T(8,128)(2,1)S(1)} %convolution_convert_fusion.3), channel_id=1, source_target_pairs={{0,1},{1,0},{2,3},{3,2},{4,5},{5,4},{6,7},{7,6},{8,9},{9,8},{10,11... | collective-permute-start | bytes 589832 | tf_op jit(solution)/shard_map/ppermute | solution.py:22
  102.5 9.1 %collective-permute-start.1 = (bf16[1536,128]{0,1:T(8,128)(2,1)S(1)}, bf16[1536,128]{0,1:T(8,128)(2,1)S(1)}, u32[]{:S(2)}, u32[]{:S(2)}) collective-permute-start(bf16[1536,128]{0,1:T(8,128)(2,1)S(1)} %maximum_select_fusion.1), channel_id=1, source_target_pairs={{0,2},{1,3},{2,0},{3,1},{4,6},{5,7},{6,4},{7,5},{8,10},{9,11},{10,... | collective-permute-start | bytes 1179656 | tf_op jit(solution)/shard_map/ppermute | solution.py:22
  116.1 0.7 copy-start.3
  118.8 19.7 %copy-start.7 = (bf16[128,2560]{1,0:T(8,128)(2,1)S(1)}, bf16[128,2560]{1,0:T(8,128)(2,1)}, u32[]{:S(2)}) copy-start(bf16[128,2560]{1,0:T(8,128)(2,1)} %param.26) | copy-start | bytes 1966084
  120.1 3.2 copy-start.8
  126.7 3.2 copy-start.8
  133.3 3.2 copy-start.8
  144.8 9.5 %copy-start.9 = (bf16[2560]{0:T(1024)(128)(2,1)S(1)}, bf16[2560]{0:T(1024)(128)(2,1)}, u32[]{:S(2)}) copy-start(bf16[2560]{0:T(1024)(128)(2,1)} %param.23) | copy-start | bytes 15364
  144.8 122.1 %all-to-all-start = ((bf16[32,48,2560]{2,1,0:T(8,128)(2,1)}), bf16[32,48,2560]{2,1,0:T(8,128)(2,1)}, u32[]{:S(2)}, u32[]{:S(2)}) async-start(bf16[32,48,2560]{2,1,0:T(8,128)(2,1)} %bitcast.89), calls=%async_computation | async-start | bytes 15728640 | tf_op jit(solution)/shard_map/all_to_all | solution.py:27
  154.0 198.5 %all-gather.6.cloned.1.call-start = ((), (), s32[]{:S(2)}) async-start(), calls=%async_computation.6 | async-start | bytes 8355840 | tf_op jit(solution)/shard_map/all_gather | solution.py:33
  154.3 117.1 %copy-start.2 = (bf16[48,2560]{1,0:T(8,128)(2,1)S(1)}, bf16[48,2560]{1,0:T(8,128)(2,1)}, u32[]{:S(2)}) copy-start(bf16[48,2560]{1,0:T(8,128)(2,1)} %param.16) | copy-start | bytes 737284
  154.3 124.8 %copy-start.10 = (s32[96]{0:T(128)S(1)}, s32[96]{0:T(128)}, u32[]{:S(2)}) copy-start(s32[96]{0:T(128)} %param.18) | copy-start | bytes 1156
  282.3 91.0 %all-to-all-start.2 = ((s32[4,1,24]{2,1,0:T(1,128)}), s32[4,1,24]{2,1,0:T(1,128)S(1)}, u32[]{:S(2)}, u32[]{:S(2)}) async-start(s32[4,1,24]{2,1,0:T(1,128)} %bitcast.11), calls=%async_computation.2 | async-start | bytes 4096 | tf_op jit(solution)/shard_map/all_to_all | solution.py:137
  373.3 10.7 %copy-start.4 = (bf16[1536,64]{0,1:T(8,128)(2,1)S(1)}, bf16[1536,64]{0,1:T(8,128)(2,1)}, u32[]{:S(2)}) copy-start(bf16[1536,64]{0,1:T(8,128)(2,1)} %copy-done.3) | copy-start | bytes 589828
  373.3 130.8 %all-to-all-start.1 = ((bf16[32,48,2560]{2,1,0:T(8,128)(2,1)}), bf16[32,48,2560]{2,1,0:T(8,128)(2,1)}, u32[]{:S(2)}, u32[]{:S(2)}) async-start(bf16[32,48,2560]{2,1,0:T(8,128)(2,1)} %bitcast.90), calls=%async_computation.1 | async-start | bytes 15728640 | tf_op jit(solution)/shard_map/all_to_all | solution.py:27
  504.1 10.7 %all-to-all-start.3 = ((bf16[4,2,12288]{2,1,0:T(2,128)(2,1)}), bf16[4,2,12288]{2,1,0:T(2,128)(2,1)S(1)}, u32[]{:S(2)}, u32[]{:S(2)}) async-start(bf16[4,2,12288]{2,1,0:T(2,128)(2,1)} %reshape.454), calls=%async_computation.3 | async-start | bytes 393216 | tf_op jit(solution)/shard_map/all_to_all | solution.py:136
  513.6 20.7 %copy-start.11 = (s32[16]{0:T(128)S(1)}, s32[16]{0:T(128)}, u32[]{:S(2)}) copy-start(s32[16]{0:T(128)} %param.19) | copy-start | bytes 196
  513.7 21.4 %copy-start.5 = (bf16[48,2560]{1,0:T(8,128)(2,1)}, bf16[48,2560]{1,0:T(8,128)(2,1)S(1)}, u32[]{:S(2)}) copy-start(bf16[48,2560]{1,0:T(8,128)(2,1)S(1)} %fusion.46) | copy-start | bytes 737284
  514.8 12.9 %all-to-all-start.4 = ((bf16[32,2,240]{2,1,0:T(2,128)(2,1)}), bf16[32,2,240]{2,1,0:T(2,128)(2,1)S(1)}, u32[]{:S(2)}, u32[]{:S(2)}) async-start(bf16[32,2,240]{2,1,0:T(2,128)(2,1)} %reshape.456), calls=%async_computation.4 | async-start | bytes 65536 | tf_op jit(solution)/shard_map/all_to_all | solution.py:27
Sparse Core Ops, SparseCore 0:
  20.4 68.9 all-gather.3
  279.2 73.2 all-gather.5

commit v3 on v2

--- a/solution.py
+++ b/solution.py
@@ -173,6 +173,7 @@
     block_ids = jnp.arange(block_total, dtype=jnp.int32)
     blocks_out = lax.map(dense_block, block_ids)
     attn = jnp.transpose(blocks_out, (0, 2, 1, 3)).reshape(token_count, query_cols)
+    paged_key_value_cache, attn = lax.optimization_barrier((paged_key_value_cache, attn))
     attn_sum = scatter_sum(
         jnp.dot(attn, w_out, preferred_element_type=jnp.float32).astype(jnp.bfloat16),
         tensor_element_count,

time: 546 us -> 554 us (1.015)
  waiting for transfers between devices: 370 us -> 381 us
    all_to_all x3, waiting for transfers between devices: 232 us -> 252 us  [scatter_sum(): got = lax.all_to_all(pieces, TENSOR, 0, 0, tiled=True)]
    all_gather x2, waiting for transfers between devices: 129 us -> 121 us  [gather_rows(): return lax.all_gather(rows, ('ty', 'tx'), axis=0, tiled=True)]
  transfers between devices with their start and end apart: 9 -> 9, of which waited for: 7 -> 7; matrix products, arithmetic and copies ran while one was open for 8% -> 5% of each run, Pallas kernels for 0% -> 0%
where the time goes in v3:
time: 554 us; the launch traced here: 549 us
  waiting for transfers between devices  381 us (69%)
  matrix products  44.5 us (8%)
  starting transfers between devices  40.1 us (7%)
  blocking collectives  26.7 us (5%)
  other arithmetic  26.4 us (5%)
  between operations  14.4 us (3%)
  local copies, waits for them, and re-layouts  14.3 us (3%)
    all_to_all x3, waiting for transfers between devices, scatter_sum(): got = lax.all_to_all(pieces, TENSOR, 0, 0, tiled=True)  252 us
    all_gather x2, waiting for transfers between devices, gather_rows(): return lax.all_gather(rows, ('ty', 'tx'), axis=0, tiled=True)  121 us
    all_to_all x3, starting transfers between devices, scatter_sum(): got = lax.all_to_all(pieces, TENSOR, 0, 0, tiled=True)  25.2 us
    all_gather x2, blocking collectives, gather_rows(): rows = lax.all_gather(rows, 'tz', axis=0, tiled=True)  18.7 us
    dot_general x1, matrix products, per_device(): jnp.dot(hidden, w_down, preferred_element_type=jnp.float32)  13.4 us
  transfers between devices with their start and end apart: 9, of which 7 were waited for; matrix products, arithmetic and copies ran while one was open for 5% of the time, Pallas kernels for 0%

profile of v3, /device:TPU:27, one launch (start us, length us, event | category | flops | bytes accessed | tf_op | source)
XLA Modules:
  0.0 549.5 jit_solution(10616995148324011621)
XLA Ops:
  7.2 1.2 fusion.39
  10.3 10.0 %all_gather.15 = bf16[96,2560]{1,0:T(8,128)(2,1)} all-gather(bf16[48,2560]{1,0:T(8,128)(2,1)S(1)} %fusion.41), channel_id=1, replica_groups=mesh['dp'=4,'ty'=4,'tx'=4,'tz'=2] {'tz'}, dimensions={0}, use_global_device_ids=true | all-gather | bytes 737280 | tf_op jit(solution)/shard_map/all_gather | solution.py:32
  22.3 1.2 gather_fusion
  24.2 4.4 all-to-all-start
  34.4 55.0 %all-gather.4.cloned.1.call-done = bf16[1536,2560]{1,0:T(8,128)(2,1)} async-done(((bf16[96,2560]{1,0:T(8,128)(2,1)}), bf16[1536,2560]{1,0:T(8,128)(2,1)}) %all-gather.4.cloned.1.call-update) | async-done | bytes 7864336 | tf_op jit(solution)/shard_map/all_gather | solution.py:33
  89.4 5.8 %convolution_convert_fusion.3 = bf16[1536,64]{0,1:T(8,128)(2,1)S(1)} fusion(bf16[1536,2560]{1,0:T(8,128)(2,1)} %all-gather.4.cloned.1.call-done, bf16[2560,64]{0,1:T(8,128)(2,1)S(1)} %copy-done.9), kind=kOutput, calls=%fused_computation.32 | convolution fusion | flops 503414784 | bytes 8388608 | tf_op jit(solution)/shard_map/dot_general | solution.py:94
  95.3 3.0 collective-permute-start
  98.2 2.7 multiply_reduce_fusion
  101.0 1.5 collective-permute-done
  102.6 1.6 collective-permute-start.1
  104.3 7.4 %collective-permute-done.1 = bf16[1536,128]{0,1:T(8,128)(2,1)S(1)} collective-permute-done((bf16[1536,128]{0,1:T(8,128)(2,1)S(1)}, bf16[1536,128]{0,1:T(8,128)(2,1)S(1)}, u32[]{:S(2)}, u32[]{:S(2)}) %collective-permute-start.1) | collective-permute-done | bytes 393248 | tf_op jit(solution)/shard_map/ppermute | solution.py:22
  113.7 3.0 fusion.52
  119.0 5.9 %all-to-all-start.1 = ((bf16[4,2,12288]{2,1,0:T(2,128)(2,1)}), bf16[4,2,12288]{2,1,0:T(2,128)(2,1)S(1)}, u32[]{:S(2)}, u32[]{:S(2)}) async-start(bf16[4,2,12288]{2,1,0:T(2,128)(2,1)} %reshape.454), calls=%async_computation.1 | async-start | bytes 393216 | tf_op jit(solution)/shard_map/all_to_all | solution.py:136
  124.9 15.0 %while.11 = (s32[]{:T(128)}, bf16[3,1,512,128]{3,2,1,0:T(8,128)(2,1)S(1)}, s32[3]{0:T(128)S(1)}, s32[1536]{0:T(1024)S(1)}, bf16[1536,1,128]{0,2,1:T(8,128)(2,1)S...) while((s32[]{:T(128)}, ...), condition=%wide.region_13.14_spmd.clone, body=%wide.region_10.13_spmd.clone.sunk | while | flops 416939520 | bytes 12110043 | solution.py:174
  128.4 1.5 fusion.96
  133.4 1.5 fusion.96
  138.4 1.5 fusion.96
  140.2 3.5 scatter_fusion
  143.7 6.4 %convolution_convert_fusion.1 = bf16[1536,2560]{1,0:T(8,128)(2,1)} fusion(bf16[1536,128]{1,0:T(8,128)(2,1)S(1)} %bitcast.94, bf16[128,2560]{1,0:T(8,128)(2,1)} %param.26), kind=kOutput, calls=%fused_computation.28 | convolution fusion | flops 1010565120 | bytes 8912896 | tf_op jit(solution)/shard_map/dot_general | solution.py:178
  150.2 9.3 %all-to-all-start.2 = ((bf16[32,48,2560]{2,1,0:T(8,128)(2,1)}), bf16[32,48,2560]{2,1,0:T(8,128)(2,1)}, u32[]{:S(2)}, u32[]{:S(2)}) async-start(bf16[32,48,2560]{2,1,0:T(8,128)(2,1)} %bitcast.89), calls=%async_computation.2 | async-start | bytes 15728640 | tf_op jit(solution)/shard_map/all_to_all | solution.py:27
  159.6 124.3 %all-to-all-done.2 = bf16[32,48,2560]{2,1,0:T(8,128)(2,1)} async-done(((bf16[32,48,2560]{2,1,0:T(8,128)(2,1)}), bf16[32,48,2560]{2,1,0:T(8,128)(2,1)}, u32[]{:S(2)}, u32[]{:S(2)}) %all-to-all-start.2) | async-done | bytes 7864352 | tf_op jit(solution)/shard_map/all_to_all | solution.py:27
  283.9 4.5 convert_reduce_fusion.1
  288.8 8.7 %all_gather.17 = bf16[96,2560]{1,0:T(8,128)(2,1)} all-gather(bf16[48,2560]{1,0:T(8,128)(2,1)S(1)} %fusion.45), channel_id=1, replica_groups=mesh['dp'=4,'ty'=4,'tx'=4,'tz'=2] {'tz'}, dimensions={0}, use_global_device_ids=true | all-gather | bytes 737280 | tf_op jit(solution)/shard_map/all_gather | solution.py:32
  297.4 65.5 %all-gather.6.cloned.1.call-done = bf16[1536,2560]{1,0:T(8,128)(2,1)} async-done(((bf16[96,2560]{1,0:T(8,128)(2,1)}), bf16[1536,2560]{1,0:T(8,128)(2,1)}) %all-gather.6.cloned.1.call-update) | async-done | bytes 7864336 | tf_op jit(solution)/shard_map/all_gather | solution.py:33
  362.9 7.5 %fusion.71 = f32[1536,304]{0,1:T(8,128)} fusion(bf16[1536,2560]{1,0:T(8,128)(2,1)} %all-gather.6.cloned.1.call-done, bf16[2560,304]{0,1:T(8,128)(2,1)} %param.27), kind=kOutput, calls=%fused_computation.119 | convolution fusion | flops 2390753280 | bytes 11288576 | tf_op jit(solution)/shard_map/dot_general | solution.py:183
  370.4 13.4 %convolution_convert_fusion = bf16[1536,2560]{1,0:T(8,128)(2,1)} fusion(bf16[304,2560]{1,0:T(8,128)(2,1)S(1)} %copy-done, bf16[1536,2560]{1,0:T(8,128)(2,1)} %all-gather.6.cloned.1.call-done, bf16[2560,304]{0,1:T(8,128)(2,1)} %param.28, f32[1536,304]{0,1:T(8,128)} %fusion.71), kind=kOutput, calls=%fused_computation.27 | convolution fusion | flops 4788240384 | bytes 20709376 | tf_op jit(solution)/shard_map/dot_general | solution.py:187
  383.7 9.3 %all-to-all-start.3 = ((bf16[32,48,2560]{2,1,0:T(8,128)(2,1)}), bf16[32,48,2560]{2,1,0:T(8,128)(2,1)}, u32[]{:S(2)}, u32[]{:S(2)}) async-start(bf16[32,48,2560]{2,1,0:T(8,128)(2,1)} %bitcast.90), calls=%async_computation.3 | async-start | bytes 15728640 | tf_op jit(solution)/shard_map/all_to_all | solution.py:27
  393.1 122.2 %all-to-all-done.3 = bf16[32,48,2560]{2,1,0:T(8,128)(2,1)} async-done(((bf16[32,48,2560]{2,1,0:T(8,128)(2,1)}), bf16[32,48,2560]{2,1,0:T(8,128)(2,1)}, u32[]{:S(2)}, u32[]{:S(2)}) %all-to-all-start.3) | async-done | bytes 7864352 | tf_op jit(solution)/shard_map/all_to_all | solution.py:27
  515.3 4.5 convert_reduce_fusion
  521.0 6.5 %all-to-all-start.4 = ((bf16[32,2,240]{2,1,0:T(2,128)(2,1)}), bf16[32,2,240]{2,1,0:T(2,128)(2,1)S(1)}, u32[]{:S(2)}, u32[]{:S(2)}) async-start(bf16[32,2,240]{2,1,0:T(2,128)(2,1)} %reshape.456), calls=%async_computation.4 | async-start | bytes 65536 | tf_op jit(solution)/shard_map/all_to_all | solution.py:27
  528.6 5.0 all-to-all-done.4
  533.8 8.0 %all-gather = bf16[4,6,80]{2,1,0:T(8,128)(2,1)S(1)} all-gather(bf16[1,6,80]{2,1,0:T(8,128)(2,1)S(1)} %bitcast.96), channel_id=1, replica_groups=mesh['dp'=4,'ty'=4,'tx'=4,'tz'=2] {'dp'}, dimensions={0}, use_global_device_ids=true | all-gather | bytes 4800 | tf_op jit(solution)/shard_map/all_gather | solution.py:200
  (115 shorter events, 27.0 us)
Async XLA Ops:
  7.2 363.2 %copy-start = (bf16[304,2560]{1,0:T(8,128)(2,1)S(1)}, bf16[304,2560]{1,0:T(8,128)(2,1)}, u32[]{:S(2)}) copy-start(bf16[304,2560]{1,0:T(8,128)(2,1)} %param.29) | copy-start | bytes 4669444
  7.2 82.2 %copy-start.9 = (bf16[2560,64]{0,1:T(8,128)(2,1)S(1)}, bf16[2560,64]{0,1:T(8,128)(2,1)}, u32[]{:S(2)}) copy-start(bf16[2560,64]{0,1:T(8,128)(2,1)} %param.25) | copy-start | bytes 983044
  7.2 82.2 %all-gather.4.cloned.1.call-start = ((), (), s32[]{:S(2)}) async-start(), calls=%async_computation.5 | async-start | bytes 8355840 | tf_op jit(solution)/shard_map/all_gather | solution.py:33
  24.2 8.9 %all-to-all-start = ((s32[4,1,24]{2,1,0:T(1,128)}), s32[4,1,24]{2,1,0:T(1,128)S(1)}, u32[]{:S(2)}, u32[]{:S(2)}) async-start(s32[4,1,24]{2,1,0:T(1,128)} %bitcast), calls=%async_computation | async-start | bytes 4096 | tf_op jit(solution)/shard_map/all_to_all | solution.py:137
  29.5 3.6 copy-start.12
  34.4 63.8 %copy-start.7 = (bf16[2560,128]{1,0:T(8,128)(2,1)S(1)}, bf16[2560,128]{1,0:T(8,128)(2,1)}, u32[]{:S(2)}) copy-start(bf16[2560,128]{1,0:T(8,128)(2,1)} %param.24) | copy-start | bytes 1966084
  89.4 8.8 %copy-start.1 = (bf16[1536,2560]{1,0:T(8,128)(2,1)S(1)}, bf16[1536,2560]{1,0:T(8,128)(2,1)}, u32[]{:S(2)}) copy-start(bf16[1536,2560]{1,0:T(8,128)(2,1)} %all-gather.4.cloned.1.call-done) | copy-start | bytes 23592964
  95.3 8.9 %copy-start.11 = (f32[128]{0:T(128)S(1)}, f32[128]{0:T(128)}, u32[]{:S(2)}) copy-start(f32[128]{0:T(128)} %convert_element_type.107) | copy-start | bytes 1540
  95.3 7.2 %collective-permute-start = (bf16[1536,64]{0,1:T(8,128)(2,1)S(1)}, bf16[1536,64]{0,1:T(8,128)(2,1)S(1)}, u32[]{:S(2)}, u32[]{:S(2)}) collective-permute-start(bf16[1536,64]{0,1:T(8,128)(2,1)S(1)} %convolution_convert_fusion.3), channel_id=1, source_target_pairs={{0,1},{1,0},{2,3},{3,2},{4,5},{5,4},{6,7},{7,6},{8,9},{9,8},{10,11... | collective-permute-start | bytes 589832 | tf_op jit(solution)/shard_map/ppermute | solution.py:22
  102.6 9.1 %collective-permute-start.1 = (bf16[1536,128]{0,1:T(8,128)(2,1)S(1)}, bf16[1536,128]{0,1:T(8,128)(2,1)S(1)}, u32[]{:S(2)}, u32[]{:S(2)}) collective-permute-start(bf16[1536,128]{0,1:T(8,128)(2,1)S(1)} %maximum_select_fusion.1), channel_id=1, source_target_pairs={{0,2},{1,3},{2,0},{3,1},{4,6},{5,7},{6,4},{7,5},{8,10},{9,11},{10,... | collective-permute-start | bytes 1179656 | tf_op jit(solution)/shard_map/ppermute | solution.py:22
  116.7 8.2 %copy-start.5 = (bf16[1536,1,64]{0,2,1:T(8,128)(2,1)S(1)}, bf16[1536,1,64]{0,2,1:T(8,128)(2,1)}, u32[]{:S(2)}) copy-start(bf16[1536,1,64]{0,2,1:T(8,128)(2,1)} %get-tuple-element.129) | copy-start | bytes 589828
  116.7 8.2 %copy-start.6 = (bf16[1536,1,64]{0,2,1:T(8,128)(2,1)S(1)}, bf16[1536,1,64]{0,2,1:T(8,128)(2,1)}, u32[]{:S(2)}) copy-start(bf16[1536,1,64]{0,2,1:T(8,128)(2,1)} %get-tuple-element.130) | copy-start | bytes 589828
  116.7 8.2 %copy-start.4 = (bf16[3,1,512,128]{3,2,1,0:T(8,128)(2,1)S(1)}, bf16[3,1,512,128]{3,2,1,0:T(8,128)(2,1)}, u32[]{:S(2)}) copy-start(bf16[3,1,512,128]{3,2,1,0:T(8,128)(2,1)} %custom-call.4) | copy-start | bytes 1179652
  119.0 20.9 %all-to-all-start.1 = ((bf16[4,2,12288]{2,1,0:T(2,128)(2,1)}), bf16[4,2,12288]{2,1,0:T(2,128)(2,1)S(1)}, u32[]{:S(2)}, u32[]{:S(2)}) async-start(bf16[4,2,12288]{2,1,0:T(2,128)(2,1)} %reshape.454), calls=%async_computation.1 | async-start | bytes 393216 | tf_op jit(solution)/shard_map/all_to_all | solution.py:136
  126.3 2.1 copy-start.8
  131.3 2.1 copy-start.8
  136.2 2.1 copy-start.8
  150.2 9.4 %copy-start.10 = (bf16[2560]{0:T(1024)(128)(2,1)S(1)}, bf16[2560]{0:T(1024)(128)(2,1)}, u32[]{:S(2)}) copy-start(bf16[2560]{0:T(1024)(128)(2,1)} %param.23) | copy-start | bytes 15364
  150.2 133.7 %all-to-all-start.2 = ((bf16[32,48,2560]{2,1,0:T(8,128)(2,1)}), bf16[32,48,2560]{2,1,0:T(8,128)(2,1)}, u32[]{:S(2)}, u32[]{:S(2)}) async-start(bf16[32,48,2560]{2,1,0:T(8,128)(2,1)} %bitcast.89), calls=%async_computation.2 | async-start | bytes 15728640 | tf_op jit(solution)/shard_map/all_to_all | solution.py:27
  159.5 203.5 %all-gather.6.cloned.1.call-start = ((), (), s32[]{:S(2)}) async-start(), calls=%async_computation.6 | async-start | bytes 8355840 | tf_op jit(solution)/shard_map/all_gather | solution.py:33
  159.5 128.9 %copy-start.2 = (bf16[48,2560]{1,0:T(8,128)(2,1)S(1)}, bf16[48,2560]{1,0:T(8,128)(2,1)}, u32[]{:S(2)}) copy-start(bf16[48,2560]{1,0:T(8,128)(2,1)} %param.16) | copy-start | bytes 737284
  383.7 9.4 %copy-start.13 = (s32[6,1]{0,1:T(1,128)S(1)}, s32[6,1]{0,1:T(1,128)}, u32[]{:S(2)}) copy-start(s32[6,1]{0,1:T(1,128)} %copy-done.12) | copy-start | bytes 76
  383.7 131.5 %all-to-all-start.3 = ((bf16[32,48,2560]{2,1,0:T(8,128)(2,1)}), bf16[32,48,2560]{2,1,0:T(8,128)(2,1)}, u32[]{:S(2)}, u32[]{:S(2)}) async-start(bf16[32,48,2560]{2,1,0:T(8,128)(2,1)} %bitcast.90), calls=%async_computation.3 | async-start | bytes 15728640 | tf_op jit(solution)/shard_map/all_to_all | solution.py:27
  393.1 148.7 %copy-start.14 = (s32[16]{0:T(128)S(1)}, s32[16]{0:T(128)}, u32[]{:S(2)}) copy-start(s32[16]{0:T(128)} %param.19) | copy-start | bytes 196
  519.9 22.7 %copy-start.3 = (bf16[48,2560]{1,0:T(8,128)(2,1)}, bf16[48,2560]{1,0:T(8,128)(2,1)S(1)}, u32[]{:S(2)}) copy-start(bf16[48,2560]{1,0:T(8,128)(2,1)S(1)} %fusion.46) | copy-start | bytes 737284
  521.0 12.6 %all-to-all-start.4 = ((bf16[32,2,240]{2,1,0:T(2,128)(2,1)}), bf16[32,2,240]{2,1,0:T(2,128)(2,1)S(1)}, u32[]{:S(2)}, u32[]{:S(2)}) async-start(bf16[32,2,240]{2,1,0:T(2,128)(2,1)} %reshape.456), calls=%async_computation.4 | async-start | bytes 65536 | tf_op jit(solution)/shard_map/all_to_all | solution.py:27
Sparse Core Ops, SparseCore 0:
  20.4 68.9 all-gather.3
  297.6 65.3 all-gather.5

commit v4 on v2

--- a/solution.py
+++ b/solution.py
@@ -182,19 +182,40 @@
     gate_rows = jnp.dot(portion, w_gate, preferred_element_type=jnp.float32)
     upward = jnp.dot(portion, w_up, preferred_element_type=jnp.float32)
     hidden = (jax.nn.silu(gate_rows) * upward).astype(jnp.bfloat16)
-    mlp_sum = scatter_sum(
-        jnp.dot(hidden, w_down, preferred_element_type=jnp.float32).astype(jnp.bfloat16),
-        tensor_element_count,
-    )
-    layer_out = (resid.astype(jnp.float32) + mlp_sum).astype(jnp.bfloat16)
+    down = jnp.dot(hidden, w_down, preferred_element_type=jnp.float32).astype(jnp.bfloat16)
+    width = down.shape[1]
+    feat = width // tensor_element_count
+    nprompt = prompt_ends.shape[0]
+    end_pick = ((prompt_ends - 1)[:, None] == all_ids[None, :]).astype(jnp.bfloat16)
+    end_hidden = jnp.dot(end_pick, hidden, preferred_element_type=jnp.float32).astype(jnp.bfloat16)
+    end_down = jnp.dot(end_hidden, w_down, preferred_element_type=jnp.float32).astype(jnp.bfloat16)
     my_rows = my_index * tok_dev + jnp.arange(tok_dev, dtype=jnp.int32)
     select = ((prompt_ends - 1)[:, None] == my_rows[None, :]).astype(jnp.bfloat16)
-    end_terms = jnp.dot(select, layer_out, preferred_element_type=jnp.float32)
-    end_blocks = end_terms.astype(jnp.bfloat16).reshape(
-        end_terms.shape[0], tensor_element_count, -1
-    )
-    end_rows = scatter_sum(jnp.transpose(end_blocks, (1, 0, 2)), tensor_element_count)[0].astype(
-        jnp.bfloat16
+    end_resid = jnp.dot(select, resid, preferred_element_type=jnp.float32).astype(jnp.bfloat16)
+
+    def by_feature_block(rows):
+        blocks = rows.reshape(nprompt, tensor_element_count, feat)
+        return jnp.transpose(blocks, (1, 0, 2)).reshape(tensor_element_count, nprompt * feat)
+
+    extra = jnp.concatenate([by_feature_block(end_down), by_feature_block(end_resid)], axis=1)
+    extra_rows = -(-extra.shape[1] // width)
+    extra = jnp.pad(extra, ((0, 0), (0, extra_rows * width - extra.shape[1])))
+    payload = jnp.concatenate(
+        [
+            down.reshape(tensor_element_count, tok_dev, width),
+            extra.reshape(tensor_element_count, extra_rows, width),
+        ],
+        axis=1,
+    )
+    got = lax.all_to_all(payload, TENSOR, 0, 0, tiled=True)
+    summed = jnp.sum(got.astype(jnp.float32), axis=0)
+    mlp_sum = summed[:tok_dev]
+    layer_out = (resid.astype(jnp.float32) + mlp_sum).astype(jnp.bfloat16)
+    tail = summed[tok_dev:].reshape(-1)
+    end_rows = (
+        (tail[: nprompt * feat] + tail[nprompt * feat : 2 * nprompt * feat])
+        .reshape(nprompt, feat)
+        .astype(jnp.bfloat16)
     )
     table = lax.all_gather(end_rows, "dp", axis=0, tiled=True)
     pick = (request_prompt[:, None] == jnp.arange(table.shape[0], dtype=jnp.int32)[None, :]).astype(

time: 546 us -> 567 us (1.038)
  waiting for transfers between devices: 370 us -> 397 us
  other arithmetic: 25.1 us -> 34.3 us
  starting transfers between devices: 41.9 us -> 34.2 us
    all_to_all x0 -> x1, waiting for transfers between devices: none -> 149 us  [per_device(): got = lax.all_to_all(payload, TENSOR, 0, 0, tiled=True)]
    all_to_all x3 -> x1, waiting for transfers between devices: 232 us -> 113 us  [scatter_sum(): got = lax.all_to_all(pieces, TENSOR, 0, 0, tiled=True)]
    all_to_all x3 -> x1, starting transfers between devices: 25.4 us -> 9.25 us  [scatter_sum(): got = lax.all_to_all(pieces, TENSOR, 0, 0, tiled=True)]
    all_to_all x0 -> x1, starting transfers between devices: none -> 9.22 us  [per_device(): got = lax.all_to_all(payload, TENSOR, 0, 0, tiled=True)]
    concatenate x0 -> x1, other arithmetic: none -> 7.6 us  [per_device(): jnp.concatenate([down.reshape(tensor_element_count, tok_dev, width), extr...]
    dot_general x1, matrix products: 13.3 us -> 6.46 us  [per_device(): jnp.dot(hidden, w_down, preferred_element_type=jnp.float32)]
  transfers between devices with their start and end apart: 9 -> 8, of which waited for: 7 -> 6; matrix products, arithmetic and copies ran while one was open for 8% -> 7% of each run, Pallas kernels for 0% -> 0%
where the time goes in v4:
time: 567 us; the launch traced here: 566 us
  waiting for transfers between devices  397 us (70%)
  matrix products  44 us (8%)
  other arithmetic  34.3 us (6%)
  starting transfers between devices  34.2 us (6%)
  blocking collectives  23.5 us (4%)
  local copies, waits for them, and re-layouts  16.4 us (3%)
  between operations  14.5 us (3%)
    all_to_all x1, waiting for transfers between devices, per_device(): got = lax.all_to_all(payload, TENSOR, 0, 0, tiled=True)  149 us
    all_gather x2, waiting for transfers between devices, gather_rows(): return lax.all_gather(rows, ('ty', 'tx'), axis=0, tiled=True)  126 us
    all_to_all x1, waiting for transfers between devices, scatter_sum(): got = lax.all_to_all(pieces, TENSOR, 0, 0, tiled=True)  113 us
    all_gather x2, blocking collectives, gather_rows(): rows = lax.all_gather(rows, 'tz', axis=0, tiled=True)  17.3 us
  transfers between devices with their start and end apart: 8, of which 6 were waited for; matrix products, arithmetic and copies ran while one was open for 7% of the time, Pallas kernels for 0%

profile of v4, /device:TPU:27, one launch (start us, length us, event | category | flops | bytes accessed | tf_op | source)
XLA Modules:
  0.0 565.8 jit_solution(16884610319791853713)
XLA Ops:
  10.2 10.0 %all_gather.15 = bf16[96,2560]{1,0:T(8,128)(2,1)} all-gather(bf16[48,2560]{1,0:T(8,128)(2,1)S(1)} %fusion.41), channel_id=1, replica_groups=mesh['dp'=4,'ty'=4,'tx'=4,'tz'=2] {'tz'}, dimensions={0}, use_global_device_ids=true | all-gather | bytes 737280 | tf_op jit(solution)/shard_map/all_gather | solution.py:32
  23.9 65.5 %all-gather.4.cloned.1.call-done = bf16[1536,2560]{1,0:T(8,128)(2,1)} async-done(((bf16[96,2560]{1,0:T(8,128)(2,1)}), bf16[1536,2560]{1,0:T(8,128)(2,1)}) %all-gather.4.cloned.1.call-update) | async-done | bytes 7864336 | tf_op jit(solution)/shard_map/all_gather | solution.py:33
  89.4 5.9 %convolution_convert_fusion.4 = bf16[1536,64]{0,1:T(8,128)(2,1)S(1)} fusion(bf16[1536,2560]{1,0:T(8,128)(2,1)} %all-gather.4.cloned.1.call-done, bf16[2560,64]{0,1:T(8,128)(2,1)} %param.25), kind=kOutput, calls=%fused_computation.34 | convolution fusion | flops 503414784 | bytes 8388608 | tf_op jit(solution)/shard_map/dot_general | solution.py:94
  95.2 2.9 collective-permute-start
  98.2 2.7 multiply_reduce_fusion
  102.5 1.6 collective-permute-start.1
  104.2 7.4 %collective-permute-done.1 = bf16[1536,128]{0,1:T(8,128)(2,1)S(1)} collective-permute-done((bf16[1536,128]{0,1:T(8,128)(2,1)S(1)}, bf16[1536,128]{0,1:T(8,128)(2,1)S(1)}, u32[]{:S(2)}, u32[]{:S(2)}) %collective-permute-start.1) | collective-permute-done | bytes 393248 | tf_op jit(solution)/shard_map/ppermute | solution.py:22
  113.0 3.1 fusion.60
  118.8 19.7 %while.11 = (s32[]{:T(128)}, bf16[3,1,512,128]{3,2,1,0:T(8,128)(2,1)}, s32[3]{0:T(128)S(1)}, s32[1536]{0:T(1024)S(1)}, bf16[1536,1,128]{0,2,1:T(8,128)(2,1)S(1)}...) while((s32[]{:T(128)}, ...), condition=%wide.region_9.10_spmd.clone, body=%wide.region_6.9_spmd.clone.sunk | while | flops 416939520 | bytes 12107995 | solution.py:174
  120.1 2.1 select_reduce_fusion.4
  123.3 2.1 fusion.106
  126.7 2.1 select_reduce_fusion.4
  129.9 2.0 fusion.106
  133.2 2.1 select_reduce_fusion.4
  136.4 2.0 fusion.106
  138.5 6.3 %convolution_convert_fusion.1 = bf16[1536,2560]{1,0:T(8,128)(2,1)} fusion(bf16[1536,128]{1,0:T(8,128)(2,1)} %bitcast.99, bf16[128,2560]{1,0:T(8,128)(2,1)S(1)} %copy-done.6), kind=kOutput, calls=%fused_computation.28 | convolution fusion | flops 1010565120 | bytes 8912896 | tf_op jit(solution)/shard_map/dot_general | solution.py:177
  144.7 9.3 %all-to-all-start = ((bf16[32,48,2560]{2,1,0:T(8,128)(2,1)}), bf16[32,48,2560]{2,1,0:T(8,128)(2,1)}, u32[]{:S(2)}, u32[]{:S(2)}) async-start(bf16[32,48,2560]{2,1,0:T(8,128)(2,1)} %bitcast.94), calls=%async_computation | async-start | bytes 15728640 | tf_op jit(solution)/shard_map/all_to_all | solution.py:27
  154.3 112.6 %all-to-all-done = bf16[32,48,2560]{2,1,0:T(8,128)(2,1)} async-done(((bf16[32,48,2560]{2,1,0:T(8,128)(2,1)}), bf16[32,48,2560]{2,1,0:T(8,128)(2,1)}, u32[]{:S(2)}, u32[]{:S(2)}) %all-to-all-start) | async-done | bytes 7864352 | tf_op jit(solution)/shard_map/all_to_all | solution.py:27
  266.9 4.5 convert_reduce_fusion.1
  271.8 7.3 %all_gather.17 = bf16[96,2560]{1,0:T(8,128)(2,1)} all-gather(bf16[48,2560]{1,0:T(8,128)(2,1)S(1)} %fusion.45), channel_id=1, replica_groups=mesh['dp'=4,'ty'=4,'tx'=4,'tz'=2] {'tz'}, dimensions={0}, use_global_device_ids=true | all-gather | bytes 737280 | tf_op jit(solution)/shard_map/all_gather | solution.py:32
  282.4 6.7 %all-to-all-start.2 = ((s32[4,1,24]{2,1,0:T(1,128)}), s32[4,1,24]{2,1,0:T(1,128)S(1)}, u32[]{:S(2)}, u32[]{:S(2)}) async-start(s32[4,1,24]{2,1,0:T(1,128)} %bitcast.14), calls=%async_computation.2 | async-start | bytes 4096 | tf_op jit(solution)/shard_map/all_to_all | solution.py:137
  291.7 60.8 %all-gather.6.cloned.1.call-done = bf16[1536,2560]{1,0:T(8,128)(2,1)} async-done(((bf16[96,2560]{1,0:T(8,128)(2,1)}), bf16[1536,2560]{1,0:T(8,128)(2,1)}) %all-gather.6.cloned.1.call-update) | async-done | bytes 7864336 | tf_op jit(solution)/shard_map/all_gather | solution.py:33
  352.5 5.6 fusion.78
  358.9 2.7 fusion.27
  362.5 6.5 %convolution_convert_fusion = bf16[1536,2560]{1,0:T(8,128)(2,1)} fusion(bf16[1536,304]{0,1:T(8,128)(2,1)S(1)} %fusion.27, bf16[304,2560]{1,0:T(8,128)(2,1)S(1)} %copy-done), kind=kOutput, calls=%fused_computation.27 | convolution fusion | flops 2394685440 | bytes 10354688 | tf_op jit(solution)/shard_map/dot_general | solution.py:185
  369.6 4.2 all-to-all-start.3
  373.8 7.6 %pad_maximum_fusion = bf16[32,49,2560]{2,1,0:T(8,128)(2,1)} fusion(bf16[32,1,2560]{2,1,0:T(2,128)(2,1)S(1)} %copy.44, bf16[32,48,2560]{2,1,0:T(8,128)(2,1)} %bitcast.95), kind=kLoop, calls=%fused_computation.29 | loop fusion | flops 16056320 | bytes 16056320 | tf_op jit(solution)/shard_map/concatenate | solution.py:203
  381.4 9.2 %all-to-all-start.1 = ((bf16[32,49,2560]{2,1,0:T(8,128)(2,1)}), bf16[32,49,2560]{2,1,0:T(8,128)(2,1)}, u32[]{:S(2)}, u32[]{:S(2)}) async-start(bf16[32,49,2560]{2,1,0:T(8,128)(2,1)} %pad_maximum_fusion), calls=%async_computation.1 | async-start | bytes 18350080 | tf_op jit(solution)/shard_map/all_to_all | solution.py:210
  392.2 3.5 scatter_fusion
  396.8 149.0 %all-to-all-done.1 = bf16[32,49,2560]{2,1,0:T(8,128)(2,1)} async-done(((bf16[32,49,2560]{2,1,0:T(8,128)(2,1)}), bf16[32,49,2560]{2,1,0:T(8,128)(2,1)}, u32[]{:S(2)}, u32[]{:S(2)}) %all-to-all-start.1) | async-done | bytes 8028192 | tf_op jit(solution)/shard_map/all_to_all | solution.py:210
  545.8 5.2 convert_reduce_fusion
  551.9 6.2 %all-gather = bf16[4,6,80]{2,1,0:T(8,128)(2,1)S(1)} all-gather(bf16[1,6,80]{2,1,0:T(8,128)(2,1)S(1)} %reshape.457), channel_id=1, replica_groups=mesh['dp'=4,'ty'=4,'tx'=4,'tz'=2] {'dp'}, dimensions={0}, use_global_device_ids=true | all-gather | bytes 4800 | tf_op jit(solution)/shard_map/all_gather | solution.py:220
  (117 shorter events, 30.5 us)
Async XLA Ops:
  7.2 354.4 %copy-start = (bf16[304,2560]{1,0:T(8,128)(2,1)S(1)}, bf16[304,2560]{1,0:T(8,128)(2,1)}, u32[]{:S(2)}) copy-start(bf16[304,2560]{1,0:T(8,128)(2,1)} %param.29) | copy-start | bytes 4669444
  7.2 82.2 %all-gather.4.cloned.1.call-start = ((), (), s32[]{:S(2)}) async-start(), calls=%async_computation.4 | async-start | bytes 8355840 | tf_op jit(solution)/shard_map/all_gather | solution.py:33
  23.8 74.3 %copy-start.5 = (bf16[2560,128]{1,0:T(8,128)(2,1)S(1)}, bf16[2560,128]{1,0:T(8,128)(2,1)}, u32[]{:S(2)}) copy-start(bf16[2560,128]{1,0:T(8,128)(2,1)} %param.24) | copy-start | bytes 1966084
  89.4 8.8 %copy-start.1 = (bf16[1536,2560]{1,0:T(8,128)(2,1)S(1)}, bf16[1536,2560]{1,0:T(8,128)(2,1)}, u32[]{:S(2)}) copy-start(bf16[1536,2560]{1,0:T(8,128)(2,1)} %all-gather.4.cloned.1.call-done) | copy-start | bytes 23592964
  95.2 7.2 %collective-permute-start = (bf16[1536,64]{0,1:T(8,128)(2,1)S(1)}, bf16[1536,64]{0,1:T(8,128)(2,1)S(1)}, u32[]{:S(2)}, u32[]{:S(2)}) collective-permute-start(bf16[1536,64]{0,1:T(8,128)(2,1)S(1)} %convolution_convert_fusion.4), channel_id=1, source_target_pairs={{0,1},{1,0},{2,3},{3,2},{4,5},{5,4},{6,7},{7,6},{8,9},{9,8},{10,11... | collective-permute-start | bytes 589832 | tf_op jit(solution)/shard_map/ppermute | solution.py:22
  102.5 9.1 %collective-permute-start.1 = (bf16[1536,128]{0,1:T(8,128)(2,1)S(1)}, bf16[1536,128]{0,1:T(8,128)(2,1)S(1)}, u32[]{:S(2)}, u32[]{:S(2)}) collective-permute-start(bf16[1536,128]{0,1:T(8,128)(2,1)S(1)} %maximum_select_fusion.1), channel_id=1, source_target_pairs={{0,2},{1,3},{2,0},{3,1},{4,6},{5,7},{6,4},{7,5},{8,10},{9,11},{10,... | collective-permute-start | bytes 1179656 | tf_op jit(solution)/shard_map/ppermute | solution.py:22
  116.1 0.7 copy-start.3
  118.8 19.7 %copy-start.6 = (bf16[128,2560]{1,0:T(8,128)(2,1)S(1)}, bf16[128,2560]{1,0:T(8,128)(2,1)}, u32[]{:S(2)}) copy-start(bf16[128,2560]{1,0:T(8,128)(2,1)} %param.26) | copy-start | bytes 1966084
  120.1 3.2 copy-start.7
  126.7 3.2 copy-start.7
  133.2 3.2 copy-start.7
  144.7 9.5 %copy-start.8 = (bf16[2560]{0:T(1024)(128)(2,1)S(1)}, bf16[2560]{0:T(1024)(128)(2,1)}, u32[]{:S(2)}) copy-start(bf16[2560]{0:T(1024)(128)(2,1)} %param.23) | copy-start | bytes 15364
  144.7 122.2 %all-to-all-start = ((bf16[32,48,2560]{2,1,0:T(8,128)(2,1)}), bf16[32,48,2560]{2,1,0:T(8,128)(2,1)}, u32[]{:S(2)}, u32[]{:S(2)}) async-start(bf16[32,48,2560]{2,1,0:T(8,128)(2,1)} %bitcast.94), calls=%async_computation | async-start | bytes 15728640 | tf_op jit(solution)/shard_map/all_to_all | solution.py:27
  154.0 198.5 %all-gather.6.cloned.1.call-start = ((), (), s32[]{:S(2)}) async-start(), calls=%async_computation.5 | async-start | bytes 8355840 | tf_op jit(solution)/shard_map/all_gather | solution.py:33
  154.2 117.2 %copy-start.2 = (bf16[48,2560]{1,0:T(8,128)(2,1)S(1)}, bf16[48,2560]{1,0:T(8,128)(2,1)}, u32[]{:S(2)}) copy-start(bf16[48,2560]{1,0:T(8,128)(2,1)} %param.16) | copy-start | bytes 737284
  154.3 124.9 %copy-start.11 = (s32[96]{0:T(128)S(1)}, s32[96]{0:T(128)}, u32[]{:S(2)}) copy-start(s32[96]{0:T(128)} %param.18) | copy-start | bytes 1156
  271.5 17.7 %copy-start.4 = (bf16[1536,64]{0,1:T(8,128)(2,1)S(1)}, bf16[1536,64]{0,1:T(8,128)(2,1)}, u32[]{:S(2)}) copy-start(bf16[1536,64]{0,1:T(8,128)(2,1)} %copy-done.3) | copy-start | bytes 589828
  282.4 87.2 %all-to-all-start.2 = ((s32[4,1,24]{2,1,0:T(1,128)}), s32[4,1,24]{2,1,0:T(1,128)S(1)}, u32[]{:S(2)}, u32[]{:S(2)}) async-start(s32[4,1,24]{2,1,0:T(1,128)} %bitcast.14), calls=%async_computation.2 | async-start | bytes 4096 | tf_op jit(solution)/shard_map/all_to_all | solution.py:137
  352.5 6.0 %copy-start.9 = (bf16[1536,2560]{1,0:T(8,128)(2,1)S(1)}, bf16[1536,2560]{1,0:T(8,128)(2,1)}, u32[]{:S(2)}) copy-start(bf16[1536,2560]{1,0:T(8,128)(2,1)} %all-gather.6.cloned.1.call-done) | copy-start | bytes 23592964
  352.5 6.4 %copy-start.10 = (bf16[2560,304]{0,1:T(8,128)(2,1)S(1)}, bf16[2560,304]{0,1:T(8,128)(2,1)}, u32[]{:S(2)}) copy-start(bf16[2560,304]{0,1:T(8,128)(2,1)} %param.28) | copy-start | bytes 4669444
  369.6 11.8 %all-to-all-start.3 = ((bf16[4,2,12288]{2,1,0:T(2,128)(2,1)}), bf16[4,2,12288]{2,1,0:T(2,128)(2,1)S(1)}, u32[]{:S(2)}, u32[]{:S(2)}) async-start(bf16[4,2,12288]{2,1,0:T(2,128)(2,1)} %reshape.474), calls=%async_computation.3 | async-start | bytes 393216 | tf_op jit(solution)/shard_map/all_to_all | solution.py:136
  381.4 164.4 %all-to-all-start.1 = ((bf16[32,49,2560]{2,1,0:T(8,128)(2,1)}), bf16[32,49,2560]{2,1,0:T(8,128)(2,1)}, u32[]{:S(2)}, u32[]{:S(2)}) async-start(bf16[32,49,2560]{2,1,0:T(8,128)(2,1)} %pad_maximum_fusion), calls=%async_computation.1 | async-start | bytes 18350080 | tf_op jit(solution)/shard_map/all_to_all | solution.py:210
  396.8 161.4 %copy-start.12 = (s32[16]{0:T(128)S(1)}, s32[16]{0:T(128)}, u32[]{:S(2)}) copy-start(s32[16]{0:T(128)} %param.19) | copy-start | bytes 196
Sparse Core Ops, SparseCore 0:
  20.4 68.9 all-gather.3
  279.3 73.1 all-gather.5

commit v5 on v4

--- a/solution.py
+++ b/solution.py
@@ -179,6 +179,7 @@
     )
     resid = (stream.astype(jnp.float32) + attn_sum).astype(jnp.bfloat16)
     portion = gather_rows(row_norm(resid, mlp_gain).astype(jnp.bfloat16))
+    paged_key_value_cache, portion = lax.optimization_barrier((paged_key_value_cache, portion))
     gate_rows = jnp.dot(portion, w_gate, preferred_element_type=jnp.float32)
     upward = jnp.dot(portion, w_up, preferred_element_type=jnp.float32)
     hidden = (jax.nn.silu(gate_rows) * upward).astype(jnp.bfloat16)

time: 567 us -> 558 us (0.984)
  waiting for transfers between devices: 397 us -> 388 us
    all_gather x2, waiting for transfers between devices: 126 us -> 110 us  [gather_rows(): return lax.all_gather(rows, ('ty', 'tx'), axis=0, tiled=True)]
  transfers between devices with their start and end apart: 8 -> 8, of which waited for: 6 -> 8; matrix products, arithmetic and copies ran while one was open for 7% -> 3% of each run, Pallas kernels for 0% -> 0%
where the time goes in v5:
time: 558 us; the launch traced here: 557 us
  waiting for transfers between devices  388 us (70%)
  matrix products  44 us (8%)
  other arithmetic  34.3 us (6%)
  starting transfers between devices  34 us (6%)
  blocking collectives  23.9 us (4%)
  local copies, waits for them, and re-layouts  16.3 us (3%)
  between operations  14.5 us (3%)
    all_to_all x1, waiting for transfers between devices, per_device(): got = lax.all_to_all(payload, TENSOR, 0, 0, tiled=True)  149 us
    all_to_all x1, waiting for transfers between devices, scatter_sum(): got = lax.all_to_all(pieces, TENSOR, 0, 0, tiled=True)  113 us
    all_gather x2, waiting for transfers between devices, gather_rows(): return lax.all_gather(rows, ('ty', 'tx'), axis=0, tiled=True)  110 us
    all_gather x2, blocking collectives, gather_rows(): rows = lax.all_gather(rows, 'tz', axis=0, tiled=True)  17.3 us
  transfers between devices with their start and end apart: 8, of which 8 were waited for; matrix products, arithmetic and copies ran while one was open for 3% of the time, Pallas kernels for 0%

profile of v5, /device:TPU:27, one launch (start us, length us, event | category | flops | bytes accessed | tf_op | source)
XLA Modules:
  0.0 557.2 jit_solution(1373693248494202912)
XLA Ops:
  10.2 10.0 %all_gather.15 = bf16[96,2560]{1,0:T(8,128)(2,1)} all-gather(bf16[48,2560]{1,0:T(8,128)(2,1)S(1)} %fusion.41), channel_id=1, replica_groups=mesh['dp'=4,'ty'=4,'tx'=4,'tz'=2] {'tz'}, dimensions={0}, use_global_device_ids=true | all-gather | bytes 737280 | tf_op jit(solution)/shard_map/all_gather | solution.py:32
  23.9 65.5 %all-gather.4.cloned.1.call-done = bf16[1536,2560]{1,0:T(8,128)(2,1)} async-done(((bf16[96,2560]{1,0:T(8,128)(2,1)}), bf16[1536,2560]{1,0:T(8,128)(2,1)}) %all-gather.4.cloned.1.call-update) | async-done | bytes 7864336 | tf_op jit(solution)/shard_map/all_gather | solution.py:33
  89.4 5.9 %convolution_convert_fusion.4 = bf16[1536,64]{0,1:T(8,128)(2,1)S(1)} fusion(bf16[1536,2560]{1,0:T(8,128)(2,1)} %all-gather.4.cloned.1.call-done, bf16[2560,64]{0,1:T(8,128)(2,1)} %param.25), kind=kOutput, calls=%fused_computation.34 | convolution fusion | flops 503414784 | bytes 8388608 | tf_op jit(solution)/shard_map/dot_general | solution.py:94
  95.2 2.9 collective-permute-start
  98.2 2.7 multiply_reduce_fusion
  104.2 7.4 %collective-permute-done.1 = bf16[1536,128]{0,1:T(8,128)(2,1)S(1)} collective-permute-done((bf16[1536,128]{0,1:T(8,128)(2,1)S(1)}, bf16[1536,128]{0,1:T(8,128)(2,1)S(1)}, u32[]{:S(2)}, u32[]{:S(2)}) %collective-permute-start.1) | collective-permute-done | bytes 393248 | tf_op jit(solution)/shard_map/ppermute | solution.py:22
  113.0 3.1 fusion.60
  118.8 19.7 %while.11 = (s32[]{:T(128)}, bf16[3,1,512,128]{3,2,1,0:T(8,128)(2,1)}, s32[3]{0:T(128)S(1)}, s32[1536]{0:T(1024)S(1)}, bf16[1536,1,128]{0,2,1:T(8,128)(2,1)S(1)}...) while((s32[]{:T(128)}, ...), condition=%wide.region_9.10_spmd.clone, body=%wide.region_6.9_spmd.clone.sunk | while | flops 416939520 | bytes 12107995 | solution.py:174
  120.1 2.1 select_reduce_fusion.4
  123.3 2.1 fusion.106
  126.7 2.1 select_reduce_fusion.4
  133.2 2.1 select_reduce_fusion.4
  136.4 2.0 fusion.106
  138.5 6.3 %convolution_convert_fusion.1 = bf16[1536,2560]{1,0:T(8,128)(2,1)} fusion(bf16[1536,128]{1,0:T(8,128)(2,1)} %bitcast.99, bf16[128,2560]{1,0:T(8,128)(2,1)S(1)} %copy-done.6), kind=kOutput, calls=%fused_computation.28 | convolution fusion | flops 1010565120 | bytes 8912896 | tf_op jit(solution)/shard_map/dot_general | solution.py:177
  144.7 9.3 %all-to-all-start = ((bf16[32,48,2560]{2,1,0:T(8,128)(2,1)}), bf16[32,48,2560]{2,1,0:T(8,128)(2,1)}, u32[]{:S(2)}, u32[]{:S(2)}) async-start(bf16[32,48,2560]{2,1,0:T(8,128)(2,1)} %bitcast.94), calls=%async_computation | async-start | bytes 15728640 | tf_op jit(solution)/shard_map/all_to_all | solution.py:27
  154.3 112.6 %all-to-all-done = bf16[32,48,2560]{2,1,0:T(8,128)(2,1)} async-done(((bf16[32,48,2560]{2,1,0:T(8,128)(2,1)}), bf16[32,48,2560]{2,1,0:T(8,128)(2,1)}, u32[]{:S(2)}, u32[]{:S(2)}) %all-to-all-start) | async-done | bytes 7864352 | tf_op jit(solution)/shard_map/all_to_all | solution.py:27
  266.9 4.5 convert_reduce_fusion.1
  271.8 7.3 %all_gather.17 = bf16[96,2560]{1,0:T(8,128)(2,1)} all-gather(bf16[48,2560]{1,0:T(8,128)(2,1)S(1)} %fusion.45), channel_id=1, replica_groups=mesh['dp'=4,'ty'=4,'tx'=4,'tz'=2] {'tz'}, dimensions={0}, use_global_device_ids=true | all-gather | bytes 737280 | tf_op jit(solution)/shard_map/all_gather | solution.py:32
  282.4 6.7 %all-to-all-start.1 = ((s32[4,1,24]{2,1,0:T(1,128)}), s32[4,1,24]{2,1,0:T(1,128)S(1)}, u32[]{:S(2)}, u32[]{:S(2)}) async-start(s32[4,1,24]{2,1,0:T(1,128)} %bitcast.10), calls=%async_computation.1 | async-start | bytes 4096 | tf_op jit(solution)/shard_map/all_to_all | solution.py:137
  289.1 3.0 all-to-all-done.1
  295.5 4.0 all-to-all-start.2
  299.5 4.5 all-to-all-done.2
  304.4 3.5 scatter_fusion
  308.3 44.2 %all-gather.6.cloned.1.call-done = bf16[1536,2560]{1,0:T(8,128)(2,1)} async-done(((bf16[96,2560]{1,0:T(8,128)(2,1)}), bf16[1536,2560]{1,0:T(8,128)(2,1)}) %all-gather.6.cloned.1.call-update) | async-done | bytes 7864336 | tf_op jit(solution)/shard_map/all_gather | solution.py:33
  352.5 5.6 %fusion.78 = f32[1536,304]{0,1:T(8,128)S(1)} fusion(bf16[1536,2560]{1,0:T(8,128)(2,1)} %all-gather.6.cloned.1.call-done, bf16[2560,304]{0,1:T(8,128)(2,1)} %param.27), kind=kOutput, calls=%fused_computation.132 | convolution fusion | flops 2390753280 | bytes 11288576 | tf_op jit(solution)/shard_map/dot_general | solution.py:183
  358.9 2.7 fusion.27
  362.5 6.5 %convolution_convert_fusion = bf16[1536,2560]{1,0:T(8,128)(2,1)} fusion(bf16[1536,304]{0,1:T(8,128)(2,1)S(1)} %fusion.27, bf16[304,2560]{1,0:T(8,128)(2,1)S(1)} %copy-done), kind=kOutput, calls=%fused_computation.27 | convolution fusion | flops 2394685440 | bytes 10354688 | tf_op jit(solution)/shard_map/dot_general | solution.py:186
  369.6 7.6 %pad_maximum_fusion = bf16[32,49,2560]{2,1,0:T(8,128)(2,1)} fusion(bf16[32,1,2560]{2,1,0:T(2,128)(2,1)S(1)} %copy.46, bf16[32,48,2560]{2,1,0:T(8,128)(2,1)} %bitcast.95), kind=kLoop, calls=%fused_computation.29 | loop fusion | flops 16056320 | bytes 16056320 | tf_op jit(solution)/shard_map/concatenate | solution.py:204
  377.2 9.2 %all-to-all-start.3 = ((bf16[32,49,2560]{2,1,0:T(8,128)(2,1)}), bf16[32,49,2560]{2,1,0:T(8,128)(2,1)}, u32[]{:S(2)}, u32[]{:S(2)}) async-start(bf16[32,49,2560]{2,1,0:T(8,128)(2,1)} %pad_maximum_fusion), calls=%async_computation.3 | async-start | bytes 18350080 | tf_op jit(solution)/shard_map/all_to_all | solution.py:211
  387.5 149.3 %all-to-all-done.3 = bf16[32,49,2560]{2,1,0:T(8,128)(2,1)} async-done(((bf16[32,49,2560]{2,1,0:T(8,128)(2,1)}), bf16[32,49,2560]{2,1,0:T(8,128)(2,1)}, u32[]{:S(2)}, u32[]{:S(2)}) %all-to-all-start.3) | async-done | bytes 8028192 | tf_op jit(solution)/shard_map/all_to_all | solution.py:211
  536.8 5.2 convert_reduce_fusion
  542.9 6.6 %all-gather = bf16[4,6,80]{2,1,0:T(8,128)(2,1)S(1)} all-gather(bf16[1,6,80]{2,1,0:T(8,128)(2,1)S(1)} %reshape.457), channel_id=1, replica_groups=mesh['dp'=4,'ty'=4,'tx'=4,'tz'=2] {'dp'}, dimensions={0}, use_global_device_ids=true | all-gather | bytes 4800 | tf_op jit(solution)/shard_map/all_gather | solution.py:221
  (117 shorter events, 34.1 us)
Async XLA Ops:
  7.2 354.4 %copy-start = (bf16[304,2560]{1,0:T(8,128)(2,1)S(1)}, bf16[304,2560]{1,0:T(8,128)(2,1)}, u32[]{:S(2)}) copy-start(bf16[304,2560]{1,0:T(8,128)(2,1)} %param.29) | copy-start | bytes 4669444
  7.2 82.2 %all-gather.4.cloned.1.call-start = ((), (), s32[]{:S(2)}) async-start(), calls=%async_computation.4 | async-start | bytes 8355840 | tf_op jit(solution)/shard_map/all_gather | solution.py:33
  23.8 74.3 %copy-start.5 = (bf16[2560,128]{1,0:T(8,128)(2,1)S(1)}, bf16[2560,128]{1,0:T(8,128)(2,1)}, u32[]{:S(2)}) copy-start(bf16[2560,128]{1,0:T(8,128)(2,1)} %param.24) | copy-start | bytes 1966084
  89.4 8.8 %copy-start.1 = (bf16[1536,2560]{1,0:T(8,128)(2,1)S(1)}, bf16[1536,2560]{1,0:T(8,128)(2,1)}, u32[]{:S(2)}) copy-start(bf16[1536,2560]{1,0:T(8,128)(2,1)} %all-gather.4.cloned.1.call-done) | copy-start | bytes 23592964
  95.2 7.2 %collective-permute-start = (bf16[1536,64]{0,1:T(8,128)(2,1)S(1)}, bf16[1536,64]{0,1:T(8,128)(2,1)S(1)}, u32[]{:S(2)}, u32[]{:S(2)}) collective-permute-start(bf16[1536,64]{0,1:T(8,128)(2,1)S(1)} %convolution_convert_fusion.4), channel_id=1, source_target_pairs={{0,1},{1,0},{2,3},{3,2},{4,5},{5,4},{6,7},{7,6},{8,9},{9,8},{10,11... | collective-permute-start | bytes 589832 | tf_op jit(solution)/shard_map/ppermute | solution.py:22
  102.5 9.1 %collective-permute-start.1 = (bf16[1536,128]{0,1:T(8,128)(2,1)S(1)}, bf16[1536,128]{0,1:T(8,128)(2,1)S(1)}, u32[]{:S(2)}, u32[]{:S(2)}) collective-permute-start(bf16[1536,128]{0,1:T(8,128)(2,1)S(1)} %maximum_select_fusion.1), channel_id=1, source_target_pairs={{0,2},{1,3},{2,0},{3,1},{4,6},{5,7},{6,4},{7,5},{8,10},{9,11},{10,... | collective-permute-start | bytes 1179656 | tf_op jit(solution)/shard_map/ppermute | solution.py:22
  116.1 0.7 copy-start.3
  118.8 19.7 %copy-start.6 = (bf16[128,2560]{1,0:T(8,128)(2,1)S(1)}, bf16[128,2560]{1,0:T(8,128)(2,1)}, u32[]{:S(2)}) copy-start(bf16[128,2560]{1,0:T(8,128)(2,1)} %param.26) | copy-start | bytes 1966084
  120.1 3.2 copy-start.7
  126.7 3.2 copy-start.7
  133.2 3.2 copy-start.7
  144.7 9.5 %copy-start.8 = (bf16[2560]{0:T(1024)(128)(2,1)S(1)}, bf16[2560]{0:T(1024)(128)(2,1)}, u32[]{:S(2)}) copy-start(bf16[2560]{0:T(1024)(128)(2,1)} %param.23) | copy-start | bytes 15364
  144.7 122.2 %all-to-all-start = ((bf16[32,48,2560]{2,1,0:T(8,128)(2,1)}), bf16[32,48,2560]{2,1,0:T(8,128)(2,1)}, u32[]{:S(2)}, u32[]{:S(2)}) async-start(bf16[32,48,2560]{2,1,0:T(8,128)(2,1)} %bitcast.94), calls=%async_computation | async-start | bytes 15728640 | tf_op jit(solution)/shard_map/all_to_all | solution.py:27
  154.0 198.5 %all-gather.6.cloned.1.call-start = ((), (), s32[]{:S(2)}) async-start(), calls=%async_computation.5 | async-start | bytes 8355840 | tf_op jit(solution)/shard_map/all_gather | solution.py:33
  154.2 117.2 %copy-start.2 = (bf16[48,2560]{1,0:T(8,128)(2,1)S(1)}, bf16[48,2560]{1,0:T(8,128)(2,1)}, u32[]{:S(2)}) copy-start(bf16[48,2560]{1,0:T(8,128)(2,1)} %param.16) | copy-start | bytes 737284
  154.3 124.9 %copy-start.11 = (s32[96]{0:T(128)S(1)}, s32[96]{0:T(128)}, u32[]{:S(2)}) copy-start(s32[96]{0:T(128)} %param.18) | copy-start | bytes 1156
  271.5 22.0 %copy-start.4 = (bf16[1536,64]{0,1:T(8,128)(2,1)S(1)}, bf16[1536,64]{0,1:T(8,128)(2,1)}, u32[]{:S(2)}) copy-start(bf16[1536,64]{0,1:T(8,128)(2,1)} %copy-done.3) | copy-start | bytes 589828
  282.4 9.8 %all-to-all-start.1 = ((s32[4,1,24]{2,1,0:T(1,128)}), s32[4,1,24]{2,1,0:T(1,128)S(1)}, u32[]{:S(2)}, u32[]{:S(2)}) async-start(s32[4,1,24]{2,1,0:T(1,128)} %bitcast.10), calls=%async_computation.1 | async-start | bytes 4096 | tf_op jit(solution)/shard_map/all_to_all | solution.py:137
  295.5 8.5 %all-to-all-start.2 = ((bf16[4,2,12288]{2,1,0:T(2,128)(2,1)}), bf16[4,2,12288]{2,1,0:T(2,128)(2,1)S(1)}, u32[]{:S(2)}, u32[]{:S(2)}) async-start(bf16[4,2,12288]{2,1,0:T(2,128)(2,1)} %reshape.474), calls=%async_computation.2 | async-start | bytes 393216 | tf_op jit(solution)/shard_map/all_to_all | solution.py:136
  352.5 6.0 %copy-start.9 = (bf16[1536,2560]{1,0:T(8,128)(2,1)S(1)}, bf16[1536,2560]{1,0:T(8,128)(2,1)}, u32[]{:S(2)}) copy-start(bf16[1536,2560]{1,0:T(8,128)(2,1)} %all-gather.6.cloned.1.call-done) | copy-start | bytes 23592964
  352.5 6.4 %copy-start.10 = (bf16[2560,304]{0,1:T(8,128)(2,1)S(1)}, bf16[2560,304]{0,1:T(8,128)(2,1)}, u32[]{:S(2)}) copy-start(bf16[2560,304]{0,1:T(8,128)(2,1)} %param.28) | copy-start | bytes 4669444
  377.2 159.5 %all-to-all-start.3 = ((bf16[32,49,2560]{2,1,0:T(8,128)(2,1)}), bf16[32,49,2560]{2,1,0:T(8,128)(2,1)}, u32[]{:S(2)}, u32[]{:S(2)}) async-start(bf16[32,49,2560]{2,1,0:T(8,128)(2,1)} %pad_maximum_fusion), calls=%async_computation.3 | async-start | bytes 18350080 | tf_op jit(solution)/shard_map/all_to_all | solution.py:211
  387.5 162.1 %copy-start.12 = (s32[16]{0:T(128)S(1)}, s32[16]{0:T(128)}, u32[]{:S(2)}) copy-start(s32[16]{0:T(128)} %param.19) | copy-start | bytes 196
Sparse Core Ops, SparseCore 0:
  20.4 68.9 all-gather.3
  279.3 73.1 all-gather.5

commit v6 on v5

--- a/solution.py
+++ b/solution.py
@@ -202,14 +202,10 @@
     extra_rows = -(-extra.shape[1] // width)
     extra = jnp.pad(extra, ((0, 0), (0, extra_rows * width - extra.shape[1])))
     payload = jnp.concatenate(
-        [
-            down.reshape(tensor_element_count, tok_dev, width),
-            extra.reshape(tensor_element_count, extra_rows, width),
-        ],
-        axis=1,
+        [down.reshape(tensor_element_count, tok_dev * width), extra], axis=1
     )
     got = lax.all_to_all(payload, TENSOR, 0, 0, tiled=True)
-    summed = jnp.sum(got.astype(jnp.float32), axis=0)
+    summed = jnp.sum(got.astype(jnp.float32), axis=0).reshape(tok_dev + extra_rows, width)
     mlp_sum = summed[:tok_dev]
     layer_out = (resid.astype(jnp.float32) + mlp_sum).astype(jnp.bfloat16)
     tail = summed[tok_dev:].reshape(-1)

time: 558 us -> 601 us (1.077)
  local copies, waits for them, and re-layouts: 16.3 us -> 59.6 us
  waiting for transfers between devices: 388 us -> 363 us
  other arithmetic: 34.3 us -> 58.1 us
    unnamed x31 -> x33, local copies, waits for them, and re-layouts: 5.77 us -> 40.2 us
    all_to_all x1, waiting for transfers between devices: 149 us -> 124 us  [per_device(): got = lax.all_to_all(payload, TENSOR, 0, 0, tiled=True)]
    all_to_all x0 -> x2, other arithmetic: none -> 18 us  [per_device(): got = lax.all_to_all(payload, TENSOR, 0, 0, tiled=True)]
    reduce_sum x1, other arithmetic: 5.22 us -> 18.7 us  [per_device(): jnp.sum(got.astype(jnp.float32), axis=0)]
    reshape x1, local copies, waits for them, and re-layouts: 0.25 us -> 8.46 us  [per_device(): down.reshape(tensor_element_count, tok_dev * width)]
    concatenate x1, other arithmetic: 7.6 us -> 0.08 us  [per_device(): jnp.concatenate([by_feature_block(end_down), by_feature_block(end_resid)]...]
where the time goes in v6:
time: 601 us; the launch traced here: 599 us
  waiting for transfers between devices  363 us (60%)
  local copies, waits for them, and re-layouts  59.6 us (10%)
  other arithmetic  58.1 us (10%)
  matrix products  44.1 us (7%)
  starting transfers between devices  34 us (6%)
  blocking collectives  23.9 us (4%)
  between operations  14.5 us (2%)
    all_to_all x1, waiting for transfers between devices, per_device(): got = lax.all_to_all(payload, TENSOR, 0, 0, tiled=True)  124 us
    all_to_all x1, waiting for transfers between devices, scatter_sum(): got = lax.all_to_all(pieces, TENSOR, 0, 0, tiled=True)  113 us
    all_gather x2, waiting for transfers between devices, gather_rows(): return lax.all_gather(rows, ('ty', 'tx'), axis=0, tiled=True)  110 us
    unnamed x33, local copies, waits for them, and re-layouts  40.2 us
    reduce_sum x1, other arithmetic, per_device(): jnp.sum(got.astype(jnp.float32), axis=0)  18.7 us
    all_to_all x2, other arithmetic, per_device(): got = lax.all_to_all(payload, TENSOR, 0, 0, tiled=True)  18 us
    all_gather x2, blocking collectives, gather_rows(): rows = lax.all_gather(rows, 'tz', axis=0, tiled=True)  17.3 us
  transfers between devices with their start and end apart: 8, of which 8 were waited for; matrix products, arithmetic and copies ran while one was open for 3% of the time, Pallas kernels for 0%

profile of v6, /device:TPU:27, one launch (start us, length us, event | category | flops | bytes accessed | tf_op | source)
XLA Modules:
  0.0 599.4 jit_solution(10988245409558427627)
XLA Ops:
  10.2 10.0 %all_gather.15 = bf16[96,2560]{1,0:T(8,128)(2,1)} all-gather(bf16[48,2560]{1,0:T(8,128)(2,1)S(1)} %fusion.41), channel_id=1, replica_groups=mesh['dp'=4,'ty'=4,'tx'=4,'tz'=2] {'tz'}, dimensions={0}, use_global_device_ids=true | all-gather | bytes 737280 | tf_op jit(solution)/shard_map/all_gather | solution.py:32
  23.9 65.5 %all-gather.4.cloned.1.call-done = bf16[1536,2560]{1,0:T(8,128)(2,1)} async-done(((bf16[96,2560]{1,0:T(8,128)(2,1)}), bf16[1536,2560]{1,0:T(8,128)(2,1)}) %all-gather.4.cloned.1.call-update) | async-done | bytes 7864336 | tf_op jit(solution)/shard_map/all_gather | solution.py:33
  89.4 5.9 convolution_convert_fusion.4
  95.2 2.9 collective-permute-start
  98.2 2.7 multiply_reduce_fusion
  104.2 7.4 %collective-permute-done.1 = bf16[1536,128]{0,1:T(8,128)(2,1)S(1)} collective-permute-done((bf16[1536,128]{0,1:T(8,128)(2,1)S(1)}, bf16[1536,128]{0,1:T(8,128)(2,1)S(1)}, u32[]{:S(2)}, u32[]{:S(2)}) %collective-permute-start.1) | collective-permute-done | bytes 393248 | tf_op jit(solution)/shard_map/ppermute | solution.py:22
  113.0 3.1 fusion.60
  118.8 19.7 %while.11 = (s32[]{:T(128)}, bf16[3,1,512,128]{3,2,1,0:T(8,128)(2,1)}, s32[3]{0:T(128)S(1)}, s32[1536]{0:T(1024)S(1)}, bf16[1536,1,128]{0,2,1:T(8,128)(2,1)S(1)}...) while((s32[]{:T(128)}, ...), condition=%wide.region_9.10_spmd.clone, body=%wide.region_6.9_spmd.clone.sunk | while | flops 416939520 | bytes 12107995 | solution.py:174
  126.7 2.1 select_reduce_fusion.4
  138.5 6.3 %convolution_convert_fusion.1 = bf16[1536,2560]{1,0:T(8,128)(2,1)} fusion(bf16[1536,128]{1,0:T(8,128)(2,1)} %bitcast.97, bf16[128,2560]{1,0:T(8,128)(2,1)S(1)} %copy-done.6), kind=kOutput, calls=%fused_computation.28 | convolution fusion | flops 1010565120 | bytes 8912896 | tf_op jit(solution)/shard_map/dot_general | solution.py:177
  144.7 9.3 %all-to-all-start = ((bf16[32,48,2560]{2,1,0:T(8,128)(2,1)}), bf16[32,48,2560]{2,1,0:T(8,128)(2,1)}, u32[]{:S(2)}, u32[]{:S(2)}) async-start(bf16[32,48,2560]{2,1,0:T(8,128)(2,1)} %bitcast.93), calls=%async_computation | async-start | bytes 15728640 | tf_op jit(solution)/shard_map/all_to_all | solution.py:27
  154.3 112.6 %all-to-all-done = bf16[32,48,2560]{2,1,0:T(8,128)(2,1)} async-done(((bf16[32,48,2560]{2,1,0:T(8,128)(2,1)}), bf16[32,48,2560]{2,1,0:T(8,128)(2,1)}, u32[]{:S(2)}, u32[]{:S(2)}) %all-to-all-start) | async-done | bytes 7864352 | tf_op jit(solution)/shard_map/all_to_all | solution.py:27
  266.9 4.5 convert_reduce_fusion.1
  271.8 7.3 %all_gather.17 = bf16[96,2560]{1,0:T(8,128)(2,1)} all-gather(bf16[48,2560]{1,0:T(8,128)(2,1)S(1)} %fusion.45), channel_id=1, replica_groups=mesh['dp'=4,'ty'=4,'tx'=4,'tz'=2] {'tz'}, dimensions={0}, use_global_device_ids=true | all-gather | bytes 737280 | tf_op jit(solution)/shard_map/all_gather | solution.py:32
  282.4 6.7 %all-to-all-start.1 = ((s32[4,1,24]{2,1,0:T(1,128)}), s32[4,1,24]{2,1,0:T(1,128)S(1)}, u32[]{:S(2)}, u32[]{:S(2)}) async-start(s32[4,1,24]{2,1,0:T(1,128)} %bitcast.10), calls=%async_computation.1 | async-start | bytes 4096 | tf_op jit(solution)/shard_map/all_to_all | solution.py:137
  289.1 3.0 all-to-all-done.1
  295.5 4.0 all-to-all-start.2
  299.5 4.5 all-to-all-done.2
  304.4 3.5 scatter_fusion
  308.3 44.2 %all-gather.6.cloned.1.call-done = bf16[1536,2560]{1,0:T(8,128)(2,1)} async-done(((bf16[96,2560]{1,0:T(8,128)(2,1)}), bf16[1536,2560]{1,0:T(8,128)(2,1)}) %all-gather.6.cloned.1.call-update) | async-done | bytes 7864336 | tf_op jit(solution)/shard_map/all_gather | solution.py:33
  352.5 5.6 fusion.76
  358.9 2.7 fusion.27
  362.5 6.5 %convolution_convert_fusion = bf16[1536,2560]{1,0:T(8,128)(2,1)} fusion(bf16[1536,304]{0,1:T(8,128)(2,1)S(1)} %fusion.27, bf16[304,2560]{1,0:T(8,128)(2,1)S(1)} %copy-done), kind=kOutput, calls=%fused_computation.27 | convolution fusion | flops 2394685440 | bytes 10354688 | tf_op jit(solution)/shard_map/dot_general | solution.py:186
  369.3 8.5 %reshape.442 = bf16[32,122880]{1,0:T(8,128)(2,1)} reshape(bf16[1536,2560]{1,0:T(8,128)(2,1)} %convolution_convert_fusion) | data formatting | bytes 15728640 | tf_op jit(solution)/shard_map/reshape | solution.py:205
  377.8 6.8 %maximum_bitcast_fusion = bf16[32,1,125440]{2,0,1:T(8,128)(2,1)} fusion(bf16[32,2560]{1,0:T(8,128)(2,1)S(1)} %fusion.61, bf16[32,122880]{1,0:T(8,128)(2,1)} %reshape.442), kind=kLoop, calls=%fused_computation.29 | loop fusion | flops 16056320 | bytes 16056320 | tf_op jit(solution)/shard_map/all_to_all | solution.py:207
  385.2 11.2 %reduce.11 = bf16[32,125440]{1,0:T(8,128)(2,1)} reduce(bf16[32,1,125440]{2,0,1:T(8,128)(2,1)} %maximum_bitcast_fusion, bf16[]{:T(256)} %broadcast.322), dimensions={1}, to_apply=%copy.53.reduce_sub_computation | reduce | bytes 16056322 | tf_op jit(solution)/shard_map/all_to_all | solution.py:207
  396.3 7.5 %reshape.500 = bf16[32,2,62720]{2,1,0:T(2,128)(2,1)} reshape(bf16[32,125440]{1,0:T(8,128)(2,1)} %reduce.11) | data formatting | bytes 16056320
  403.8 9.2 %all-to-all-start.3 = ((bf16[32,2,62720]{2,1,0:T(2,128)(2,1)}), bf16[32,2,62720]{2,1,0:T(2,128)(2,1)}, u32[]{:S(2)}, u32[]{:S(2)}) async-start(bf16[32,2,62720]{2,1,0:T(2,128)(2,1)} %reshape.500), calls=%async_computation.3 | async-start | bytes 16056320 | tf_op jit(solution)/shard_map/all_to_all | solution.py:207
  414.1 124.3 %all-to-all-done.3 = bf16[32,2,62720]{2,1,0:T(2,128)(2,1)} async-done(((bf16[32,2,62720]{2,1,0:T(2,128)(2,1)}), bf16[32,2,62720]{2,1,0:T(2,128)(2,1)}, u32[]{:S(2)}, u32[]{:S(2)}) %all-to-all-start.3) | async-done | bytes 8028192 | tf_op jit(solution)/shard_map/all_to_all | solution.py:207
  538.4 27.0 %reshape.501 = bf16[32,1,125440]{2,1,0:T(2,128)(2,1)} reshape(bf16[32,2,62720]{2,1,0:T(2,128)(2,1)} %all-to-all-done.3) | data formatting | bytes 16056320
  565.4 18.7 %convert_reduce_fusion = f32[125440]{0:T(1024)S(1)} fusion(bf16[32,1,125440]{2,1,0:T(2,128)(2,1)} %reshape.501), kind=kLoop, calls=%fused_computation.25 | loop fusion | flops 7902720 | bytes 8529920 | tf_op jit(solution)/shard_map/reduce_sum | solution.py:208
  585.1 6.6 %all-gather = bf16[4,6,80]{2,1,0:T(8,128)(2,1)S(1)} all-gather(bf16[1,6,80]{2,1,0:T(8,128)(2,1)S(1)} %reshape.482), channel_id=1, replica_groups=mesh['dp'=4,'ty'=4,'tx'=4,'tz'=2] {'dp'}, dimensions={0}, use_global_device_ids=true | all-gather | bytes 4800 | tf_op jit(solution)/shard_map/all_gather | solution.py:217
  (123 shorter events, 42.8 us)
Async XLA Ops:
  7.2 354.4 %copy-start = (bf16[304,2560]{1,0:T(8,128)(2,1)S(1)}, bf16[304,2560]{1,0:T(8,128)(2,1)}, u32[]{:S(2)}) copy-start(bf16[304,2560]{1,0:T(8,128)(2,1)} %param.29) | copy-start | bytes 4669444
  7.2 82.2 %all-gather.4.cloned.1.call-start = ((), (), s32[]{:S(2)}) async-start(), calls=%async_computation.4 | async-start | bytes 8355840 | tf_op jit(solution)/shard_map/all_gather | solution.py:33
  23.8 74.3 %copy-start.5 = (bf16[2560,128]{1,0:T(8,128)(2,1)S(1)}, bf16[2560,128]{1,0:T(8,128)(2,1)}, u32[]{:S(2)}) copy-start(bf16[2560,128]{1,0:T(8,128)(2,1)} %param.24) | copy-start | bytes 1966084
  89.4 8.8 %copy-start.1 = (bf16[1536,2560]{1,0:T(8,128)(2,1)S(1)}, bf16[1536,2560]{1,0:T(8,128)(2,1)}, u32[]{:S(2)}) copy-start(bf16[1536,2560]{1,0:T(8,128)(2,1)} %all-gather.4.cloned.1.call-done) | copy-start | bytes 23592964
  95.2 7.2 %collective-permute-start = (bf16[1536,64]{0,1:T(8,128)(2,1)S(1)}, bf16[1536,64]{0,1:T(8,128)(2,1)S(1)}, u32[]{:S(2)}, u32[]{:S(2)}) collective-permute-start(bf16[1536,64]{0,1:T(8,128)(2,1)S(1)} %convolution_convert_fusion.4), channel_id=1, source_target_pairs={{0,1},{1,0},{2,3},{3,2},{4,5},{5,4},{6,7},{7,6},{8,9},{9,8},{10,11... | collective-permute-start | bytes 589832 | tf_op jit(solution)/shard_map/ppermute | solution.py:22
  102.5 9.1 %collective-permute-start.1 = (bf16[1536,128]{0,1:T(8,128)(2,1)S(1)}, bf16[1536,128]{0,1:T(8,128)(2,1)S(1)}, u32[]{:S(2)}, u32[]{:S(2)}) collective-permute-start(bf16[1536,128]{0,1:T(8,128)(2,1)S(1)} %maximum_select_fusion.1), channel_id=1, source_target_pairs={{0,2},{1,3},{2,0},{3,1},{4,6},{5,7},{6,4},{7,5},{8,10},{9,11},{10,... | collective-permute-start | bytes 1179656 | tf_op jit(solution)/shard_map/ppermute | solution.py:22
  116.1 0.7 copy-start.3
  118.8 19.7 %copy-start.6 = (bf16[128,2560]{1,0:T(8,128)(2,1)S(1)}, bf16[128,2560]{1,0:T(8,128)(2,1)}, u32[]{:S(2)}) copy-start(bf16[128,2560]{1,0:T(8,128)(2,1)} %param.26) | copy-start | bytes 1966084
  120.1 3.2 copy-start.7
  126.7 3.2 copy-start.7
  133.2 3.2 copy-start.7
  144.7 9.5 %copy-start.8 = (bf16[2560]{0:T(1024)(128)(2,1)S(1)}, bf16[2560]{0:T(1024)(128)(2,1)}, u32[]{:S(2)}) copy-start(bf16[2560]{0:T(1024)(128)(2,1)} %param.23) | copy-start | bytes 15364
  144.7 122.2 %all-to-all-start = ((bf16[32,48,2560]{2,1,0:T(8,128)(2,1)}), bf16[32,48,2560]{2,1,0:T(8,128)(2,1)}, u32[]{:S(2)}, u32[]{:S(2)}) async-start(bf16[32,48,2560]{2,1,0:T(8,128)(2,1)} %bitcast.93), calls=%async_computation | async-start | bytes 15728640 | tf_op jit(solution)/shard_map/all_to_all | solution.py:27
  154.0 198.5 %all-gather.6.cloned.1.call-start = ((), (), s32[]{:S(2)}) async-start(), calls=%async_computation.5 | async-start | bytes 8355840 | tf_op jit(solution)/shard_map/all_gather | solution.py:33
  154.2 117.2 %copy-start.2 = (bf16[48,2560]{1,0:T(8,128)(2,1)S(1)}, bf16[48,2560]{1,0:T(8,128)(2,1)}, u32[]{:S(2)}) copy-start(bf16[48,2560]{1,0:T(8,128)(2,1)} %param.16) | copy-start | bytes 737284
  154.3 124.9 %copy-start.11 = (s32[96]{0:T(128)S(1)}, s32[96]{0:T(128)}, u32[]{:S(2)}) copy-start(s32[96]{0:T(128)} %param.18) | copy-start | bytes 1156
  271.5 22.0 %copy-start.4 = (bf16[1536,64]{0,1:T(8,128)(2,1)S(1)}, bf16[1536,64]{0,1:T(8,128)(2,1)}, u32[]{:S(2)}) copy-start(bf16[1536,64]{0,1:T(8,128)(2,1)} %copy-done.3) | copy-start | bytes 589828
  282.4 9.8 %all-to-all-start.1 = ((s32[4,1,24]{2,1,0:T(1,128)}), s32[4,1,24]{2,1,0:T(1,128)S(1)}, u32[]{:S(2)}, u32[]{:S(2)}) async-start(s32[4,1,24]{2,1,0:T(1,128)} %bitcast.10), calls=%async_computation.1 | async-start | bytes 4096 | tf_op jit(solution)/shard_map/all_to_all | solution.py:137
  295.5 8.5 %all-to-all-start.2 = ((bf16[4,2,12288]{2,1,0:T(2,128)(2,1)}), bf16[4,2,12288]{2,1,0:T(2,128)(2,1)S(1)}, u32[]{:S(2)}, u32[]{:S(2)}) async-start(bf16[4,2,12288]{2,1,0:T(2,128)(2,1)} %reshape.498), calls=%async_computation.2 | async-start | bytes 393216 | tf_op jit(solution)/shard_map/all_to_all | solution.py:136
  352.5 6.0 copy-start.9
  352.5 6.4 %copy-start.10 = (bf16[2560,304]{0,1:T(8,128)(2,1)S(1)}, bf16[2560,304]{0,1:T(8,128)(2,1)}, u32[]{:S(2)}) copy-start(bf16[2560,304]{0,1:T(8,128)(2,1)} %param.28) | copy-start | bytes 4669444
  403.8 134.6 %all-to-all-start.3 = ((bf16[32,2,62720]{2,1,0:T(2,128)(2,1)}), bf16[32,2,62720]{2,1,0:T(2,128)(2,1)}, u32[]{:S(2)}, u32[]{:S(2)}) async-start(bf16[32,2,62720]{2,1,0:T(2,128)(2,1)} %reshape.500), calls=%async_computation.3 | async-start | bytes 16056320 | tf_op jit(solution)/shard_map/all_to_all | solution.py:207
  565.4 26.4 %copy-start.12 = (s32[16]{0:T(128)S(1)}, s32[16]{0:T(128)}, u32[]{:S(2)}) copy-start(s32[16]{0:T(128)} %param.19) | copy-start | bytes 196
Sparse Core Ops, SparseCore 0:
  20.4 68.9 all-gather.3
  279.3 73.1 all-gather.5

commit v7 on v2

--- a/solution.py
+++ b/solution.py
@@ -179,6 +179,7 @@
     )
     resid = (stream.astype(jnp.float32) + attn_sum).astype(jnp.bfloat16)
     portion = gather_rows(row_norm(resid, mlp_gain).astype(jnp.bfloat16))
+    paged_key_value_cache, portion = lax.optimization_barrier((paged_key_value_cache, portion))
     gate_rows = jnp.dot(portion, w_gate, preferred_element_type=jnp.float32)
     upward = jnp.dot(portion, w_up, preferred_element_type=jnp.float32)
     hidden = (jax.nn.silu(gate_rows) * upward).astype(jnp.bfloat16)

time: 546 us -> 541 us (level)
    all_gather x2, waiting for transfers between devices: 129 us -> 110 us  [gather_rows(): return lax.all_gather(rows, ('ty', 'tx'), axis=0, tiled=True)]
    all_to_all x3, waiting for transfers between devices: 232 us -> 240 us  [scatter_sum(): got = lax.all_to_all(pieces, TENSOR, 0, 0, tiled=True)]
  transfers between devices with their start and end apart: 9 -> 9, of which waited for: 7 -> 9; matrix products, arithmetic and copies ran while one was open for 8% -> 3% of each run, Pallas kernels for 0% -> 0%
where the time goes in v7:
time: 541 us; the launch traced here: 537 us
  waiting for transfers between devices  366 us (68%)
  matrix products  46.6 us (9%)
  starting transfers between devices  40.5 us (7%)
  blocking collectives  25.4 us (5%)
  other arithmetic  25.2 us (5%)
  local copies, waits for them, and re-layouts  15.8 us (3%)
  between operations  14.5 us (3%)
    all_to_all x3, waiting for transfers between devices, scatter_sum(): got = lax.all_to_all(pieces, TENSOR, 0, 0, tiled=True)  240 us
    all_gather x2, waiting for transfers between devices, gather_rows(): return lax.all_gather(rows, ('ty', 'tx'), axis=0, tiled=True)  110 us
    all_to_all x3, starting transfers between devices, scatter_sum(): got = lax.all_to_all(pieces, TENSOR, 0, 0, tiled=True)  25 us
    all_gather x2, blocking collectives, gather_rows(): rows = lax.all_gather(rows, 'tz', axis=0, tiled=True)  17.3 us
    dot_general x1, matrix products, per_device(): jnp.dot(hidden, w_down, preferred_element_type=jnp.float32)  13.4 us
  transfers between devices with their start and end apart: 9, of which 9 were waited for; matrix products, arithmetic and copies ran while one was open for 3% of the time, Pallas kernels for 0%

profile of v7, /device:TPU:27, one launch (start us, length us, event | category | flops | bytes accessed | tf_op | source)
XLA Modules:
  0.0 536.6 jit_solution(8192135752190453658)
XLA Ops:
  10.2 10.0 %all_gather.15 = bf16[96,2560]{1,0:T(8,128)(2,1)} all-gather(bf16[48,2560]{1,0:T(8,128)(2,1)S(1)} %fusion.41), channel_id=1, replica_groups=mesh['dp'=4,'ty'=4,'tx'=4,'tz'=2] {'tz'}, dimensions={0}, use_global_device_ids=true | all-gather | bytes 737280 | tf_op jit(solution)/shard_map/all_gather | solution.py:32
  23.9 65.5 %all-gather.4.cloned.1.call-done = bf16[1536,2560]{1,0:T(8,128)(2,1)} async-done(((bf16[96,2560]{1,0:T(8,128)(2,1)}), bf16[1536,2560]{1,0:T(8,128)(2,1)}) %all-gather.4.cloned.1.call-update) | async-done | bytes 7864336 | tf_op jit(solution)/shard_map/all_gather | solution.py:33
  89.4 5.9 %convolution_convert_fusion.3 = bf16[1536,64]{0,1:T(8,128)(2,1)S(1)} fusion(bf16[1536,2560]{1,0:T(8,128)(2,1)} %all-gather.4.cloned.1.call-done, bf16[2560,64]{0,1:T(8,128)(2,1)} %param.25), kind=kOutput, calls=%fused_computation.32 | convolution fusion | flops 503414784 | bytes 8388608 | tf_op jit(solution)/shard_map/dot_general | solution.py:94
  95.2 2.9 collective-permute-start
  98.2 2.7 multiply_reduce_fusion
  100.9 1.5 collective-permute-done
  102.5 1.6 collective-permute-start.1
  104.2 7.4 %collective-permute-done.1 = bf16[1536,128]{0,1:T(8,128)(2,1)S(1)} collective-permute-done((bf16[1536,128]{0,1:T(8,128)(2,1)S(1)}, bf16[1536,128]{0,1:T(8,128)(2,1)S(1)}, u32[]{:S(2)}, u32[]{:S(2)}) %collective-permute-start.1) | collective-permute-done | bytes 393248 | tf_op jit(solution)/shard_map/ppermute | solution.py:22
  113.0 3.1 fusion.48
  118.9 18.1 %while.11 = (s32[]{:T(128)}, bf16[3,1,512,128]{3,2,1,0:T(8,128)(2,1)S(1)}, s32[3]{0:T(128)S(1)}, s32[1536]{0:T(1024)S(1)}, bf16[1536,1,128]{0,2,1:T(8,128)(2,1)S...) while((s32[]{:T(128)}, ...), condition=%wide.region_9.10_spmd.clone, body=%wide.region_6.9_spmd.clone.sunk | while | flops 416939520 | bytes 12110043 | solution.py:174
  120.3 2.1 select_reduce_fusion.4
  126.3 2.1 select_reduce_fusion.4
  132.3 2.1 select_reduce_fusion.4
  137.0 5.3 convolution_convert_fusion.1
  142.4 9.2 %all-to-all-start = ((bf16[32,48,2560]{2,1,0:T(8,128)(2,1)}), bf16[32,48,2560]{2,1,0:T(8,128)(2,1)}, u32[]{:S(2)}, u32[]{:S(2)}) async-start(bf16[32,48,2560]{2,1,0:T(8,128)(2,1)} %bitcast.89), calls=%async_computation | async-start | bytes 15728640 | tf_op jit(solution)/shard_map/all_to_all | solution.py:27
  151.9 112.6 %all-to-all-done = bf16[32,48,2560]{2,1,0:T(8,128)(2,1)} async-done(((bf16[32,48,2560]{2,1,0:T(8,128)(2,1)}), bf16[32,48,2560]{2,1,0:T(8,128)(2,1)}, u32[]{:S(2)}, u32[]{:S(2)}) %all-to-all-start) | async-done | bytes 7864352 | tf_op jit(solution)/shard_map/all_to_all | solution.py:27
  264.5 4.5 convert_reduce_fusion.1
  269.4 7.3 %all_gather.17 = bf16[96,2560]{1,0:T(8,128)(2,1)} all-gather(bf16[48,2560]{1,0:T(8,128)(2,1)S(1)} %fusion.45), channel_id=1, replica_groups=mesh['dp'=4,'ty'=4,'tx'=4,'tz'=2] {'tz'}, dimensions={0}, use_global_device_ids=true | all-gather | bytes 737280 | tf_op jit(solution)/shard_map/all_gather | solution.py:32
  280.0 6.7 %all-to-all-start.1 = ((s32[4,1,24]{2,1,0:T(1,128)}), s32[4,1,24]{2,1,0:T(1,128)S(1)}, u32[]{:S(2)}, u32[]{:S(2)}) async-start(s32[4,1,24]{2,1,0:T(1,128)} %bitcast.10), calls=%async_computation.1 | async-start | bytes 4096 | tf_op jit(solution)/shard_map/all_to_all | solution.py:137
  286.8 3.0 all-to-all-done.1
  293.1 4.0 all-to-all-start.2
  297.1 4.5 all-to-all-done.2
  302.0 3.5 scatter_fusion
  305.4 44.7 %all-gather.6.cloned.1.call-done = bf16[1536,2560]{1,0:T(8,128)(2,1)} async-done(((bf16[96,2560]{1,0:T(8,128)(2,1)}), bf16[1536,2560]{1,0:T(8,128)(2,1)}) %all-gather.6.cloned.1.call-update) | async-done | bytes 7864336 | tf_op jit(solution)/shard_map/all_gather | solution.py:33
  350.2 7.5 %fusion.71 = f32[1536,304]{0,1:T(8,128)} fusion(bf16[1536,2560]{1,0:T(8,128)(2,1)} %all-gather.6.cloned.1.call-done, bf16[2560,304]{0,1:T(8,128)(2,1)} %param.27), kind=kOutput, calls=%fused_computation.119 | convolution fusion | flops 2390753280 | bytes 11288576 | tf_op jit(solution)/shard_map/dot_general | solution.py:183
  357.6 13.4 %convolution_convert_fusion = bf16[1536,2560]{1,0:T(8,128)(2,1)} fusion(bf16[304,2560]{1,0:T(8,128)(2,1)S(1)} %copy-done, bf16[1536,2560]{1,0:T(8,128)(2,1)} %all-gather.6.cloned.1.call-done, bf16[2560,304]{0,1:T(8,128)(2,1)} %param.28, f32[1536,304]{0,1:T(8,128)} %fusion.71), kind=kOutput, calls=%fused_computation.27 | convolution fusion | flops 4788240384 | bytes 20709376 | tf_op jit(solution)/shard_map/dot_general | solution.py:187
  371.0 9.2 %all-to-all-start.3 = ((bf16[32,48,2560]{2,1,0:T(8,128)(2,1)}), bf16[32,48,2560]{2,1,0:T(8,128)(2,1)}, u32[]{:S(2)}, u32[]{:S(2)}) async-start(bf16[32,48,2560]{2,1,0:T(8,128)(2,1)} %bitcast.90), calls=%async_computation.3 | async-start | bytes 15728640 | tf_op jit(solution)/shard_map/all_to_all | solution.py:27
  380.3 122.1 %all-to-all-done.3 = bf16[32,48,2560]{2,1,0:T(8,128)(2,1)} async-done(((bf16[32,48,2560]{2,1,0:T(8,128)(2,1)}), bf16[32,48,2560]{2,1,0:T(8,128)(2,1)}, u32[]{:S(2)}, u32[]{:S(2)}) %all-to-all-start.3) | async-done | bytes 7864352 | tf_op jit(solution)/shard_map/all_to_all | solution.py:27
  502.4 4.5 convert_reduce_fusion
  508.1 6.5 %all-to-all-start.4 = ((bf16[32,2,240]{2,1,0:T(2,128)(2,1)}), bf16[32,2,240]{2,1,0:T(2,128)(2,1)S(1)}, u32[]{:S(2)}, u32[]{:S(2)}) async-start(bf16[32,2,240]{2,1,0:T(2,128)(2,1)} %reshape.456), calls=%async_computation.4 | async-start | bytes 65536 | tf_op jit(solution)/shard_map/all_to_all | solution.py:27
  515.7 5.1 all-to-all-done.4
  520.9 8.0 %all-gather = bf16[4,6,80]{2,1,0:T(8,128)(2,1)S(1)} all-gather(bf16[1,6,80]{2,1,0:T(8,128)(2,1)S(1)} %bitcast.96), channel_id=1, replica_groups=mesh['dp'=4,'ty'=4,'tx'=4,'tz'=2] {'dp'}, dimensions={0}, use_global_device_ids=true | all-gather | bytes 4800 | tf_op jit(solution)/shard_map/all_gather | solution.py:200
  (115 shorter events, 31.1 us)
Async XLA Ops:
  7.2 350.5 %copy-start = (bf16[304,2560]{1,0:T(8,128)(2,1)S(1)}, bf16[304,2560]{1,0:T(8,128)(2,1)}, u32[]{:S(2)}) copy-start(bf16[304,2560]{1,0:T(8,128)(2,1)} %param.29) | copy-start | bytes 4669444
  7.2 82.2 %all-gather.4.cloned.1.call-start = ((), (), s32[]{:S(2)}) async-start(), calls=%async_computation.5 | async-start | bytes 8355840 | tf_op jit(solution)/shard_map/all_gather | solution.py:33
  23.8 74.3 %copy-start.9 = (bf16[2560,128]{1,0:T(8,128)(2,1)S(1)}, bf16[2560,128]{1,0:T(8,128)(2,1)}, u32[]{:S(2)}) copy-start(bf16[2560,128]{1,0:T(8,128)(2,1)} %param.24) | copy-start | bytes 1966084
  89.4 8.8 %copy-start.1 = (bf16[1536,2560]{1,0:T(8,128)(2,1)S(1)}, bf16[1536,2560]{1,0:T(8,128)(2,1)}, u32[]{:S(2)}) copy-start(bf16[1536,2560]{1,0:T(8,128)(2,1)} %all-gather.4.cloned.1.call-done) | copy-start | bytes 23592964
  95.2 7.2 %collective-permute-start = (bf16[1536,64]{0,1:T(8,128)(2,1)S(1)}, bf16[1536,64]{0,1:T(8,128)(2,1)S(1)}, u32[]{:S(2)}, u32[]{:S(2)}) collective-permute-start(bf16[1536,64]{0,1:T(8,128)(2,1)S(1)} %convolution_convert_fusion.3), channel_id=1, source_target_pairs={{0,1},{1,0},{2,3},{3,2},{4,5},{5,4},{6,7},{7,6},{8,9},{9,8},{10,11... | collective-permute-start | bytes 589832 | tf_op jit(solution)/shard_map/ppermute | solution.py:22
  102.5 9.1 %collective-permute-start.1 = (bf16[1536,128]{0,1:T(8,128)(2,1)S(1)}, bf16[1536,128]{0,1:T(8,128)(2,1)S(1)}, u32[]{:S(2)}, u32[]{:S(2)}) collective-permute-start(bf16[1536,128]{0,1:T(8,128)(2,1)S(1)} %maximum_select_fusion.1), channel_id=1, source_target_pairs={{0,2},{1,3},{2,0},{3,1},{4,6},{5,7},{6,4},{7,5},{8,10},{9,11},{10,... | collective-permute-start | bytes 1179656 | tf_op jit(solution)/shard_map/ppermute | solution.py:22
  113.0 5.9 %copy-start.8 = (bf16[3,1,512,128]{3,2,1,0:T(8,128)(2,1)S(1)}, bf16[3,1,512,128]{3,2,1,0:T(8,128)(2,1)}, u32[]{:S(2)}) copy-start(bf16[3,1,512,128]{3,2,1,0:T(8,128)(2,1)} %custom-call.4) | copy-start | bytes 1179652
  116.1 0.7 copy-start.3
  116.1 0.8 copy-start.5
  118.9 18.1 %copy-start.10 = (bf16[128,2560]{1,0:T(8,128)(2,1)S(1)}, bf16[128,2560]{1,0:T(8,128)(2,1)}, u32[]{:S(2)}) copy-start(bf16[128,2560]{1,0:T(8,128)(2,1)} %param.26) | copy-start | bytes 1966084
  120.3 3.2 copy-start.11
  126.3 3.2 copy-start.11
  132.3 3.2 copy-start.11
  142.4 9.5 %copy-start.12 = (bf16[2560]{0:T(1024)(128)(2,1)S(1)}, bf16[2560]{0:T(1024)(128)(2,1)}, u32[]{:S(2)}) copy-start(bf16[2560]{0:T(1024)(128)(2,1)} %param.23) | copy-start | bytes 15364
  142.4 122.2 %all-to-all-start = ((bf16[32,48,2560]{2,1,0:T(8,128)(2,1)}), bf16[32,48,2560]{2,1,0:T(8,128)(2,1)}, u32[]{:S(2)}, u32[]{:S(2)}) async-start(bf16[32,48,2560]{2,1,0:T(8,128)(2,1)} %bitcast.89), calls=%async_computation | async-start | bytes 15728640 | tf_op jit(solution)/shard_map/all_to_all | solution.py:27
  151.6 198.5 %all-gather.6.cloned.1.call-start = ((), (), s32[]{:S(2)}) async-start(), calls=%async_computation.6 | async-start | bytes 8355840 | tf_op jit(solution)/shard_map/all_gather | solution.py:33
  151.9 117.2 %copy-start.2 = (bf16[48,2560]{1,0:T(8,128)(2,1)S(1)}, bf16[48,2560]{1,0:T(8,128)(2,1)}, u32[]{:S(2)}) copy-start(bf16[48,2560]{1,0:T(8,128)(2,1)} %param.16) | copy-start | bytes 737284
  151.9 124.9 %copy-start.13 = (s32[96]{0:T(128)S(1)}, s32[96]{0:T(128)}, u32[]{:S(2)}) copy-start(s32[96]{0:T(128)} %param.18) | copy-start | bytes 1156
  269.1 22.0 %copy-start.4 = (bf16[1536,64]{0,1:T(8,128)(2,1)S(1)}, bf16[1536,64]{0,1:T(8,128)(2,1)}, u32[]{:S(2)}) copy-start(bf16[1536,64]{0,1:T(8,128)(2,1)} %copy-done.3) | copy-start | bytes 589828
  269.1 22.0 %copy-start.6 = (bf16[1536,64]{0,1:T(8,128)(2,1)S(1)}, bf16[1536,64]{0,1:T(8,128)(2,1)}, u32[]{:S(2)}) copy-start(bf16[1536,64]{0,1:T(8,128)(2,1)} %copy-done.5) | copy-start | bytes 589828
  280.0 9.8 %all-to-all-start.1 = ((s32[4,1,24]{2,1,0:T(1,128)}), s32[4,1,24]{2,1,0:T(1,128)S(1)}, u32[]{:S(2)}, u32[]{:S(2)}) async-start(s32[4,1,24]{2,1,0:T(1,128)} %bitcast.10), calls=%async_computation.1 | async-start | bytes 4096 | tf_op jit(solution)/shard_map/all_to_all | solution.py:137
  293.1 8.5 %all-to-all-start.2 = ((bf16[4,2,12288]{2,1,0:T(2,128)(2,1)}), bf16[4,2,12288]{2,1,0:T(2,128)(2,1)S(1)}, u32[]{:S(2)}, u32[]{:S(2)}) async-start(bf16[4,2,12288]{2,1,0:T(2,128)(2,1)} %reshape.454), calls=%async_computation.2 | async-start | bytes 393216 | tf_op jit(solution)/shard_map/all_to_all | solution.py:136
  371.0 131.4 %all-to-all-start.3 = ((bf16[32,48,2560]{2,1,0:T(8,128)(2,1)}), bf16[32,48,2560]{2,1,0:T(8,128)(2,1)}, u32[]{:S(2)}, u32[]{:S(2)}) async-start(bf16[32,48,2560]{2,1,0:T(8,128)(2,1)} %bitcast.90), calls=%async_computation.3 | async-start | bytes 15728640 | tf_op jit(solution)/shard_map/all_to_all | solution.py:27
  380.3 148.7 %copy-start.14 = (s32[16]{0:T(128)S(1)}, s32[16]{0:T(128)}, u32[]{:S(2)}) copy-start(s32[16]{0:T(128)} %param.19) | copy-start | bytes 196
  507.0 22.7 %copy-start.7 = (bf16[48,2560]{1,0:T(8,128)(2,1)}, bf16[48,2560]{1,0:T(8,128)(2,1)S(1)}, u32[]{:S(2)}) copy-start(bf16[48,2560]{1,0:T(8,128)(2,1)S(1)} %fusion.46) | copy-start | bytes 737284
  508.1 12.6 %all-to-all-start.4 = ((bf16[32,2,240]{2,1,0:T(2,128)(2,1)}), bf16[32,2,240]{2,1,0:T(2,128)(2,1)S(1)}, u32[]{:S(2)}, u32[]{:S(2)}) async-start(bf16[32,2,240]{2,1,0:T(2,128)(2,1)} %reshape.456), calls=%async_computation.4 | async-start | bytes 65536 | tf_op jit(solution)/shard_map/all_to_all | solution.py:27
Sparse Core Ops, SparseCore 0:
  20.4 68.9 all-gather.3
  276.9 73.2 all-gather.5

commit v8 on v7

--- a/solution.py
+++ b/solution.py
@@ -88,24 +88,25 @@
     query_cols = heads_dev * HEAD_SIZE
     prompt, position, prompt_starts, prompt_ends = prompt_layout(lengths[0], token_count)
     portion = gather_rows(row_norm(stream, attn_gain).astype(jnp.bfloat16))
+    key_value_group = tensor_element_count // KEY_VALUE_HEADS
+    head_weight = key_value_weight
+    for bit_id in range(key_value_group.bit_length() - 1):
+        partner = partner_2(head_weight, TENSOR, bit_id)
+        upper_half = my_index // 2**bit_id % 2
+        head_weight = jnp.where(
+            upper_half == 1,
+            jnp.concatenate([partner, head_weight], axis=1),
+            jnp.concatenate([head_weight, partner], axis=1),
+        )
     joined = jnp.concatenate(
         [
             jnp.dot(portion, w_query, preferred_element_type=jnp.float32),
-            jnp.dot(portion, key_value_weight, preferred_element_type=jnp.float32),
+            jnp.dot(portion, head_weight, preferred_element_type=jnp.float32),
         ],
         axis=1,
     )
     queries = joined[:, :query_cols].reshape(token_count, heads_dev, HEAD_SIZE)
     kv_part = joined[:, query_cols:].astype(jnp.bfloat16)
-    key_value_group = tensor_element_count // KEY_VALUE_HEADS
-    for bit_id in range(key_value_group.bit_length() - 1):
-        partner = partner_2(kv_part, TENSOR, bit_id)
-        upper_half = my_index // 2**bit_id % 2
-        kv_part = jnp.where(
-            upper_half == 1,
-            jnp.concatenate([partner, kv_part], axis=1),
-            jnp.concatenate([kv_part, partner], axis=1),
-        )
     key_flat = rotate(row_norm(kv_part[:, None, :HEAD_SIZE], key_gain), position).astype(
         jnp.bfloat16
     )[:, 0, :]

time: 541 us -> 537 us (level)
    all_gather x2, waiting for transfers between devices: 110 us -> 79.1 us  [gather_rows(): return lax.all_gather(rows, ('ty', 'tx'), axis=0, tiled=True)]
    ppermute x2, waiting for transfers between devices: 8.92 us -> 26.4 us  [partner_2(): return lax.ppermute(value, axis, pairs)]
    all_to_all x3, waiting for transfers between devices: 240 us -> 248 us  [scatter_sum(): got = lax.all_to_all(pieces, TENSOR, 0, 0, tiled=True)]
where the time goes in v8:
time: 537 us; the launch traced here: 532 us
  waiting for transfers between devices  361 us (67%)
  matrix products  47.8 us (9%)
  starting transfers between devices  38.4 us (7%)
  other arithmetic  26.9 us (5%)
  blocking collectives  26.2 us (5%)
  local copies, waits for them, and re-layouts  15 us (3%)
  between operations  14.5 us (3%)
    all_to_all x3, waiting for transfers between devices, scatter_sum(): got = lax.all_to_all(pieces, TENSOR, 0, 0, tiled=True)  248 us
    all_gather x2, waiting for transfers between devices, gather_rows(): return lax.all_gather(rows, ('ty', 'tx'), axis=0, tiled=True)  79.1 us
    ppermute x2, waiting for transfers between devices, partner_2(): return lax.ppermute(value, axis, pairs)  26.4 us
    all_to_all x3, starting transfers between devices, scatter_sum(): got = lax.all_to_all(pieces, TENSOR, 0, 0, tiled=True)  25.3 us
    all_gather x2, blocking collectives, gather_rows(): rows = lax.all_gather(rows, 'tz', axis=0, tiled=True)  18.2 us
    dot_general x1, matrix products, per_device(): jnp.dot(hidden, w_down, preferred_element_type=jnp.float32)  13.4 us
  transfers between devices with their start and end apart: 9, of which 9 were waited for; matrix products, arithmetic and copies ran while one was open for 3% of the time, Pallas kernels for 0%

profile of v8, /device:TPU:27, one launch (start us, length us, event | category | flops | bytes accessed | tf_op | source)
XLA Modules:
  0.0 532.2 jit_solution(14077269350634117763)
XLA Ops:
  10.2 10.0 %all_gather.15 = bf16[96,2560]{1,0:T(8,128)(2,1)} all-gather(bf16[48,2560]{1,0:T(8,128)(2,1)S(1)} %fusion.47), channel_id=1, replica_groups=mesh['dp'=4,'ty'=4,'tx'=4,'tz'=2] {'tz'}, dimensions={0}, use_global_device_ids=true | all-gather | bytes 737280 | tf_op jit(solution)/shard_map/all_gather | solution.py:32
  20.3 2.8 collective-permute-start
  26.3 3.8 collective-permute-done
  32.3 22.6 %collective-permute-done.1 = bf16[2560,128]{0,1:T(8,128)(2,1)} collective-permute-done((bf16[2560,128]{0,1:T(8,128)(2,1)S(1)}, bf16[2560,128]{0,1:T(8,128)(2,1)}, u32[]{:S(2)}, u32[]{:S(2)}) %collective-permute-start.1) | collective-permute-done | bytes 655392 | tf_op jit(solution)/shard_map/ppermute | solution.py:22
  54.9 39.2 %all-gather.4.cloned.1.call-done = bf16[1536,2560]{1,0:T(8,128)(2,1)} async-done(((bf16[96,2560]{1,0:T(8,128)(2,1)}), bf16[1536,2560]{1,0:T(8,128)(2,1)}) %all-gather.4.cloned.1.call-update) | async-done | bytes 7864336 | tf_op jit(solution)/shard_map/all_gather | solution.py:33
  94.1 5.9 %convolution_convert_fusion.3 = bf16[1536,256]{0,1:T(8,128)(2,1)S(1)} fusion(bf16[1536,2560]{1,0:T(8,128)(2,1)} %all-gather.4.cloned.1.call-done, bf16[2560,128]{0,1:T(8,128)(2,1)S(1)} %maximum_select_fusion.2, bf16[2560,128]{0,1:T(8,128)(2,1)} %collective-permute-done.1, pred[]{:T(512)S(6)} %eq.71), kind=kOutput, calls=%fused_computation.32 | convolution fusion | flops 2019557376 | bytes 9961473 | tf_op jit(solution)/shard_map/dot_general | solution.py:104
  100.2 3.8 multiply_reduce_fusion
  106.6 2.4 fusion.54
  110.7 18.2 %while.11 = (s32[]{:T(128)}, bf16[3,1,512,128]{3,2,1,0:T(8,128)(2,1)S(1)}, s32[3]{0:T(128)S(1)}, s32[1536]{0:T(1024)S(1)}, bf16[1536,1,128]{0,2,1:T(8,128)(2,1)}...) while((s32[]{:T(128)}, ...), condition=%wide.region_9.10_spmd.clone, body=%wide.region_6.9_spmd.clone.sunk | while | flops 416939520 | bytes 12107995 | solution.py:175
  112.0 2.2 select_reduce_fusion.4
  118.1 2.2 select_reduce_fusion.4
  124.2 2.2 select_reduce_fusion.4
  127.5 1.5 fusion.102
  129.0 5.3 %convolution_convert_fusion.1 = bf16[1536,2560]{1,0:T(8,128)(2,1)} fusion(bf16[1536,128]{1,0:T(8,128)(2,1)S(1)} %bitcast.93, bf16[128,2560]{1,0:T(8,128)(2,1)S(1)} %copy-done.5), kind=kOutput, calls=%fused_computation.28 | convolution fusion | flops 1010565120 | bytes 8912896 | tf_op jit(solution)/shard_map/dot_general | solution.py:178
  134.3 9.3 %all-to-all-start = ((bf16[32,48,2560]{2,1,0:T(8,128)(2,1)}), bf16[32,48,2560]{2,1,0:T(8,128)(2,1)}, u32[]{:S(2)}, u32[]{:S(2)}) async-start(bf16[32,48,2560]{2,1,0:T(8,128)(2,1)} %bitcast.88), calls=%async_computation | async-start | bytes 15728640 | tf_op jit(solution)/shard_map/all_to_all | solution.py:27
  143.9 121.5 %all-to-all-done = bf16[32,48,2560]{2,1,0:T(8,128)(2,1)} async-done(((bf16[32,48,2560]{2,1,0:T(8,128)(2,1)}), bf16[32,48,2560]{2,1,0:T(8,128)(2,1)}, u32[]{:S(2)}, u32[]{:S(2)}) %all-to-all-start) | async-done | bytes 7864352 | tf_op jit(solution)/shard_map/all_to_all | solution.py:27
  265.4 4.5 convert_reduce_fusion.1
  270.3 8.2 %all_gather.17 = bf16[96,2560]{1,0:T(8,128)(2,1)} all-gather(bf16[48,2560]{1,0:T(8,128)(2,1)S(1)} %fusion.51), channel_id=1, replica_groups=mesh['dp'=4,'ty'=4,'tx'=4,'tz'=2] {'tz'}, dimensions={0}, use_global_device_ids=true | all-gather | bytes 737280 | tf_op jit(solution)/shard_map/all_gather | solution.py:32
  281.8 5.6 %all-to-all-start.1 = ((s32[4,1,24]{2,1,0:T(1,128)}), s32[4,1,24]{2,1,0:T(1,128)S(1)}, u32[]{:S(2)}, u32[]{:S(2)}) async-start(s32[4,1,24]{2,1,0:T(1,128)} %bitcast.10), calls=%async_computation.1 | async-start | bytes 4096 | tf_op jit(solution)/shard_map/all_to_all | solution.py:138
  287.4 3.0 all-to-all-done.1
  293.7 4.0 all-to-all-start.2
  297.8 4.5 all-to-all-done.2
  302.6 3.5 scatter_fusion
  306.1 39.9 %all-gather.6.cloned.1.call-done = bf16[1536,2560]{1,0:T(8,128)(2,1)} async-done(((bf16[96,2560]{1,0:T(8,128)(2,1)}), bf16[1536,2560]{1,0:T(8,128)(2,1)}) %all-gather.6.cloned.1.call-update) | async-done | bytes 7864336 | tf_op jit(solution)/shard_map/all_gather | solution.py:33
  346.0 7.5 %fusion.78 = f32[1536,304]{0,1:T(8,128)} fusion(bf16[1536,2560]{1,0:T(8,128)(2,1)} %all-gather.6.cloned.1.call-done, bf16[2560,304]{0,1:T(8,128)(2,1)} %param.27), kind=kOutput, calls=%fused_computation.126 | convolution fusion | flops 2390753280 | bytes 11288576 | tf_op jit(solution)/shard_map/dot_general | solution.py:184
  353.4 13.4 %convolution_convert_fusion = bf16[1536,2560]{1,0:T(8,128)(2,1)} fusion(bf16[304,2560]{1,0:T(8,128)(2,1)S(1)} %copy-done, bf16[1536,2560]{1,0:T(8,128)(2,1)} %all-gather.6.cloned.1.call-done, bf16[2560,304]{0,1:T(8,128)(2,1)} %param.28, f32[1536,304]{0,1:T(8,128)} %fusion.78), kind=kOutput, calls=%fused_computation.27 | convolution fusion | flops 4788240384 | bytes 20709376 | tf_op jit(solution)/shard_map/dot_general | solution.py:188
  366.8 9.3 %all-to-all-start.3 = ((bf16[32,48,2560]{2,1,0:T(8,128)(2,1)}), bf16[32,48,2560]{2,1,0:T(8,128)(2,1)}, u32[]{:S(2)}, u32[]{:S(2)}) async-start(bf16[32,48,2560]{2,1,0:T(8,128)(2,1)} %bitcast.89), calls=%async_computation.3 | async-start | bytes 15728640 | tf_op jit(solution)/shard_map/all_to_all | solution.py:27
  376.2 121.7 %all-to-all-done.3 = bf16[32,48,2560]{2,1,0:T(8,128)(2,1)} async-done(((bf16[32,48,2560]{2,1,0:T(8,128)(2,1)}), bf16[32,48,2560]{2,1,0:T(8,128)(2,1)}, u32[]{:S(2)}, u32[]{:S(2)}) %all-to-all-start.3) | async-done | bytes 7864352 | tf_op jit(solution)/shard_map/all_to_all | solution.py:27
  497.9 4.5 convert_reduce_fusion
  503.6 6.7 %all-to-all-start.4 = ((bf16[32,2,240]{2,1,0:T(2,128)(2,1)}), bf16[32,2,240]{2,1,0:T(2,128)(2,1)S(1)}, u32[]{:S(2)}, u32[]{:S(2)}) async-start(bf16[32,2,240]{2,1,0:T(2,128)(2,1)} %reshape.456), calls=%async_computation.4 | async-start | bytes 65536 | tf_op jit(solution)/shard_map/all_to_all | solution.py:27
  511.3 5.0 all-to-all-done.4
  516.5 8.0 %all-gather = bf16[4,6,80]{2,1,0:T(8,128)(2,1)S(1)} all-gather(bf16[1,6,80]{2,1,0:T(8,128)(2,1)S(1)} %bitcast.95), channel_id=1, replica_groups=mesh['dp'=4,'ty'=4,'tx'=4,'tz'=2] {'dp'}, dimensions={0}, use_global_device_ids=true | all-gather | bytes 4800 | tf_op jit(solution)/shard_map/all_gather | solution.py:201
  (110 shorter events, 31.6 us)
Async XLA Ops:
  7.2 346.3 %copy-start = (bf16[304,2560]{1,0:T(8,128)(2,1)S(1)}, bf16[304,2560]{1,0:T(8,128)(2,1)}, u32[]{:S(2)}) copy-start(bf16[304,2560]{1,0:T(8,128)(2,1)} %param.29) | copy-start | bytes 4669444
  7.2 25.0 %copy-start.10 = (s32[1,6]{1,0:T(1,128)S(1)}, s32[1,6]{1,0:T(1,128)}, u32[]{:S(2)}) copy-start(s32[1,6]{1,0:T(1,128)} %param.17) | copy-start | bytes 76
  7.2 86.9 %all-gather.4.cloned.1.call-start = ((), (), s32[]{:S(2)}) async-start(), calls=%async_computation.5 | async-start | bytes 8355840 | tf_op jit(solution)/shard_map/all_gather | solution.py:33
  20.3 9.8 %collective-permute-start = (bf16[2560,64]{0,1:T(8,128)(2,1)}, bf16[2560,64]{0,1:T(8,128)(2,1)S(1)}, u32[]{:S(2)}, u32[]{:S(2)}) collective-permute-start(bf16[2560,64]{0,1:T(8,128)(2,1)} %param.25), channel_id=1, source_target_pairs={{0,1},{1,0},{2,3},{3,2},{4,5},{5,4},{6,7},{7,6},{8,9},{9,8},{10,11... | collective-permute-start | bytes 983048 | tf_op jit(solution)/shard_map/ppermute | solution.py:22
  23.9 76.2 %copy-start.8 = (s32[6,1]{0,1:T(1,128)}, s32[6,1]{0,1:T(1,128)S(1)}, u32[]{:S(2)}) copy-start(s32[6,1]{0,1:T(1,128)S(1)} %reduce-window.4) | copy-start | bytes 76
  31.3 23.6 %collective-permute-start.1 = (bf16[2560,128]{0,1:T(8,128)(2,1)S(1)}, bf16[2560,128]{0,1:T(8,128)(2,1)}, u32[]{:S(2)}, u32[]{:S(2)}) collective-permute-start(bf16[2560,128]{0,1:T(8,128)(2,1)S(1)} %maximum_select_fusion.2), channel_id=1, source_target_pairs={{0,2},{1,3},{2,0},{3,1},{4,6},{5,7},{6,4},{7,5},{8,10},{9,11},{10,... | collective-permute-start | bytes 1966088 | tf_op jit(solution)/shard_map/ppermute | solution.py:22
  94.1 6.0 %copy-start.1 = (bf16[1536,2560]{1,0:T(8,128)(2,1)S(1)}, bf16[1536,2560]{1,0:T(8,128)(2,1)}, u32[]{:S(2)}) copy-start(bf16[1536,2560]{1,0:T(8,128)(2,1)} %all-gather.4.cloned.1.call-done) | copy-start | bytes 23592964
  105.7 5.0 copy-start.4
  110.7 18.2 %copy-start.5 = (bf16[128,2560]{1,0:T(8,128)(2,1)S(1)}, bf16[128,2560]{1,0:T(8,128)(2,1)}, u32[]{:S(2)}) copy-start(bf16[128,2560]{1,0:T(8,128)(2,1)} %param.26) | copy-start | bytes 1966084
  112.0 3.2 copy-start.6
  118.1 3.2 copy-start.6
  124.2 3.2 copy-start.6
  134.3 9.6 %copy-start.7 = (bf16[2560]{0:T(1024)(128)(2,1)S(1)}, bf16[2560]{0:T(1024)(128)(2,1)}, u32[]{:S(2)}) copy-start(bf16[2560]{0:T(1024)(128)(2,1)} %param.23) | copy-start | bytes 15364
  134.3 131.1 %all-to-all-start = ((bf16[32,48,2560]{2,1,0:T(8,128)(2,1)}), bf16[32,48,2560]{2,1,0:T(8,128)(2,1)}, u32[]{:S(2)}, u32[]{:S(2)}) async-start(bf16[32,48,2560]{2,1,0:T(8,128)(2,1)} %bitcast.88), calls=%async_computation | async-start | bytes 15728640 | tf_op jit(solution)/shard_map/all_to_all | solution.py:27
  143.7 202.3 %all-gather.6.cloned.1.call-start = ((), (), s32[]{:S(2)}) async-start(), calls=%async_computation.6 | async-start | bytes 8355840 | tf_op jit(solution)/shard_map/all_gather | solution.py:33
  143.9 126.1 %copy-start.2 = (bf16[48,2560]{1,0:T(8,128)(2,1)S(1)}, bf16[48,2560]{1,0:T(8,128)(2,1)}, u32[]{:S(2)}) copy-start(bf16[48,2560]{1,0:T(8,128)(2,1)} %param.16) | copy-start | bytes 737284
  143.9 134.6 %copy-start.11 = (s32[96]{0:T(128)S(1)}, s32[96]{0:T(128)}, u32[]{:S(2)}) copy-start(s32[96]{0:T(128)} %param.18) | copy-start | bytes 1156
  281.8 8.7 %all-to-all-start.1 = ((s32[4,1,24]{2,1,0:T(1,128)}), s32[4,1,24]{2,1,0:T(1,128)S(1)}, u32[]{:S(2)}, u32[]{:S(2)}) async-start(s32[4,1,24]{2,1,0:T(1,128)} %bitcast.10), calls=%async_computation.1 | async-start | bytes 4096 | tf_op jit(solution)/shard_map/all_to_all | solution.py:138
  293.7 8.5 %all-to-all-start.2 = ((bf16[4,2,12288]{2,1,0:T(2,128)(2,1)}), bf16[4,2,12288]{2,1,0:T(2,128)(2,1)S(1)}, u32[]{:S(2)}, u32[]{:S(2)}) async-start(bf16[4,2,12288]{2,1,0:T(2,128)(2,1)} %reshape.454), calls=%async_computation.2 | async-start | bytes 393216 | tf_op jit(solution)/shard_map/all_to_all | solution.py:137
  366.8 9.4 %copy-start.9 = (s32[6,1]{0,1:T(1,128)S(1)}, s32[6,1]{0,1:T(1,128)}, u32[]{:S(2)}) copy-start(s32[6,1]{0,1:T(1,128)} %copy-done.8) | copy-start | bytes 76
  366.8 131.1 %all-to-all-start.3 = ((bf16[32,48,2560]{2,1,0:T(8,128)(2,1)}), bf16[32,48,2560]{2,1,0:T(8,128)(2,1)}, u32[]{:S(2)}, u32[]{:S(2)}) async-start(bf16[32,48,2560]{2,1,0:T(8,128)(2,1)} %bitcast.89), calls=%async_computation.3 | async-start | bytes 15728640 | tf_op jit(solution)/shard_map/all_to_all | solution.py:27
  376.2 148.4 %copy-start.12 = (s32[16]{0:T(128)S(1)}, s32[16]{0:T(128)}, u32[]{:S(2)}) copy-start(s32[16]{0:T(128)} %param.19) | copy-start | bytes 196
  502.5 22.9 %copy-start.3 = (bf16[48,2560]{1,0:T(8,128)(2,1)}, bf16[48,2560]{1,0:T(8,128)(2,1)S(1)}, u32[]{:S(2)}) copy-start(bf16[48,2560]{1,0:T(8,128)(2,1)S(1)} %fusion.52) | copy-start | bytes 737284
  503.6 12.8 %all-to-all-start.4 = ((bf16[32,2,240]{2,1,0:T(2,128)(2,1)}), bf16[32,2,240]{2,1,0:T(2,128)(2,1)S(1)}, u32[]{:S(2)}, u32[]{:S(2)}) async-start(bf16[32,2,240]{2,1,0:T(2,128)(2,1)} %reshape.456), calls=%async_computation.4 | async-start | bytes 65536 | tf_op jit(solution)/shard_map/all_to_all | solution.py:27
Sparse Core Ops, SparseCore 0:
  20.4 73.6 all-gather.3
  278.6 67.2 all-gather.5

commit v9 on v8

--- a/solution.py
+++ b/solution.py
@@ -189,15 +189,21 @@
         tensor_element_count,
     )
     layer_out = (resid.astype(jnp.float32) + mlp_sum).astype(jnp.bfloat16)
+    width = w_down.shape[1]
+    feat = width // tensor_element_count
+    nprompt = prompt_ends.shape[0]
+    end_pick = ((prompt_ends - 1)[:, None] == all_ids[None, :]).astype(jnp.bfloat16)
+    end_hidden = jnp.dot(end_pick, hidden, preferred_element_type=jnp.float32).astype(jnp.bfloat16)
+    end_down = jnp.dot(end_hidden, w_down, preferred_element_type=jnp.float32).astype(jnp.bfloat16)
     my_rows = my_index * tok_dev + jnp.arange(tok_dev, dtype=jnp.int32)
     select = ((prompt_ends - 1)[:, None] == my_rows[None, :]).astype(jnp.bfloat16)
-    end_terms = jnp.dot(select, layer_out, preferred_element_type=jnp.float32)
-    end_blocks = end_terms.astype(jnp.bfloat16).reshape(
-        end_terms.shape[0], tensor_element_count, -1
-    )
-    end_rows = scatter_sum(jnp.transpose(end_blocks, (1, 0, 2)), tensor_element_count)[0].astype(
-        jnp.bfloat16
-    )
+    end_resid = jnp.dot(select, resid, preferred_element_type=jnp.float32)
+    end_terms = jnp.stack([end_down.astype(jnp.float32), end_resid])
+    end_blocks = jnp.transpose(
+        end_terms.reshape(2, nprompt, tensor_element_count, feat), (2, 0, 1, 3)
+    )
+    end_sums = lax.psum_scatter(end_blocks, TENSOR, scatter_dimension=0, tiled=True)[0]
+    end_rows = (end_sums[0] + end_sums[1]).astype(jnp.bfloat16)
     table = lax.all_gather(end_rows, "dp", axis=0, tiled=True)
     pick = (request_prompt[:, None] == jnp.arange(table.shape[0], dtype=jnp.int32)[None, :]).astype(
         jnp.bfloat16

time: 537 us -> 797 us (1.48)
  waiting for transfers between devices: 361 us -> 609 us
  blocking collectives: 26.2 us -> 43.8 us
    unnamed x2 -> x4, waiting for transfers between devices: 0.03 us -> 374 us
    all_to_all x3 -> x2, waiting for transfers between devices: 248 us -> 122 us  [scatter_sum(): got = lax.all_to_all(pieces, TENSOR, 0, 0, tiled=True)]
    all_gather x1, blocking collectives: 8.03 us -> 25.6 us  [per_device(): table = lax.all_gather(end_rows, 'dp', axis=0, tiled=True)]
    all_to_all x3 -> x2, starting transfers between devices: 25.3 us -> 18.7 us  [scatter_sum(): got = lax.all_to_all(pieces, TENSOR, 0, 0, tiled=True)]
  transfers between devices with their start and end apart: 9 -> 9, of which waited for: 9 -> 8; matrix products, arithmetic and copies ran while one was open for 3% -> 3% of each run, Pallas kernels for 0% -> 0%
where the time goes in v9:
time: 797 us; the launch traced here: 789 us
  waiting for transfers between devices  609 us (76%)
  blocking collectives  43.8 us (5%)
  matrix products  42.8 us (5%)
  starting transfers between devices  31.8 us (4%)
  other arithmetic  29.9 us (4%)
  local copies, waits for them, and re-layouts  15.6 us (2%)
  between operations  14.2 us (2%)
    unnamed x4, waiting for transfers between devices  374 us
    all_to_all x2, waiting for transfers between devices, scatter_sum(): got = lax.all_to_all(pieces, TENSOR, 0, 0, tiled=True)  122 us
    all_gather x2, waiting for transfers between devices, gather_rows(): return lax.all_gather(rows, ('ty', 'tx'), axis=0, tiled=True)  79.1 us
    ppermute x2, waiting for transfers between devices, partner_2(): return lax.ppermute(value, axis, pairs)  26.4 us
    all_gather x1, blocking collectives, per_device(): table = lax.all_gather(end_rows, 'dp', axis=0, tiled=True)  25.6 us
    all_to_all x2, starting transfers between devices, scatter_sum(): got = lax.all_to_all(pieces, TENSOR, 0, 0, tiled=True)  18.7 us
    all_gather x2, blocking collectives, gather_rows(): rows = lax.all_gather(rows, 'tz', axis=0, tiled=True)  18.2 us
  transfers between devices with their start and end apart: 9, of which 8 were waited for; matrix products, arithmetic and copies ran while one was open for 3% of the time, Pallas kernels for 0%

profile of v9, /device:TPU:27, one launch (start us, length us, event | category | flops | bytes accessed | tf_op | source)
XLA Modules:
  0.0 788.6 jit_solution(10298598283091658743)
XLA Ops:
  10.2 10.0 %all_gather.15 = bf16[96,2560]{1,0:T(8,128)(2,1)} all-gather(bf16[48,2560]{1,0:T(8,128)(2,1)S(1)} %fusion.48), channel_id=1, replica_groups=mesh['dp'=4,'ty'=4,'tx'=4,'tz'=2] {'tz'}, dimensions={0}, use_global_device_ids=true | all-gather | bytes 737280 | tf_op jit(solution)/shard_map/all_gather | solution.py:32
  20.3 2.8 collective-permute-start
  26.3 3.8 collective-permute-done
  32.3 22.6 %collective-permute-done.1 = bf16[2560,128]{0,1:T(8,128)(2,1)} collective-permute-done((bf16[2560,128]{0,1:T(8,128)(2,1)S(1)}, bf16[2560,128]{0,1:T(8,128)(2,1)}, u32[]{:S(2)}, u32[]{:S(2)}) %collective-permute-start.1) | collective-permute-done | bytes 655392 | tf_op jit(solution)/shard_map/ppermute | solution.py:22
  54.9 39.2 %all-gather.4.cloned.1.call-done = bf16[1536,2560]{1,0:T(8,128)(2,1)} async-done(((bf16[96,2560]{1,0:T(8,128)(2,1)}), bf16[1536,2560]{1,0:T(8,128)(2,1)}) %all-gather.4.cloned.1.call-update) | async-done | bytes 7864336 | tf_op jit(solution)/shard_map/all_gather | solution.py:33
  94.1 5.9 convolution_convert_fusion.3
  100.2 3.8 multiply_reduce_fusion
  106.6 2.4 fusion.55
  110.7 18.2 %while.11 = (s32[]{:T(128)}, bf16[3,1,512,128]{3,2,1,0:T(8,128)(2,1)S(1)}, s32[3]{0:T(128)S(1)}, s32[1536]{0:T(1024)S(1)}, bf16[1536,1,128]{0,2,1:T(8,128)(2,1)}...) while((s32[]{:T(128)}, ...), condition=%wide.region_9.10_spmd.clone, body=%wide.region_6.9_spmd.clone.sunk | while | flops 416939520 | bytes 12107995 | solution.py:175
  112.0 2.2 select_reduce_fusion.4
  115.3 1.5 fusion.110
  118.1 2.2 select_reduce_fusion.4
  124.2 2.2 select_reduce_fusion.4
  127.5 1.5 fusion.110
  129.0 5.3 convolution_convert_fusion.1
  134.3 9.3 %all-to-all-start = ((bf16[32,48,2560]{2,1,0:T(8,128)(2,1)}), bf16[32,48,2560]{2,1,0:T(8,128)(2,1)}, u32[]{:S(2)}, u32[]{:S(2)}) async-start(bf16[32,48,2560]{2,1,0:T(8,128)(2,1)} %bitcast.96), calls=%async_computation | async-start | bytes 15728640 | tf_op jit(solution)/shard_map/all_to_all | solution.py:27
  143.9 121.5 %all-to-all-done = bf16[32,48,2560]{2,1,0:T(8,128)(2,1)} async-done(((bf16[32,48,2560]{2,1,0:T(8,128)(2,1)}), bf16[32,48,2560]{2,1,0:T(8,128)(2,1)}, u32[]{:S(2)}, u32[]{:S(2)}) %all-to-all-start) | async-done | bytes 7864352 | tf_op jit(solution)/shard_map/all_to_all | solution.py:27
  265.4 4.5 convert_reduce_fusion.1
  270.3 8.2 %all_gather.17 = bf16[96,2560]{1,0:T(8,128)(2,1)} all-gather(bf16[48,2560]{1,0:T(8,128)(2,1)S(1)} %fusion.52), channel_id=1, replica_groups=mesh['dp'=4,'ty'=4,'tx'=4,'tz'=2] {'tz'}, dimensions={0}, use_global_device_ids=true | all-gather | bytes 737280 | tf_op jit(solution)/shard_map/all_gather | solution.py:32
  281.8 5.6 all-to-all-start.1
  287.4 3.0 all-to-all-done.1
  293.8 4.0 all-to-all-start.2
  297.8 4.5 all-to-all-done.2
  302.6 3.5 scatter_fusion
  306.1 39.9 %all-gather.6.cloned.1.call-done = bf16[1536,2560]{1,0:T(8,128)(2,1)} async-done(((bf16[96,2560]{1,0:T(8,128)(2,1)}), bf16[1536,2560]{1,0:T(8,128)(2,1)}) %all-gather.6.cloned.1.call-update) | async-done | bytes 7864336 | tf_op jit(solution)/shard_map/all_gather | solution.py:33
  346.0 5.6 fusion.84
  352.4 2.7 fusion.28
  355.0 6.5 convolution_convert_fusion
  361.5 9.3 %all-to-all-start.3 = ((bf16[32,48,2560]{2,1,0:T(8,128)(2,1)}), bf16[32,48,2560]{2,1,0:T(8,128)(2,1)}, u32[]{:S(2)}, u32[]{:S(2)}) async-start(bf16[32,48,2560]{2,1,0:T(8,128)(2,1)} %bitcast.97), calls=%async_computation.3 | async-start | bytes 15728640 | tf_op jit(solution)/shard_map/all_to_all | solution.py:27
  375.0 374.1 %all-reduce.3.cloned.1.call-done = f32[32,2,6,80]{3,1,0,2:T(2,128)} async-done(((f32[32,2,6,80]{3,1,0,2:T(2,128)}), f32[32,2,6,80]{3,1,0,2:T(2,128)}) %all-reduce.3.cloned.1.call-update) | async-done | bytes 122896
  750.4 25.6 %all-gather = bf16[1,1,24,80]{3,1,0,2:T(2,128)(2,1)S(1)} all-gather(bf16[1,1,6,80]{3,1,0,2:T(2,128)(2,1)S(1)} %fusion.75), channel_id=2, replica_groups=mesh['dp'=4,'ty'=4,'tx'=4,'tz'=2] {'dp'}, dimensions={2}, use_global_device_ids=true | all-gather | bytes 4800 | tf_op jit(solution)/shard_map/all_gather | solution.py:207
  776.8 4.5 convert_reduce_fusion
  (116 shorter events, 34.7 us)
Async XLA Ops:
  7.2 347.9 %copy-start = (bf16[304,2560]{1,0:T(8,128)(2,1)S(1)}, bf16[304,2560]{1,0:T(8,128)(2,1)}, u32[]{:S(2)}) copy-start(bf16[304,2560]{1,0:T(8,128)(2,1)} %param.29) | copy-start | bytes 4669444
  7.2 25.0 %copy-start.11 = (s32[1,6]{1,0:T(1,128)S(1)}, s32[1,6]{1,0:T(1,128)}, u32[]{:S(2)}) copy-start(s32[1,6]{1,0:T(1,128)} %param.17) | copy-start | bytes 76
  7.2 86.9 %all-gather.4.cloned.1.call-start = ((), (), s32[]{:S(2)}) async-start(), calls=%async_computation.4 | async-start | bytes 8355840 | tf_op jit(solution)/shard_map/all_gather | solution.py:33
  20.3 9.8 %collective-permute-start = (bf16[2560,64]{0,1:T(8,128)(2,1)}, bf16[2560,64]{0,1:T(8,128)(2,1)S(1)}, u32[]{:S(2)}, u32[]{:S(2)}) collective-permute-start(bf16[2560,64]{0,1:T(8,128)(2,1)} %param.25), channel_id=1, source_target_pairs={{0,1},{1,0},{2,3},{3,2},{4,5},{5,4},{6,7},{7,6},{8,9},{9,8},{10,11... | collective-permute-start | bytes 983048 | tf_op jit(solution)/shard_map/ppermute | solution.py:22
  23.9 76.2 %copy-start.7 = (s32[6,1]{0,1:T(1,128)}, s32[6,1]{0,1:T(1,128)S(1)}, u32[]{:S(2)}) copy-start(s32[6,1]{0,1:T(1,128)S(1)} %reduce-window.4) | copy-start | bytes 76
  31.3 23.6 %collective-permute-start.1 = (bf16[2560,128]{0,1:T(8,128)(2,1)S(1)}, bf16[2560,128]{0,1:T(8,128)(2,1)}, u32[]{:S(2)}, u32[]{:S(2)}) collective-permute-start(bf16[2560,128]{0,1:T(8,128)(2,1)S(1)} %maximum_select_fusion.2), channel_id=1, source_target_pairs={{0,2},{1,3},{2,0},{3,1},{4,6},{5,7},{6,4},{7,5},{8,10},{9,11},{10,... | collective-permute-start | bytes 1966088 | tf_op jit(solution)/shard_map/ppermute | solution.py:22
  94.1 6.0 copy-start.1
  105.7 5.0 copy-start.3
  110.7 18.2 %copy-start.4 = (bf16[128,2560]{1,0:T(8,128)(2,1)S(1)}, bf16[128,2560]{1,0:T(8,128)(2,1)}, u32[]{:S(2)}) copy-start(bf16[128,2560]{1,0:T(8,128)(2,1)} %param.26) | copy-start | bytes 1966084
  112.0 3.2 copy-start.5
  118.1 3.2 copy-start.5
  124.2 3.2 copy-start.5
  134.3 9.6 %copy-start.6 = (bf16[2560]{0:T(1024)(128)(2,1)S(1)}, bf16[2560]{0:T(1024)(128)(2,1)}, u32[]{:S(2)}) copy-start(bf16[2560]{0:T(1024)(128)(2,1)} %param.23) | copy-start | bytes 15364
  134.3 131.1 %all-to-all-start = ((bf16[32,48,2560]{2,1,0:T(8,128)(2,1)}), bf16[32,48,2560]{2,1,0:T(8,128)(2,1)}, u32[]{:S(2)}, u32[]{:S(2)}) async-start(bf16[32,48,2560]{2,1,0:T(8,128)(2,1)} %bitcast.96), calls=%async_computation | async-start | bytes 15728640 | tf_op jit(solution)/shard_map/all_to_all | solution.py:27
  143.7 202.3 %all-gather.6.cloned.1.call-start = ((), (), s32[]{:S(2)}) async-start(), calls=%async_computation.5 | async-start | bytes 8355840 | tf_op jit(solution)/shard_map/all_gather | solution.py:33
  143.9 126.1 %copy-start.2 = (bf16[48,2560]{1,0:T(8,128)(2,1)S(1)}, bf16[48,2560]{1,0:T(8,128)(2,1)}, u32[]{:S(2)}) copy-start(bf16[48,2560]{1,0:T(8,128)(2,1)} %param.16) | copy-start | bytes 737284
  143.9 134.6 %copy-start.12 = (s32[96]{0:T(128)S(1)}, s32[96]{0:T(128)}, u32[]{:S(2)}) copy-start(s32[96]{0:T(128)} %param.18) | copy-start | bytes 1156
  281.8 8.7 %all-to-all-start.1 = ((s32[4,1,24]{2,1,0:T(1,128)}), s32[4,1,24]{2,1,0:T(1,128)S(1)}, u32[]{:S(2)}, u32[]{:S(2)}) async-start(s32[4,1,24]{2,1,0:T(1,128)} %bitcast.10), calls=%async_computation.1 | async-start | bytes 4096 | tf_op jit(solution)/shard_map/all_to_all | solution.py:138
  293.8 8.5 %all-to-all-start.2 = ((bf16[4,2,12288]{2,1,0:T(2,128)(2,1)}), bf16[4,2,12288]{2,1,0:T(2,128)(2,1)S(1)}, u32[]{:S(2)}, u32[]{:S(2)}) async-start(bf16[4,2,12288]{2,1,0:T(2,128)(2,1)} %reshape.459), calls=%async_computation.2 | async-start | bytes 393216 | tf_op jit(solution)/shard_map/all_to_all | solution.py:137
  346.0 6.0 copy-start.9
  346.0 6.4 copy-start.10
  361.5 9.4 %copy-start.8 = (s32[6,1]{0,1:T(1,128)S(1)}, s32[6,1]{0,1:T(1,128)}, u32[]{:S(2)}) copy-start(s32[6,1]{0,1:T(1,128)} %copy-done.7) | copy-start | bytes 76
  361.5 415.3 %all-to-all-start.3 = ((bf16[32,48,2560]{2,1,0:T(8,128)(2,1)}), bf16[32,48,2560]{2,1,0:T(8,128)(2,1)}, u32[]{:S(2)}, u32[]{:S(2)}) async-start(bf16[32,48,2560]{2,1,0:T(8,128)(2,1)} %bitcast.97), calls=%async_computation.3 | async-start | bytes 15728640 | tf_op jit(solution)/shard_map/all_to_all | solution.py:27
  370.9 2.4 copy-start.14
  370.9 405.2 %copy-start.13 = (s32[16]{0:T(128)S(1)}, s32[16]{0:T(128)}, u32[]{:S(2)}) copy-start(s32[16]{0:T(128)} %param.19) | copy-start | bytes 196
  370.9 378.1 %all-reduce.3.cloned.1.call-start = ((), (), s32[]{:S(2)}) async-start(), calls=%async_computation.6 | async-start | bytes 393216
Sparse Core Ops, SparseCore 0:
  20.4 73.6 all-gather.3
  278.6 67.2 all-gather.5
  374.8 374.2 all-reduce.2

commit v10 on v8

--- a/solution.py
+++ b/solution.py
@@ -150,29 +150,32 @@
 
     def dense_block(block_index):
         first_row = block_index * block_rows
-        q_block = lax.dynamic_slice_in_dim(q_rot, first_row, block_rows, 0)
-        q_prompt = lax.dynamic_slice_in_dim(prompt, first_row, block_rows, 0)
+        key_count = first_row + block_rows
+        q_block = q_rot[first_row:key_count]
+        q_prompt = prompt[first_row:key_count]
         row_ids = first_row + local_ids
         scores = (
-            jnp.einsum("qhd,kd->hqk", q_block, key_flat, preferred_element_type=jnp.float32)
+            jnp.einsum(
+                "qhd,kd->hqk", q_block, key_flat[:key_count], preferred_element_type=jnp.float32
+            )
             / score_scale
         )
-        allowed = ((q_prompt[:, None] == prompt[None, :]) & (row_ids[:, None] >= all_ids[None, :]))[
-            None
-        ]
+        allowed = (
+            (q_prompt[:, None] == prompt[None, :key_count])
+            & (row_ids[:, None] >= all_ids[None, :key_count])
+        )[None]
         peak = jnp.max(jnp.where(allowed, scores, -jnp.inf), axis=2, keepdims=True)
         weight = jnp.where(allowed, jnp.exp(scores - peak), 0.0)
         total_weight = jnp.sum(weight, axis=2, keepdims=True)
         running = jnp.einsum(
             "hqk,kd->hqd",
             weight.astype(jnp.bfloat16),
-            value_matrix_rows,
+            value_matrix_rows[:key_count],
             preferred_element_type=jnp.float32,
         )
         return (running / total_weight).astype(jnp.bfloat16)
 
-    block_ids = jnp.arange(block_total, dtype=jnp.int32)
-    blocks_out = lax.map(dense_block, block_ids)
+    blocks_out = jnp.stack([dense_block(block_index) for block_index in range(block_total)])
     attn = jnp.transpose(blocks_out, (0, 2, 1, 3)).reshape(token_count, query_cols)
     attn_sum = scatter_sum(
         jnp.dot(attn, w_out, preferred_element_type=jnp.float32).astype(jnp.bfloat16),

time: 537 us -> 521 us (0.970)
  matrix products: 47.8 us -> 41.7 us
  other arithmetic: 26.9 us -> 21.5 us
    all_gather x2, waiting for transfers between devices: 79.1 us -> 102 us  [gather_rows(): return lax.all_gather(rows, ('ty', 'tx'), axis=0, tiled=True)]
    ppermute x2, waiting for transfers between devices: 26.4 us -> 5.44 us  [partner_2(): return lax.ppermute(value, axis, pairs)]
    dot_general x6, matrix products: 11 us -> 4.72 us  [the longest x3 2.73 us: dense_block(): jnp.einsum('hqk,kd->hqd', weight.astype(jnp.bfloat16), value_matrix_rows[...]
  transfers between devices with their start and end apart: 9 -> 9, of which waited for: 9 -> 8; matrix products, arithmetic and copies ran while one was open for 3% -> 4% of each run, Pallas kernels for 0% -> 0%
where the time goes in v10:
time: 521 us; the launch traced here: 517 us
  waiting for transfers between devices  364 us (70%)
  matrix products  41.7 us (8%)
  starting transfers between devices  38.1 us (7%)
  blocking collectives  26.2 us (5%)
  other arithmetic  21.5 us (4%)
  between operations  14.6 us (3%)
  local copies, waits for them, and re-layouts  11.2 us (2%)
    all_to_all x3, waiting for transfers between devices, scatter_sum(): got = lax.all_to_all(pieces, TENSOR, 0, 0, tiled=True)  248 us
    all_gather x2, waiting for transfers between devices, gather_rows(): return lax.all_gather(rows, ('ty', 'tx'), axis=0, tiled=True)  102 us
    all_to_all x3, starting transfers between devices, scatter_sum(): got = lax.all_to_all(pieces, TENSOR, 0, 0, tiled=True)  25.2 us
    all_gather x2, blocking collectives, gather_rows(): rows = lax.all_gather(rows, 'tz', axis=0, tiled=True)  18.2 us
    dot_general x1, matrix products, per_device(): jnp.dot(hidden, w_down, preferred_element_type=jnp.float32)  13.4 us
  transfers between devices with their start and end apart: 9, of which 8 were waited for; matrix products, arithmetic and copies ran while one was open for 4% of the time, Pallas kernels for 0%

profile of v10, /device:TPU:27, one launch (start us, length us, event | category | flops | bytes accessed | tf_op | source)
XLA Modules:
  0.0 516.9 jit_solution(12782284573498920695)
XLA Ops:
  7.3 1.2 fusion.58
  9.2 1.1 fusion.60
  10.3 10.0 %all_gather.15 = bf16[96,2560]{1,0:T(8,128)(2,1)} all-gather(bf16[48,2560]{1,0:T(8,128)(2,1)S(1)} %fusion.60), channel_id=1, replica_groups=mesh['dp'=4,'ty'=4,'tx'=4,'tz'=2] {'tz'}, dimensions={0}, use_global_device_ids=true | all-gather | bytes 737280 | tf_op jit(solution)/shard_map/all_gather | solution.py:32
  20.3 2.8 collective-permute-start
  24.8 5.4 %collective-permute-done = bf16[2560,64]{0,1:T(8,128)(2,1)} collective-permute-done((bf16[2560,64]{0,1:T(8,128)(2,1)}, bf16[2560,64]{0,1:T(8,128)(2,1)}, u32[]{:S(2)}, u32[]{:S(2)}) %collective-permute-start) | collective-permute-done | bytes 327712 | tf_op jit(solution)/shard_map/ppermute | solution.py:22
  30.3 1.2 maximum_select_fusion.2
  31.8 62.3 %all-gather.4.cloned.1.call-done = bf16[1536,2560]{1,0:T(8,128)(2,1)} async-done(((bf16[96,2560]{1,0:T(8,128)(2,1)}), bf16[1536,2560]{1,0:T(8,128)(2,1)}) %all-gather.4.cloned.1.call-update) | async-done | bytes 7864336 | tf_op jit(solution)/shard_map/all_gather | solution.py:33
  94.2 6.1 %multiply_reduce_fusion = (f32[1536]{0:T(1024)S(1)}, f32[1536,128]{0,1:T(8,128)S(1)}) fusion(bf16[1536,2560]{1,0:T(8,128)(2,1)} %all-gather.4.cloned.1.call-done, bf16[2560,128]{1,0:T(8,128)(2,1)S(1)} %copy-done.4), kind=kOutput, calls=%fused_computation.65 | convolution fusion | flops 1007024640 | bytes 9312256 | tf_op jit(solution)/shard_map/dot_general | solution.py:103
  100.3 3.6 convolution_convert_fusion.3
  104.4 1.9 fusion.71
  111.0 1.3 fusion.6
  112.3 1.3 fusion.30
  113.7 5.4 %convolution_convert_fusion.1 = bf16[1536,2560]{1,0:T(8,128)(2,1)} fusion(bf16[1536,128]{1,0:T(8,128)(2,1)S(1)} %bitcast.118, bf16[128,2560]{1,0:T(8,128)(2,1)S(1)} %copy-done.5), kind=kOutput, calls=%fused_computation.7 | convolution fusion | flops 1010565120 | bytes 8912896 | tf_op jit(solution)/shard_map/dot_general | solution.py:181
  119.0 9.3 %all-to-all-start = ((bf16[32,48,2560]{2,1,0:T(8,128)(2,1)}), bf16[32,48,2560]{2,1,0:T(8,128)(2,1)}, u32[]{:S(2)}, u32[]{:S(2)}) async-start(bf16[32,48,2560]{2,1,0:T(8,128)(2,1)} %bitcast.116), calls=%async_computation | async-start | bytes 15728640 | tf_op jit(solution)/shard_map/all_to_all | solution.py:27
  128.4 121.7 %all-to-all-done = bf16[32,48,2560]{2,1,0:T(8,128)(2,1)} async-done(((bf16[32,48,2560]{2,1,0:T(8,128)(2,1)}), bf16[32,48,2560]{2,1,0:T(8,128)(2,1)}, u32[]{:S(2)}, u32[]{:S(2)}) %all-to-all-start) | async-done | bytes 7864352 | tf_op jit(solution)/shard_map/all_to_all | solution.py:27
  250.1 4.5 convert_reduce_fusion.1
  255.0 8.2 %all_gather.17 = bf16[96,2560]{1,0:T(8,128)(2,1)} all-gather(bf16[48,2560]{1,0:T(8,128)(2,1)S(1)} %fusion.64), channel_id=1, replica_groups=mesh['dp'=4,'ty'=4,'tx'=4,'tz'=2] {'tz'}, dimensions={0}, use_global_device_ids=true | all-gather | bytes 737280 | tf_op jit(solution)/shard_map/all_gather | solution.py:32
  264.6 1.2 gather_fusion
  266.5 5.6 %all-to-all-start.1 = ((s32[4,1,24]{2,1,0:T(1,128)}), s32[4,1,24]{2,1,0:T(1,128)S(1)}, u32[]{:S(2)}, u32[]{:S(2)}) async-start(s32[4,1,24]{2,1,0:T(1,128)} %bitcast.30), calls=%async_computation.1 | async-start | bytes 4096 | tf_op jit(solution)/shard_map/all_to_all | solution.py:138
  272.1 3.0 all-to-all-done.1
  278.5 4.0 all-to-all-start.2
  282.5 4.5 all-to-all-done.2
  287.4 3.5 scatter_fusion
  290.8 39.9 %all-gather.6.cloned.1.call-done = bf16[1536,2560]{1,0:T(8,128)(2,1)} async-done(((bf16[96,2560]{1,0:T(8,128)(2,1)}), bf16[1536,2560]{1,0:T(8,128)(2,1)}) %all-gather.6.cloned.1.call-update) | async-done | bytes 7864336 | tf_op jit(solution)/shard_map/all_gather | solution.py:33
  330.8 7.5 %fusion.118 = f32[1536,304]{0,1:T(8,128)} fusion(bf16[1536,2560]{1,0:T(8,128)(2,1)} %all-gather.6.cloned.1.call-done, bf16[2560,304]{0,1:T(8,128)(2,1)} %param.25), kind=kOutput, calls=%fused_computation.182 | convolution fusion | flops 2390753280 | bytes 11288576 | tf_op jit(solution)/shard_map/dot_general | solution.py:187
  338.2 13.4 %convolution_convert_fusion = bf16[1536,2560]{1,0:T(8,128)(2,1)} fusion(bf16[304,2560]{1,0:T(8,128)(2,1)S(1)} %copy-done, bf16[1536,2560]{1,0:T(8,128)(2,1)} %all-gather.6.cloned.1.call-done, bf16[2560,304]{0,1:T(8,128)(2,1)} %param.26, f32[1536,304]{0,1:T(8,128)} %fusion.118), kind=kOutput, calls=%fused_computation.6 | convolution fusion | flops 4788240384 | bytes 20709376 | tf_op jit(solution)/shard_map/dot_general | solution.py:191
  351.6 9.2 %all-to-all-start.3 = ((bf16[32,48,2560]{2,1,0:T(8,128)(2,1)}), bf16[32,48,2560]{2,1,0:T(8,128)(2,1)}, u32[]{:S(2)}, u32[]{:S(2)}) async-start(bf16[32,48,2560]{2,1,0:T(8,128)(2,1)} %bitcast.117), calls=%async_computation.3 | async-start | bytes 15728640 | tf_op jit(solution)/shard_map/all_to_all | solution.py:27
  360.9 121.7 %all-to-all-done.3 = bf16[32,48,2560]{2,1,0:T(8,128)(2,1)} async-done(((bf16[32,48,2560]{2,1,0:T(8,128)(2,1)}), bf16[32,48,2560]{2,1,0:T(8,128)(2,1)}, u32[]{:S(2)}, u32[]{:S(2)}) %all-to-all-start.3) | async-done | bytes 7864352 | tf_op jit(solution)/shard_map/all_to_all | solution.py:27
  482.5 4.5 convert_reduce_fusion
  488.2 6.7 %all-to-all-start.4 = ((bf16[32,2,240]{2,1,0:T(2,128)(2,1)}), bf16[32,2,240]{2,1,0:T(2,128)(2,1)S(1)}, u32[]{:S(2)}, u32[]{:S(2)}) async-start(bf16[32,2,240]{2,1,0:T(2,128)(2,1)} %reshape.682), calls=%async_computation.4 | async-start | bytes 65536 | tf_op jit(solution)/shard_map/all_to_all | solution.py:27
  496.0 5.0 all-to-all-done.4
  501.2 8.0 %all-gather = bf16[4,6,80]{2,1,0:T(8,128)(2,1)S(1)} all-gather(bf16[1,6,80]{2,1,0:T(8,128)(2,1)S(1)} %bitcast.127), channel_id=1, replica_groups=mesh['dp'=4,'ty'=4,'tx'=4,'tz'=2] {'dp'}, dimensions={0}, use_global_device_ids=true | all-gather | bytes 4800 | tf_op jit(solution)/shard_map/all_gather | solution.py:204
  (95 shorter events, 17.1 us)
Async XLA Ops:
  7.2 331.1 %copy-start = (bf16[304,2560]{1,0:T(8,128)(2,1)S(1)}, bf16[304,2560]{1,0:T(8,128)(2,1)}, u32[]{:S(2)}) copy-start(bf16[304,2560]{1,0:T(8,128)(2,1)} %param.27) | copy-start | bytes 4669444
  7.2 23.1 %copy-start.6 = (bf16[2560,64]{0,1:T(8,128)(2,1)S(1)}, bf16[2560,64]{0,1:T(8,128)(2,1)}, u32[]{:S(2)}) copy-start(bf16[2560,64]{0,1:T(8,128)(2,1)} %param.23) | copy-start | bytes 983044
  7.2 17.4 %copy-start.9 = (s32[1,6]{1,0:T(1,128)S(1)}, s32[1,6]{1,0:T(1,128)}, u32[]{:S(2)}) copy-start(s32[1,6]{1,0:T(1,128)} %param.15) | copy-start | bytes 76
  7.2 17.4 %copy-start.8 = (bf16[128]{0:T(256)(128)(2,1)S(1)}, bf16[128]{0:T(256)(128)(2,1)}, u32[]{:S(2)}) copy-start(bf16[128]{0:T(256)(128)(2,1)} %param.20) | copy-start | bytes 772
  7.2 86.9 %copy-start.4 = (bf16[2560,128]{1,0:T(8,128)(2,1)S(1)}, bf16[2560,128]{1,0:T(8,128)(2,1)}, u32[]{:S(2)}) copy-start(bf16[2560,128]{1,0:T(8,128)(2,1)} %param.22) | copy-start | bytes 1966084
  7.2 86.9 %all-gather.4.cloned.1.call-start = ((), (), s32[]{:S(2)}) async-start(), calls=%async_computation.5 | async-start | bytes 8355840 | tf_op jit(solution)/shard_map/all_gather | solution.py:33
  20.3 9.9 %collective-permute-start = (bf16[2560,64]{0,1:T(8,128)(2,1)}, bf16[2560,64]{0,1:T(8,128)(2,1)}, u32[]{:S(2)}, u32[]{:S(2)}) collective-permute-start(bf16[2560,64]{0,1:T(8,128)(2,1)} %param.23), channel_id=1, source_target_pairs={{0,1},{1,0},{2,3},{3,2},{4,5},{5,4},{6,7},{7,6},{8,9},{9,8},{10,11... | collective-permute-start | bytes 983048 | tf_op jit(solution)/shard_map/ppermute | solution.py:22
  31.5 68.8 %collective-permute-start.1 = (bf16[2560,128]{0,1:T(8,128)(2,1)S(1)}, bf16[2560,128]{0,1:T(8,128)(2,1)}, u32[]{:S(2)}, u32[]{:S(2)}) collective-permute-start(bf16[2560,128]{0,1:T(8,128)(2,1)S(1)} %maximum_select_fusion.2), channel_id=1, source_target_pairs={{0,2},{1,3},{2,0},{3,1},{4,6},{5,7},{6,4},{7,5},{8,10},{9,11},{10,... | collective-permute-start | bytes 1966088 | tf_op jit(solution)/shard_map/ppermute | solution.py:22
  94.2 6.1 %copy-start.1 = (bf16[1536,2560]{1,0:T(8,128)(2,1)S(1)}, bf16[1536,2560]{1,0:T(8,128)(2,1)}, u32[]{:S(2)}) copy-start(bf16[1536,2560]{1,0:T(8,128)(2,1)} %all-gather.4.cloned.1.call-done) | copy-start | bytes 23592964
  112.3 1.3 copy-start.5
  119.0 9.4 %copy-start.7 = (bf16[2560]{0:T(1024)(128)(2,1)S(1)}, bf16[2560]{0:T(1024)(128)(2,1)}, u32[]{:S(2)}) copy-start(bf16[2560]{0:T(1024)(128)(2,1)} %param.21) | copy-start | bytes 15364
  119.0 131.1 %all-to-all-start = ((bf16[32,48,2560]{2,1,0:T(8,128)(2,1)}), bf16[32,48,2560]{2,1,0:T(8,128)(2,1)}, u32[]{:S(2)}, u32[]{:S(2)}) async-start(bf16[32,48,2560]{2,1,0:T(8,128)(2,1)} %bitcast.116), calls=%async_computation | async-start | bytes 15728640 | tf_op jit(solution)/shard_map/all_to_all | solution.py:27
  128.4 202.4 %all-gather.6.cloned.1.call-start = ((), (), s32[]{:S(2)}) async-start(), calls=%async_computation.6 | async-start | bytes 8355840 | tf_op jit(solution)/shard_map/all_gather | solution.py:33
  128.4 126.2 %copy-start.2 = (bf16[48,2560]{1,0:T(8,128)(2,1)S(1)}, bf16[48,2560]{1,0:T(8,128)(2,1)}, u32[]{:S(2)}) copy-start(bf16[48,2560]{1,0:T(8,128)(2,1)} %param.14) | copy-start | bytes 737284
  254.7 8.6 %copy-start.10 = (s32[96]{0:T(128)S(1)}, s32[96]{0:T(128)}, u32[]{:S(2)}) copy-start(s32[96]{0:T(128)} %param.16) | copy-start | bytes 1156
  266.5 8.7 %all-to-all-start.1 = ((s32[4,1,24]{2,1,0:T(1,128)}), s32[4,1,24]{2,1,0:T(1,128)S(1)}, u32[]{:S(2)}, u32[]{:S(2)}) async-start(s32[4,1,24]{2,1,0:T(1,128)} %bitcast.30), calls=%async_computation.1 | async-start | bytes 4096 | tf_op jit(solution)/shard_map/all_to_all | solution.py:138
  278.5 8.5 %all-to-all-start.2 = ((bf16[4,2,12288]{2,1,0:T(2,128)(2,1)}), bf16[4,2,12288]{2,1,0:T(2,128)(2,1)S(1)}, u32[]{:S(2)}, u32[]{:S(2)}) async-start(bf16[4,2,12288]{2,1,0:T(2,128)(2,1)} %reshape.680), calls=%async_computation.2 | async-start | bytes 393216 | tf_op jit(solution)/shard_map/all_to_all | solution.py:137
  351.6 130.9 %all-to-all-start.3 = ((bf16[32,48,2560]{2,1,0:T(8,128)(2,1)}), bf16[32,48,2560]{2,1,0:T(8,128)(2,1)}, u32[]{:S(2)}, u32[]{:S(2)}) async-start(bf16[32,48,2560]{2,1,0:T(8,128)(2,1)} %bitcast.117), calls=%async_computation.3 | async-start | bytes 15728640 | tf_op jit(solution)/shard_map/all_to_all | solution.py:27
  487.1 22.2 %copy-start.11 = (s32[16]{0:T(128)S(1)}, s32[16]{0:T(128)}, u32[]{:S(2)}) copy-start(s32[16]{0:T(128)} %param.17) | copy-start | bytes 196
  487.1 22.9 %copy-start.3 = (bf16[48,2560]{1,0:T(8,128)(2,1)}, bf16[48,2560]{1,0:T(8,128)(2,1)S(1)}, u32[]{:S(2)}) copy-start(bf16[48,2560]{1,0:T(8,128)(2,1)S(1)} %fusion.65) | copy-start | bytes 737284
  488.2 12.8 %all-to-all-start.4 = ((bf16[32,2,240]{2,1,0:T(2,128)(2,1)}), bf16[32,2,240]{2,1,0:T(2,128)(2,1)S(1)}, u32[]{:S(2)}, u32[]{:S(2)}) async-start(bf16[32,2,240]{2,1,0:T(2,128)(2,1)} %reshape.682), calls=%async_computation.4 | async-start | bytes 65536 | tf_op jit(solution)/shard_map/all_to_all | solution.py:27
Sparse Core Ops, SparseCore 0:
  20.5 73.6 all-gather.3
  263.4 67.3 all-gather.5

commit v11 on v10

--- a/solution.py
+++ b/solution.py
@@ -187,19 +187,40 @@
     gate_rows = jnp.dot(portion, w_gate, preferred_element_type=jnp.float32)
     upward = jnp.dot(portion, w_up, preferred_element_type=jnp.float32)
     hidden = (jax.nn.silu(gate_rows) * upward).astype(jnp.bfloat16)
-    mlp_sum = scatter_sum(
-        jnp.dot(hidden, w_down, preferred_element_type=jnp.float32).astype(jnp.bfloat16),
-        tensor_element_count,
-    )
-    layer_out = (resid.astype(jnp.float32) + mlp_sum).astype(jnp.bfloat16)
+    down = jnp.dot(hidden, w_down, preferred_element_type=jnp.float32).astype(jnp.bfloat16)
+    width = down.shape[1]
+    feat = width // tensor_element_count
+    nprompt = prompt_ends.shape[0]
+    end_pick = ((prompt_ends - 1)[:, None] == all_ids[None, :]).astype(jnp.bfloat16)
+    end_hidden = jnp.dot(end_pick, hidden, preferred_element_type=jnp.float32).astype(jnp.bfloat16)
+    end_down = jnp.dot(end_hidden, w_down, preferred_element_type=jnp.float32).astype(jnp.bfloat16)
     my_rows = my_index * tok_dev + jnp.arange(tok_dev, dtype=jnp.int32)
     select = ((prompt_ends - 1)[:, None] == my_rows[None, :]).astype(jnp.bfloat16)
-    end_terms = jnp.dot(select, layer_out, preferred_element_type=jnp.float32)
-    end_blocks = end_terms.astype(jnp.bfloat16).reshape(
-        end_terms.shape[0], tensor_element_count, -1
-    )
-    end_rows = scatter_sum(jnp.transpose(end_blocks, (1, 0, 2)), tensor_element_count)[0].astype(
-        jnp.bfloat16
+    end_resid = jnp.dot(select, resid, preferred_element_type=jnp.float32).astype(jnp.bfloat16)
+
+    def by_feature_block(rows):
+        blocks = rows.reshape(nprompt, tensor_element_count, feat)
+        return jnp.transpose(blocks, (1, 0, 2)).reshape(tensor_element_count, nprompt * feat)
+
+    extra = jnp.concatenate([by_feature_block(end_down), by_feature_block(end_resid)], axis=1)
+    extra_cols = 128
+    extra = jnp.pad(extra, ((0, 0), (0, tok_dev * extra_cols - extra.shape[1])))
+    payload = jnp.concatenate(
+        [
+            down.reshape(tensor_element_count, tok_dev, width),
+            extra.reshape(tensor_element_count, tok_dev, extra_cols),
+        ],
+        axis=2,
+    )
+    got = lax.all_to_all(payload, TENSOR, 0, 0, tiled=True)
+    summed = jnp.sum(got.astype(jnp.float32), axis=0)
+    mlp_sum = summed[:, :width]
+    layer_out = (resid.astype(jnp.float32) + mlp_sum).astype(jnp.bfloat16)
+    tail = summed[:, width:].reshape(-1)
+    end_rows = (
+        (tail[: nprompt * feat] + tail[nprompt * feat : 2 * nprompt * feat])
+        .reshape(nprompt, feat)
+        .astype(jnp.bfloat16)
     )
     table = lax.all_gather(end_rows, "dp", axis=0, tiled=True)
     pick = (request_prompt[:, None] == jnp.arange(table.shape[0], dtype=jnp.int32)[None, :]).astype(

time: 521 us -> 515 us (0.988)
  other arithmetic: 21.5 us -> 30 us
  starting transfers between devices: 38.1 us -> 31.4 us
    all_to_all x0 -> x1, waiting for transfers between devices: none -> 129 us  [per_device(): got = lax.all_to_all(payload, TENSOR, 0, 0, tiled=True)]
    all_to_all x3 -> x1, waiting for transfers between devices: 248 us -> 122 us  [scatter_sum(): got = lax.all_to_all(pieces, TENSOR, 0, 0, tiled=True)]
    all_to_all x3 -> x1, starting transfers between devices: 25.2 us -> 9.33 us  [scatter_sum(): got = lax.all_to_all(pieces, TENSOR, 0, 0, tiled=True)]
    all_to_all x0 -> x1, starting transfers between devices: none -> 9.2 us  [per_device(): got = lax.all_to_all(payload, TENSOR, 0, 0, tiled=True)]
    concatenate x0 -> x1, other arithmetic: none -> 6.97 us  [per_device(): jnp.concatenate([down.reshape(tensor_element_count, tok_dev, width), extr...]
    dot_general x1, matrix products: 13.4 us -> 6.51 us  [per_device(): jnp.dot(hidden, w_down, preferred_element_type=jnp.float32)]
  transfers between devices with their start and end apart: 9 -> 8, of which waited for: 8 -> 7; matrix products, arithmetic and copies ran while one was open for 4% -> 4% of each run, Pallas kernels for 0% -> 0%
where the time goes in v11:
time: 515 us; the launch traced here: 514 us
  waiting for transfers between devices  365 us (71%)
  matrix products  36.6 us (7%)
  starting transfers between devices  31.4 us (6%)
  other arithmetic  30 us (6%)
  blocking collectives  24.8 us (5%)
  between operations  14.6 us (3%)
  local copies, waits for them, and re-layouts  11.9 us (2%)
    all_to_all x1, waiting for transfers between devices, per_device(): got = lax.all_to_all(payload, TENSOR, 0, 0, tiled=True)  129 us
    all_to_all x1, waiting for transfers between devices, scatter_sum(): got = lax.all_to_all(pieces, TENSOR, 0, 0, tiled=True)  122 us
    all_gather x2, waiting for transfers between devices, gather_rows(): return lax.all_gather(rows, ('ty', 'tx'), axis=0, tiled=True)  102 us
    all_gather x2, blocking collectives, gather_rows(): rows = lax.all_gather(rows, 'tz', axis=0, tiled=True)  18.2 us
  transfers between devices with their start and end apart: 8, of which 7 were waited for; matrix products, arithmetic and copies ran while one was open for 4% of the time, Pallas kernels for 0%

profile of v11, /device:TPU:27, one launch (start us, length us, event | category | flops | bytes accessed | tf_op | source)
XLA Modules:
  0.0 514.2 jit_solution(12413823835630630825)
XLA Ops:
  7.3 1.2 fusion.60
  9.2 1.1 fusion.62
  10.3 10.0 %all_gather.15 = bf16[96,2560]{1,0:T(8,128)(2,1)} all-gather(bf16[48,2560]{1,0:T(8,128)(2,1)S(1)} %fusion.62), channel_id=1, replica_groups=mesh['dp'=4,'ty'=4,'tx'=4,'tz'=2] {'tz'}, dimensions={0}, use_global_device_ids=true | all-gather | bytes 737280 | tf_op jit(solution)/shard_map/all_gather | solution.py:32
  20.3 2.8 collective-permute-start
  25.3 4.9 collective-permute-done
  30.3 1.2 maximum_select_fusion.2
  31.8 62.3 %all-gather.4.cloned.1.call-done = bf16[1536,2560]{1,0:T(8,128)(2,1)} async-done(((bf16[96,2560]{1,0:T(8,128)(2,1)}), bf16[1536,2560]{1,0:T(8,128)(2,1)}) %all-gather.4.cloned.1.call-update) | async-done | bytes 7864336 | tf_op jit(solution)/shard_map/all_gather | solution.py:33
  94.2 6.1 %multiply_reduce_fusion = (f32[1536]{0:T(1024)S(1)}, f32[1536,128]{0,1:T(8,128)S(1)}) fusion(bf16[1536,2560]{1,0:T(8,128)(2,1)} %all-gather.4.cloned.1.call-done, bf16[2560,128]{1,0:T(8,128)(2,1)S(1)} %copy-done.3), kind=kOutput, calls=%fused_computation.71 | convolution fusion | flops 1007024640 | bytes 9312256 | tf_op jit(solution)/shard_map/dot_general | solution.py:103
  100.3 3.6 convolution_convert_fusion.4
  104.6 1.7 fusion.73
  111.1 1.3 fusion.6
  112.4 1.3 fusion.30
  113.7 5.3 %convolution_convert_fusion.1 = bf16[1536,2560]{1,0:T(8,128)(2,1)} fusion(bf16[1536,128]{1,0:T(8,128)(2,1)S(1)} %bitcast.126, bf16[128,2560]{1,0:T(8,128)(2,1)S(1)} %copy-done.4), kind=kOutput, calls=%fused_computation.7 | convolution fusion | flops 1010565120 | bytes 8912896 | tf_op jit(solution)/shard_map/dot_general | solution.py:181
  119.1 9.3 %all-to-all-start = ((bf16[32,48,2560]{2,1,0:T(8,128)(2,1)}), bf16[32,48,2560]{2,1,0:T(8,128)(2,1)}, u32[]{:S(2)}, u32[]{:S(2)}) async-start(bf16[32,48,2560]{2,1,0:T(8,128)(2,1)} %bitcast.124), calls=%async_computation | async-start | bytes 15728640 | tf_op jit(solution)/shard_map/all_to_all | solution.py:27
  128.5 121.7 %all-to-all-done = bf16[32,48,2560]{2,1,0:T(8,128)(2,1)} async-done(((bf16[32,48,2560]{2,1,0:T(8,128)(2,1)}), bf16[32,48,2560]{2,1,0:T(8,128)(2,1)}, u32[]{:S(2)}, u32[]{:S(2)}) %all-to-all-start) | async-done | bytes 7864352 | tf_op jit(solution)/shard_map/all_to_all | solution.py:27
  250.2 4.5 convert_reduce_fusion.1
  255.1 8.2 %all_gather.17 = bf16[96,2560]{1,0:T(8,128)(2,1)} all-gather(bf16[48,2560]{1,0:T(8,128)(2,1)S(1)} %fusion.66), channel_id=1, replica_groups=mesh['dp'=4,'ty'=4,'tx'=4,'tz'=2] {'tz'}, dimensions={0}, use_global_device_ids=true | all-gather | bytes 737280 | tf_op jit(solution)/shard_map/all_gather | solution.py:32
  264.7 1.2 gather_fusion
  266.6 5.6 %all-to-all-start.1 = ((s32[4,1,24]{2,1,0:T(1,128)}), s32[4,1,24]{2,1,0:T(1,128)S(1)}, u32[]{:S(2)}, u32[]{:S(2)}) async-start(s32[4,1,24]{2,1,0:T(1,128)} %bitcast.30), calls=%async_computation.1 | async-start | bytes 4096 | tf_op jit(solution)/shard_map/all_to_all | solution.py:138
  272.2 3.0 all-to-all-done.1
  278.6 4.0 all-to-all-start.2
  282.6 4.5 all-to-all-done.2
  287.5 3.5 scatter_fusion
  291.4 39.3 %all-gather.6.cloned.1.call-done = bf16[1536,2560]{1,0:T(8,128)(2,1)} async-done(((bf16[96,2560]{1,0:T(8,128)(2,1)}), bf16[1536,2560]{1,0:T(8,128)(2,1)}) %all-gather.6.cloned.1.call-update) | async-done | bytes 7864336 | tf_op jit(solution)/shard_map/all_gather | solution.py:33
  330.7 5.6 %fusion.124 = f32[1536,304]{0,1:T(8,128)S(1)} fusion(bf16[1536,2560]{1,0:T(8,128)(2,1)} %all-gather.6.cloned.1.call-done, bf16[2560,304]{0,1:T(8,128)(2,1)} %param.25), kind=kOutput, calls=%fused_computation.195 | convolution fusion | flops 2390753280 | bytes 11288576 | tf_op jit(solution)/shard_map/dot_general | solution.py:187
  337.1 2.7 fusion.2
  340.8 6.5 %convolution_convert_fusion = bf16[1536,2560]{1,0:T(8,128)(2,1)} fusion(bf16[1536,304]{0,1:T(8,128)(2,1)S(1)} %fusion.2, bf16[304,2560]{1,0:T(8,128)(2,1)S(1)} %copy-done), kind=kOutput, calls=%fused_computation.6 | convolution fusion | flops 2394685440 | bytes 10354688 | tf_op jit(solution)/shard_map/dot_general | solution.py:190
  347.7 7.0 %pad_maximum_fusion = bf16[32,48,2688]{2,1,0:T(8,128)(2,1)} fusion(bf16[32,48,128]{2,1,0:T(8,128)(2,1)S(1)} %bitcast.130, bf16[32,48,2560]{2,1,0:T(8,128)(2,1)} %bitcast.125), kind=kLoop, calls=%fused_computation.8 | loop fusion | flops 16515072 | bytes 16515072 | tf_op jit(solution)/shard_map/concatenate | solution.py:208
  354.7 9.2 %all-to-all-start.3 = ((bf16[32,48,2688]{2,1,0:T(8,128)(2,1)}), bf16[32,48,2688]{2,1,0:T(8,128)(2,1)}, u32[]{:S(2)}, u32[]{:S(2)}) async-start(bf16[32,48,2688]{2,1,0:T(8,128)(2,1)} %pad_maximum_fusion), calls=%async_computation.3 | async-start | bytes 16515072 | tf_op jit(solution)/shard_map/all_to_all | solution.py:215
  364.9 129.2 %all-to-all-done.3 = bf16[32,48,2688]{2,1,0:T(8,128)(2,1)} async-done(((bf16[32,48,2688]{2,1,0:T(8,128)(2,1)}), bf16[32,48,2688]{2,1,0:T(8,128)(2,1)}, u32[]{:S(2)}, u32[]{:S(2)}) %all-to-all-start.3) | async-done | bytes 8257568 | tf_op jit(solution)/shard_map/all_to_all | solution.py:215
  494.1 4.9 convert_reduce_fusion
  499.9 6.6 %all-gather = bf16[4,6,80]{2,1,0:T(8,128)(2,1)S(1)} all-gather(bf16[1,6,80]{2,1,0:T(8,128)(2,1)S(1)} %reshape.686), channel_id=1, replica_groups=mesh['dp'=4,'ty'=4,'tx'=4,'tz'=2] {'dp'}, dimensions={0}, use_global_device_ids=true | all-gather | bytes 4800 | tf_op jit(solution)/shard_map/all_gather | solution.py:225
  (106 shorter events, 20.1 us)
Async XLA Ops:
  7.2 332.6 %copy-start = (bf16[304,2560]{1,0:T(8,128)(2,1)S(1)}, bf16[304,2560]{1,0:T(8,128)(2,1)}, u32[]{:S(2)}) copy-start(bf16[304,2560]{1,0:T(8,128)(2,1)} %param.27) | copy-start | bytes 4669444
  7.2 23.1 %copy-start.5 = (bf16[2560,64]{0,1:T(8,128)(2,1)S(1)}, bf16[2560,64]{0,1:T(8,128)(2,1)}, u32[]{:S(2)}) copy-start(bf16[2560,64]{0,1:T(8,128)(2,1)} %param.23) | copy-start | bytes 983044
  7.2 17.4 %copy-start.11 = (s32[1,6]{1,0:T(1,128)S(1)}, s32[1,6]{1,0:T(1,128)}, u32[]{:S(2)}) copy-start(s32[1,6]{1,0:T(1,128)} %param.15) | copy-start | bytes 76
  7.2 17.4 %copy-start.10 = (bf16[128]{0:T(256)(128)(2,1)S(1)}, bf16[128]{0:T(256)(128)(2,1)}, u32[]{:S(2)}) copy-start(bf16[128]{0:T(256)(128)(2,1)} %param.20) | copy-start | bytes 772
  7.2 86.9 %copy-start.3 = (bf16[2560,128]{1,0:T(8,128)(2,1)S(1)}, bf16[2560,128]{1,0:T(8,128)(2,1)}, u32[]{:S(2)}) copy-start(bf16[2560,128]{1,0:T(8,128)(2,1)} %param.22) | copy-start | bytes 1966084
  7.2 86.9 %all-gather.4.cloned.1.call-start = ((), (), s32[]{:S(2)}) async-start(), calls=%async_computation.4 | async-start | bytes 8355840 | tf_op jit(solution)/shard_map/all_gather | solution.py:33
  20.3 9.9 %collective-permute-start = (bf16[2560,64]{0,1:T(8,128)(2,1)}, bf16[2560,64]{0,1:T(8,128)(2,1)}, u32[]{:S(2)}, u32[]{:S(2)}) collective-permute-start(bf16[2560,64]{0,1:T(8,128)(2,1)} %param.23), channel_id=1, source_target_pairs={{0,1},{1,0},{2,3},{3,2},{4,5},{5,4},{6,7},{7,6},{8,9},{9,8},{10,11... | collective-permute-start | bytes 983048 | tf_op jit(solution)/shard_map/ppermute | solution.py:22
  31.5 68.8 %collective-permute-start.1 = (bf16[2560,128]{0,1:T(8,128)(2,1)S(1)}, bf16[2560,128]{0,1:T(8,128)(2,1)}, u32[]{:S(2)}, u32[]{:S(2)}) collective-permute-start(bf16[2560,128]{0,1:T(8,128)(2,1)S(1)} %maximum_select_fusion.2), channel_id=1, source_target_pairs={{0,2},{1,3},{2,0},{3,1},{4,6},{5,7},{6,4},{7,5},{8,10},{9,11},{10,... | collective-permute-start | bytes 1966088 | tf_op jit(solution)/shard_map/ppermute | solution.py:22
  94.2 6.1 %copy-start.1 = (bf16[1536,2560]{1,0:T(8,128)(2,1)S(1)}, bf16[1536,2560]{1,0:T(8,128)(2,1)}, u32[]{:S(2)}) copy-start(bf16[1536,2560]{1,0:T(8,128)(2,1)} %all-gather.4.cloned.1.call-done) | copy-start | bytes 23592964
  103.9 0.7 copy-start.7
  112.4 1.3 copy-start.4
  119.1 9.4 %copy-start.6 = (bf16[2560]{0:T(1024)(128)(2,1)S(1)}, bf16[2560]{0:T(1024)(128)(2,1)}, u32[]{:S(2)}) copy-start(bf16[2560]{0:T(1024)(128)(2,1)} %param.21) | copy-start | bytes 15364
  119.1 131.1 %all-to-all-start = ((bf16[32,48,2560]{2,1,0:T(8,128)(2,1)}), bf16[32,48,2560]{2,1,0:T(8,128)(2,1)}, u32[]{:S(2)}, u32[]{:S(2)}) async-start(bf16[32,48,2560]{2,1,0:T(8,128)(2,1)} %bitcast.124), calls=%async_computation | async-start | bytes 15728640 | tf_op jit(solution)/shard_map/all_to_all | solution.py:27
  128.4 202.3 %all-gather.6.cloned.1.call-start = ((), (), s32[]{:S(2)}) async-start(), calls=%async_computation.5 | async-start | bytes 8355840 | tf_op jit(solution)/shard_map/all_gather | solution.py:33
  128.5 126.2 %copy-start.2 = (bf16[48,2560]{1,0:T(8,128)(2,1)S(1)}, bf16[48,2560]{1,0:T(8,128)(2,1)}, u32[]{:S(2)}) copy-start(bf16[48,2560]{1,0:T(8,128)(2,1)} %param.14) | copy-start | bytes 737284
  254.7 8.6 %copy-start.12 = (s32[96]{0:T(128)S(1)}, s32[96]{0:T(128)}, u32[]{:S(2)}) copy-start(s32[96]{0:T(128)} %param.16) | copy-start | bytes 1156
  266.6 8.7 %all-to-all-start.1 = ((s32[4,1,24]{2,1,0:T(1,128)}), s32[4,1,24]{2,1,0:T(1,128)S(1)}, u32[]{:S(2)}, u32[]{:S(2)}) async-start(s32[4,1,24]{2,1,0:T(1,128)} %bitcast.30), calls=%async_computation.1 | async-start | bytes 4096 | tf_op jit(solution)/shard_map/all_to_all | solution.py:138
  278.6 8.5 %all-to-all-start.2 = ((bf16[4,2,12288]{2,1,0:T(2,128)(2,1)}), bf16[4,2,12288]{2,1,0:T(2,128)(2,1)S(1)}, u32[]{:S(2)}, u32[]{:S(2)}) async-start(bf16[4,2,12288]{2,1,0:T(2,128)(2,1)} %reshape.700), calls=%async_computation.2 | async-start | bytes 393216 | tf_op jit(solution)/shard_map/all_to_all | solution.py:137
  330.7 6.0 %copy-start.8 = (bf16[1536,2560]{1,0:T(8,128)(2,1)S(1)}, bf16[1536,2560]{1,0:T(8,128)(2,1)}, u32[]{:S(2)}) copy-start(bf16[1536,2560]{1,0:T(8,128)(2,1)} %all-gather.6.cloned.1.call-done) | copy-start | bytes 23592964
  330.7 6.4 %copy-start.9 = (bf16[2560,304]{0,1:T(8,128)(2,1)S(1)}, bf16[2560,304]{0,1:T(8,128)(2,1)}, u32[]{:S(2)}) copy-start(bf16[2560,304]{0,1:T(8,128)(2,1)} %param.26) | copy-start | bytes 4669444
  354.7 139.4 %all-to-all-start.3 = ((bf16[32,48,2688]{2,1,0:T(8,128)(2,1)}), bf16[32,48,2688]{2,1,0:T(8,128)(2,1)}, u32[]{:S(2)}, u32[]{:S(2)}) async-start(bf16[32,48,2688]{2,1,0:T(8,128)(2,1)} %pad_maximum_fusion), calls=%async_computation.3 | async-start | bytes 16515072 | tf_op jit(solution)/shard_map/all_to_all | solution.py:215
  364.9 141.6 %copy-start.13 = (s32[16]{0:T(128)S(1)}, s32[16]{0:T(128)}, u32[]{:S(2)}) copy-start(s32[16]{0:T(128)} %param.17) | copy-start | bytes 196
Sparse Core Ops, SparseCore 0:
  20.5 73.6 all-gather.3
  263.4 67.2 all-gather.5

commit v12 on v11

--- a/solution.py
+++ b/solution.py
@@ -187,8 +187,7 @@
     gate_rows = jnp.dot(portion, w_gate, preferred_element_type=jnp.float32)
     upward = jnp.dot(portion, w_up, preferred_element_type=jnp.float32)
     hidden = (jax.nn.silu(gate_rows) * upward).astype(jnp.bfloat16)
-    down = jnp.dot(hidden, w_down, preferred_element_type=jnp.float32).astype(jnp.bfloat16)
-    width = down.shape[1]
+    width = w_down.shape[1]
     feat = width // tensor_element_count
     nprompt = prompt_ends.shape[0]
     end_pick = ((prompt_ends - 1)[:, None] == all_ids[None, :]).astype(jnp.bfloat16)
@@ -205,12 +204,14 @@
     extra = jnp.concatenate([by_feature_block(end_down), by_feature_block(end_resid)], axis=1)
     extra_cols = 128
     extra = jnp.pad(extra, ((0, 0), (0, tok_dev * extra_cols - extra.shape[1])))
-    payload = jnp.concatenate(
-        [
-            down.reshape(tensor_element_count, tok_dev, width),
-            extra.reshape(tensor_element_count, tok_dev, extra_cols),
-        ],
-        axis=2,
+    wide_weight = jnp.concatenate(
+        [w_down, jnp.zeros((w_down.shape[0], extra_cols), w_down.dtype)], axis=1
+    )
+    down = jnp.dot(hidden, wide_weight, preferred_element_type=jnp.float32).astype(jnp.bfloat16)
+    payload = lax.dynamic_update_slice(
+        down.reshape(tensor_element_count, tok_dev, width + extra_cols),
+        extra.reshape(tensor_element_count, tok_dev, extra_cols),
+        (0, 0, width),
     )
     got = lax.all_to_all(payload, TENSOR, 0, 0, tiled=True)
     summed = jnp.sum(got.astype(jnp.float32), axis=0)

time: 515 us -> 509 us (0.988)
  other arithmetic: 30 us -> 23.1 us
    concatenate x1 -> x0, other arithmetic: 6.97 us -> none  [per_device(): jnp.concatenate([down.reshape(tensor_element_count, tok_dev, width), extr...]
where the time goes in v12:
time: 509 us; the launch traced here: 508 us
  waiting for transfers between devices  365 us (72%)
  matrix products  36.8 us (7%)
  starting transfers between devices  31.4 us (6%)
  blocking collectives  24.8 us (5%)
  other arithmetic  23.1 us (5%)
  between operations  14.6 us (3%)
  local copies, waits for them, and re-layouts  12.3 us (2%)
    all_to_all x1, waiting for transfers between devices, per_device(): got = lax.all_to_all(payload, TENSOR, 0, 0, tiled=True)  129 us
    all_to_all x1, waiting for transfers between devices, scatter_sum(): got = lax.all_to_all(pieces, TENSOR, 0, 0, tiled=True)  122 us
    all_gather x2, waiting for transfers between devices, gather_rows(): return lax.all_gather(rows, ('ty', 'tx'), axis=0, tiled=True)  102 us
    all_gather x2, blocking collectives, gather_rows(): rows = lax.all_gather(rows, 'tz', axis=0, tiled=True)  18.2 us
  transfers between devices with their start and end apart: 8, of which 7 were waited for; matrix products, arithmetic and copies ran while one was open for 4% of the time, Pallas kernels for 0%

profile of v12, /device:TPU:27, one launch (start us, length us, event | category | flops | bytes accessed | tf_op | source)
XLA Modules:
  0.0 508.1 jit_solution(734516222981073958)
XLA Ops:
  7.3 1.2 fusion.61
  9.2 1.1 fusion.63
  10.3 10.0 %all_gather.15 = bf16[96,2560]{1,0:T(8,128)(2,1)} all-gather(bf16[48,2560]{1,0:T(8,128)(2,1)S(1)} %fusion.63), channel_id=1, replica_groups=mesh['dp'=4,'ty'=4,'tx'=4,'tz'=2] {'tz'}, dimensions={0}, use_global_device_ids=true | all-gather | bytes 737280 | tf_op jit(solution)/shard_map/all_gather | solution.py:32
  20.3 2.8 collective-permute-start
  25.3 4.9 collective-permute-done
  30.3 1.2 maximum_select_fusion.2
  31.8 62.3 %all-gather.4.cloned.1.call-done = bf16[1536,2560]{1,0:T(8,128)(2,1)} async-done(((bf16[96,2560]{1,0:T(8,128)(2,1)}), bf16[1536,2560]{1,0:T(8,128)(2,1)}) %all-gather.4.cloned.1.call-update) | async-done | bytes 7864336 | tf_op jit(solution)/shard_map/all_gather | solution.py:33
  94.2 6.1 %multiply_reduce_fusion = (f32[1536]{0:T(1024)S(1)}, f32[1536,128]{0,1:T(8,128)S(1)}) fusion(bf16[1536,2560]{1,0:T(8,128)(2,1)} %all-gather.4.cloned.1.call-done, bf16[2560,128]{1,0:T(8,128)(2,1)S(1)} %copy-done.5), kind=kOutput, calls=%fused_computation.71 | convolution fusion | flops 1007024640 | bytes 9312256 | tf_op jit(solution)/shard_map/dot_general | solution.py:103
  100.3 3.6 convolution_convert_fusion.4
  104.6 1.7 fusion.74
  111.1 1.3 fusion.6
  112.4 1.3 fusion.31
  113.7 5.3 %convolution_convert_fusion.1 = bf16[1536,2560]{1,0:T(8,128)(2,1)} fusion(bf16[1536,128]{1,0:T(8,128)(2,1)S(1)} %bitcast.125, bf16[128,2560]{1,0:T(8,128)(2,1)S(1)} %copy-done.6), kind=kOutput, calls=%fused_computation.7 | convolution fusion | flops 1010565120 | bytes 8912896 | tf_op jit(solution)/shard_map/dot_general | solution.py:181
  119.1 9.3 %all-to-all-start = ((bf16[32,48,2560]{2,1,0:T(8,128)(2,1)}), bf16[32,48,2560]{2,1,0:T(8,128)(2,1)}, u32[]{:S(2)}, u32[]{:S(2)}) async-start(bf16[32,48,2560]{2,1,0:T(8,128)(2,1)} %bitcast.123), calls=%async_computation | async-start | bytes 15728640 | tf_op jit(solution)/shard_map/all_to_all | solution.py:27
  128.5 121.7 %all-to-all-done = bf16[32,48,2560]{2,1,0:T(8,128)(2,1)} async-done(((bf16[32,48,2560]{2,1,0:T(8,128)(2,1)}), bf16[32,48,2560]{2,1,0:T(8,128)(2,1)}, u32[]{:S(2)}, u32[]{:S(2)}) %all-to-all-start) | async-done | bytes 7864352 | tf_op jit(solution)/shard_map/all_to_all | solution.py:27
  250.2 4.5 convert_reduce_fusion.1
  255.1 8.2 %all_gather.17 = bf16[96,2560]{1,0:T(8,128)(2,1)} all-gather(bf16[48,2560]{1,0:T(8,128)(2,1)S(1)} %fusion.67), channel_id=1, replica_groups=mesh['dp'=4,'ty'=4,'tx'=4,'tz'=2] {'tz'}, dimensions={0}, use_global_device_ids=true | all-gather | bytes 737280 | tf_op jit(solution)/shard_map/all_gather | solution.py:32
  264.7 1.2 gather_fusion
  266.6 5.6 %all-to-all-start.1 = ((s32[4,1,24]{2,1,0:T(1,128)}), s32[4,1,24]{2,1,0:T(1,128)S(1)}, u32[]{:S(2)}, u32[]{:S(2)}) async-start(s32[4,1,24]{2,1,0:T(1,128)} %bitcast.30), calls=%async_computation.1 | async-start | bytes 4096 | tf_op jit(solution)/shard_map/all_to_all | solution.py:138
  272.2 3.0 all-to-all-done.1
  278.6 4.0 all-to-all-start.2
  282.6 4.5 all-to-all-done.2
  287.5 3.5 scatter_fusion
  291.4 39.4 %all-gather.6.cloned.1.call-done = bf16[1536,2560]{1,0:T(8,128)(2,1)} async-done(((bf16[96,2560]{1,0:T(8,128)(2,1)}), bf16[1536,2560]{1,0:T(8,128)(2,1)}) %all-gather.6.cloned.1.call-update) | async-done | bytes 7864336 | tf_op jit(solution)/shard_map/all_gather | solution.py:33
  330.8 5.6 %fusion.126 = f32[1536,304]{0,1:T(8,128)S(1)} fusion(bf16[1536,2560]{1,0:T(8,128)(2,1)} %all-gather.6.cloned.1.call-done, bf16[2560,304]{0,1:T(8,128)(2,1)S(1)} %copy-done), kind=kOutput, calls=%fused_computation.197 | convolution fusion | flops 2390753280 | bytes 11288576 | tf_op jit(solution)/shard_map/dot_general | solution.py:187
  336.8 2.7 fusion.2
  340.4 6.8 %convolution_convert_fusion = bf16[1536,2688]{1,0:T(8,128)(2,1)} fusion(bf16[1536,304]{0,1:T(8,128)(2,1)S(1)} %fusion.2, bf16[304,2560]{1,0:T(8,128)(2,1)S(1)} %copy-done.4), kind=kOutput, calls=%fused_computation.6 | convolution fusion | flops 2514419712 | bytes 10747904 | tf_op jit(solution)/shard_map/dot_general | solution.py:210
  348.4 9.2 %all-to-all-start.3 = ((bf16[32,48,2688]{2,1,0:T(8,128)(2,1)}), bf16[32,48,2688]{2,1,0:T(8,128)(2,1)}, u32[]{:S(2)}, u32[]{:S(2)}) async-start(bf16[32,48,2688]{2,1,0:T(8,128)(2,1)} %constant_dynamic-update-slice_fusion), calls=%async_computation.3 | async-start | bytes 16515072 | tf_op jit(solution)/shard_map/all_to_all | solution.py:216
  357.7 1.1 copy.30
  358.7 129.2 %all-to-all-done.3 = bf16[32,48,2688]{2,1,0:T(8,128)(2,1)} async-done(((bf16[32,48,2688]{2,1,0:T(8,128)(2,1)}), bf16[32,48,2688]{2,1,0:T(8,128)(2,1)}, u32[]{:S(2)}, u32[]{:S(2)}) %all-to-all-start.3) | async-done | bytes 8257568 | tf_op jit(solution)/shard_map/all_to_all | solution.py:216
  487.9 5.0 convert_reduce_fusion
  493.8 6.6 %all-gather = bf16[4,6,80]{2,1,0:T(8,128)(2,1)S(1)} all-gather(bf16[1,6,80]{2,1,0:T(8,128)(2,1)S(1)} %reshape.686), channel_id=1, replica_groups=mesh['dp'=4,'ty'=4,'tx'=4,'tz'=2] {'dp'}, dimensions={0}, use_global_device_ids=true | all-gather | bytes 4800 | tf_op jit(solution)/shard_map/all_gather | solution.py:226
  (110 shorter events, 19.5 us)
Async XLA Ops:
  7.2 323.7 %copy-start = (bf16[2560,304]{0,1:T(8,128)(2,1)S(1)}, bf16[2560,304]{0,1:T(8,128)(2,1)}, u32[]{:S(2)}) copy-start(bf16[2560,304]{0,1:T(8,128)(2,1)} %param.25) | copy-start | bytes 4669444
  7.2 23.1 %copy-start.7 = (bf16[2560,64]{0,1:T(8,128)(2,1)S(1)}, bf16[2560,64]{0,1:T(8,128)(2,1)}, u32[]{:S(2)}) copy-start(bf16[2560,64]{0,1:T(8,128)(2,1)} %param.23) | copy-start | bytes 983044
  7.2 17.4 %copy-start.13 = (s32[1,6]{1,0:T(1,128)S(1)}, s32[1,6]{1,0:T(1,128)}, u32[]{:S(2)}) copy-start(s32[1,6]{1,0:T(1,128)} %param.15) | copy-start | bytes 76
  7.2 17.4 %copy-start.12 = (bf16[128]{0:T(256)(128)(2,1)S(1)}, bf16[128]{0:T(256)(128)(2,1)}, u32[]{:S(2)}) copy-start(bf16[128]{0:T(256)(128)(2,1)} %param.20) | copy-start | bytes 772
  7.2 86.9 %copy-start.5 = (bf16[2560,128]{1,0:T(8,128)(2,1)S(1)}, bf16[2560,128]{1,0:T(8,128)(2,1)}, u32[]{:S(2)}) copy-start(bf16[2560,128]{1,0:T(8,128)(2,1)} %param.22) | copy-start | bytes 1966084
  7.2 86.9 %all-gather.4.cloned.1.call-start = ((), (), s32[]{:S(2)}) async-start(), calls=%async_computation.4 | async-start | bytes 8355840 | tf_op jit(solution)/shard_map/all_gather | solution.py:33
  20.3 9.9 %collective-permute-start = (bf16[2560,64]{0,1:T(8,128)(2,1)}, bf16[2560,64]{0,1:T(8,128)(2,1)}, u32[]{:S(2)}, u32[]{:S(2)}) collective-permute-start(bf16[2560,64]{0,1:T(8,128)(2,1)} %param.23), channel_id=1, source_target_pairs={{0,1},{1,0},{2,3},{3,2},{4,5},{5,4},{6,7},{7,6},{8,9},{9,8},{10,11... | collective-permute-start | bytes 983048 | tf_op jit(solution)/shard_map/ppermute | solution.py:22
  31.5 68.8 %collective-permute-start.1 = (bf16[2560,128]{0,1:T(8,128)(2,1)S(1)}, bf16[2560,128]{0,1:T(8,128)(2,1)}, u32[]{:S(2)}, u32[]{:S(2)}) collective-permute-start(bf16[2560,128]{0,1:T(8,128)(2,1)S(1)} %maximum_select_fusion.2), channel_id=1, source_target_pairs={{0,2},{1,3},{2,0},{3,1},{4,6},{5,7},{6,4},{7,5},{8,10},{9,11},{10,... | collective-permute-start | bytes 1966088 | tf_op jit(solution)/shard_map/ppermute | solution.py:22
  94.2 6.1 %copy-start.2 = (bf16[1536,2560]{1,0:T(8,128)(2,1)S(1)}, bf16[1536,2560]{1,0:T(8,128)(2,1)}, u32[]{:S(2)}) copy-start(bf16[1536,2560]{1,0:T(8,128)(2,1)} %all-gather.4.cloned.1.call-done) | copy-start | bytes 23592964
  103.9 0.7 copy-start.9
  112.4 1.3 copy-start.6
  119.1 9.4 %copy-start.8 = (bf16[2560]{0:T(1024)(128)(2,1)S(1)}, bf16[2560]{0:T(1024)(128)(2,1)}, u32[]{:S(2)}) copy-start(bf16[2560]{0:T(1024)(128)(2,1)} %param.21) | copy-start | bytes 15364
  119.1 131.1 %all-to-all-start = ((bf16[32,48,2560]{2,1,0:T(8,128)(2,1)}), bf16[32,48,2560]{2,1,0:T(8,128)(2,1)}, u32[]{:S(2)}, u32[]{:S(2)}) async-start(bf16[32,48,2560]{2,1,0:T(8,128)(2,1)} %bitcast.123), calls=%async_computation | async-start | bytes 15728640 | tf_op jit(solution)/shard_map/all_to_all | solution.py:27
  128.4 202.4 %all-gather.6.cloned.1.call-start = ((), (), s32[]{:S(2)}) async-start(), calls=%async_computation.5 | async-start | bytes 8355840 | tf_op jit(solution)/shard_map/all_gather | solution.py:33
  128.5 126.2 %copy-start.3 = (bf16[48,2560]{1,0:T(8,128)(2,1)S(1)}, bf16[48,2560]{1,0:T(8,128)(2,1)}, u32[]{:S(2)}) copy-start(bf16[48,2560]{1,0:T(8,128)(2,1)} %param.14) | copy-start | bytes 737284
  254.7 8.6 %copy-start.14 = (s32[96]{0:T(128)S(1)}, s32[96]{0:T(128)}, u32[]{:S(2)}) copy-start(s32[96]{0:T(128)} %param.16) | copy-start | bytes 1156
  266.6 8.7 %all-to-all-start.1 = ((s32[4,1,24]{2,1,0:T(1,128)}), s32[4,1,24]{2,1,0:T(1,128)S(1)}, u32[]{:S(2)}, u32[]{:S(2)}) async-start(s32[4,1,24]{2,1,0:T(1,128)} %bitcast.30), calls=%async_computation.1 | async-start | bytes 4096 | tf_op jit(solution)/shard_map/all_to_all | solution.py:138
  278.6 8.5 %all-to-all-start.2 = ((bf16[4,2,12288]{2,1,0:T(2,128)(2,1)}), bf16[4,2,12288]{2,1,0:T(2,128)(2,1)S(1)}, u32[]{:S(2)}, u32[]{:S(2)}) async-start(bf16[4,2,12288]{2,1,0:T(2,128)(2,1)} %reshape.700), calls=%async_computation.2 | async-start | bytes 393216 | tf_op jit(solution)/shard_map/all_to_all | solution.py:137
  330.8 5.6 %copy-start.10 = (bf16[1536,2560]{1,0:T(8,128)(2,1)S(1)}, bf16[1536,2560]{1,0:T(8,128)(2,1)}, u32[]{:S(2)}) copy-start(bf16[1536,2560]{1,0:T(8,128)(2,1)} %all-gather.6.cloned.1.call-done) | copy-start | bytes 23592964
  330.8 5.9 %copy-start.11 = (bf16[2560,304]{0,1:T(8,128)(2,1)S(1)}, bf16[2560,304]{0,1:T(8,128)(2,1)}, u32[]{:S(2)}) copy-start(bf16[2560,304]{0,1:T(8,128)(2,1)} %param.26) | copy-start | bytes 4669444
  336.8 2.7 copy-start.4
  348.4 139.5 %all-to-all-start.3 = ((bf16[32,48,2688]{2,1,0:T(8,128)(2,1)}), bf16[32,48,2688]{2,1,0:T(8,128)(2,1)}, u32[]{:S(2)}, u32[]{:S(2)}) async-start(bf16[32,48,2688]{2,1,0:T(8,128)(2,1)} %constant_dynamic-update-slice_fusion), calls=%async_computation.3 | async-start | bytes 16515072 | tf_op jit(solution)/shard_map/all_to_all | solution.py:216
  358.7 141.8 %copy-start.15 = (s32[16]{0:T(128)S(1)}, s32[16]{0:T(128)}, u32[]{:S(2)}) copy-start(s32[16]{0:T(128)} %param.17) | copy-start | bytes 196
  487.9 13.4 %copy-start.1 = (bf16[2560,304]{0,1:T(8,128)(2,1)S(1)}, bf16[2560,304]{0,1:T(8,128)(2,1)}, u32[]{:S(2)}) copy-start(bf16[2560,304]{0,1:T(8,128)(2,1)} %param.25) | copy-start | bytes 4669444
Sparse Core Ops, SparseCore 0:
  20.5 73.6 all-gather.3
  263.4 67.3 all-gather.5

commit v13 on v12

--- a/solution.py
+++ b/solution.py
@@ -29,7 +29,12 @@
 
 
 def gather_rows(rows):
-    rows = lax.all_gather(rows, "tz", axis=0, tiled=True)
+    partner = lax.ppermute(rows, "tz", [(0, 1), (1, 0)])
+    rows = jnp.where(
+        lax.axis_index("tz") == 0,
+        jnp.concatenate([rows, partner], axis=0),
+        jnp.concatenate([partner, rows], axis=0),
+    )
     return lax.all_gather(rows, ("ty", "tx"), axis=0, tiled=True)
 
 

time: 509 us -> 509 us (level)
  blocking collectives: 24.8 us -> 6.65 us
  waiting for transfers between devices: 365 us -> 380 us
    all_gather x2 -> x0, blocking collectives: 18.2 us -> none  [gather_rows(): rows = lax.all_gather(rows, 'tz', axis=0, tiled=True)]
    ppermute x0 -> x2, waiting for transfers between devices: none -> 13.1 us  [gather_rows(): partner = lax.ppermute(rows, 'tz', [(0, 1), (1, 0)])]
  transfers between devices with their start and end apart: 8 -> 10, of which waited for: 7 -> 9; matrix products, arithmetic and copies ran while one was open for 4% -> 4% of each run, Pallas kernels for 0% -> 0%
where the time goes in v13:
time: 509 us; the launch traced here: 508 us
  waiting for transfers between devices  380 us (75%)
  matrix products  36.9 us (7%)
  starting transfers between devices  35.2 us (7%)
  other arithmetic  23.2 us (5%)
  between operations  14.6 us (3%)
  local copies, waits for them, and re-layouts  12.3 us (2%)
  blocking collectives  6.65 us (1%)
    all_to_all x1, waiting for transfers between devices, per_device(): got = lax.all_to_all(payload, TENSOR, 0, 0, tiled=True)  129 us
    all_to_all x1, waiting for transfers between devices, scatter_sum(): got = lax.all_to_all(pieces, TENSOR, 0, 0, tiled=True)  122 us
    all_gather x2, waiting for transfers between devices, gather_rows(): return lax.all_gather(rows, ('ty', 'tx'), axis=0, tiled=True)  102 us
    ppermute x2, waiting for transfers between devices, gather_rows(): partner = lax.ppermute(rows, 'tz', [(0, 1), (1, 0)])  13.1 us
  transfers between devices with their start and end apart: 10, of which 9 were waited for; matrix products, arithmetic and copies ran while one was open for 4% of the time, Pallas kernels for 0%

profile of v13, /device:TPU:27, one launch (start us, length us, event | category | flops | bytes accessed | tf_op | source)
XLA Modules:
  0.0 508.4 jit_solution(9898905042612850273)
XLA Ops:
  7.3 1.2 fusion.61
  9.2 1.1 fusion.63
  10.3 3.7 collective-permute-start
  14.0 5.7 %collective-permute-done = bf16[48,2560]{1,0:T(8,128)(2,1)S(1)} collective-permute-done((bf16[48,2560]{1,0:T(8,128)(2,1)S(1)}, bf16[48,2560]{1,0:T(8,128)(2,1)S(1)}, u32[]{:S(2)}, u32[]{:S(2)}) %collective-permute-start) | collective-permute-done | bytes 245792 | tf_op jit(solution)/shard_map/ppermute | solution.py:32
  20.6 2.8 collective-permute-start.1
  23.8 6.5 %collective-permute-done.1 = bf16[2560,64]{0,1:T(8,128)(2,1)} collective-permute-done((bf16[2560,64]{0,1:T(8,128)(2,1)S(1)}, bf16[2560,64]{0,1:T(8,128)(2,1)}, u32[]{:S(2)}, u32[]{:S(2)}) %collective-permute-start.1) | collective-permute-done | bytes 327712 | tf_op jit(solution)/shard_map/ppermute | solution.py:22
  30.3 1.2 maximum_select_fusion.2
  31.8 62.6 %all-gather.4.cloned.1.call-done = bf16[1536,2560]{1,0:T(8,128)(2,1)} async-done(((bf16[96,2560]{1,0:T(8,128)(2,1)}), bf16[1536,2560]{1,0:T(8,128)(2,1)}) %all-gather.4.cloned.1.call-update) | async-done | bytes 7864336 | tf_op jit(solution)/shard_map/all_gather | solution.py:38
  94.4 6.1 %multiply_reduce_fusion = (f32[1536]{0:T(1024)S(1)}, f32[1536,128]{0,1:T(8,128)S(1)}) fusion(bf16[1536,2560]{1,0:T(8,128)(2,1)} %all-gather.4.cloned.1.call-done, bf16[2560,128]{1,0:T(8,128)(2,1)S(1)} %copy-done.5), kind=kOutput, calls=%fused_computation.71 | convolution fusion | flops 1007024640 | bytes 9312256 | tf_op jit(solution)/shard_map/dot_general | solution.py:108
  100.5 3.6 convolution_convert_fusion.4
  104.6 1.9 fusion.74
  111.3 1.3 fusion.6
  112.6 1.3 fusion.31
  113.9 5.4 %convolution_convert_fusion.1 = bf16[1536,2560]{1,0:T(8,128)(2,1)} fusion(bf16[1536,128]{1,0:T(8,128)(2,1)S(1)} %bitcast.125, bf16[128,2560]{1,0:T(8,128)(2,1)S(1)} %copy-done.6), kind=kOutput, calls=%fused_computation.7 | convolution fusion | flops 1010565120 | bytes 8912896 | tf_op jit(solution)/shard_map/dot_general | solution.py:186
  119.3 9.3 %all-to-all-start = ((bf16[32,48,2560]{2,1,0:T(8,128)(2,1)}), bf16[32,48,2560]{2,1,0:T(8,128)(2,1)}, u32[]{:S(2)}, u32[]{:S(2)}) async-start(bf16[32,48,2560]{2,1,0:T(8,128)(2,1)} %bitcast.123), calls=%async_computation | async-start | bytes 15728640 | tf_op jit(solution)/shard_map/all_to_all | solution.py:27
  128.7 121.7 %all-to-all-done = bf16[32,48,2560]{2,1,0:T(8,128)(2,1)} async-done(((bf16[32,48,2560]{2,1,0:T(8,128)(2,1)}), bf16[32,48,2560]{2,1,0:T(8,128)(2,1)}, u32[]{:S(2)}, u32[]{:S(2)}) %all-to-all-start) | async-done | bytes 7864352 | tf_op jit(solution)/shard_map/all_to_all | solution.py:27
  250.4 4.5 convert_reduce_fusion.1
  255.4 7.4 %collective-permute-done.3 = bf16[48,2560]{1,0:T(8,128)(2,1)S(1)} collective-permute-done((bf16[48,2560]{1,0:T(8,128)(2,1)S(1)}, bf16[48,2560]{1,0:T(8,128)(2,1)S(1)}, u32[]{:S(2)}, u32[]{:S(2)}) %collective-permute-start.3) | collective-permute-done | bytes 245792 | tf_op jit(solution)/shard_map/ppermute | solution.py:32
  265.1 1.4 gather_fusion
  267.2 5.6 %all-to-all-start.1 = ((s32[4,1,24]{2,1,0:T(1,128)}), s32[4,1,24]{2,1,0:T(1,128)S(1)}, u32[]{:S(2)}, u32[]{:S(2)}) async-start(s32[4,1,24]{2,1,0:T(1,128)} %bitcast.30), calls=%async_computation.1 | async-start | bytes 4096 | tf_op jit(solution)/shard_map/all_to_all | solution.py:143
  272.8 3.0 all-to-all-done.1
  279.2 4.0 all-to-all-start.2
  283.3 4.5 all-to-all-done.2
  288.1 3.5 scatter_fusion
  292.1 39.1 %all-gather.6.cloned.1.call-done = bf16[1536,2560]{1,0:T(8,128)(2,1)} async-done(((bf16[96,2560]{1,0:T(8,128)(2,1)}), bf16[1536,2560]{1,0:T(8,128)(2,1)}) %all-gather.6.cloned.1.call-update) | async-done | bytes 7864336 | tf_op jit(solution)/shard_map/all_gather | solution.py:38
  331.1 5.6 %fusion.126 = f32[1536,304]{0,1:T(8,128)S(1)} fusion(bf16[1536,2560]{1,0:T(8,128)(2,1)} %all-gather.6.cloned.1.call-done, bf16[2560,304]{0,1:T(8,128)(2,1)S(1)} %copy-done), kind=kOutput, calls=%fused_computation.199 | convolution fusion | flops 2390753280 | bytes 11288576 | tf_op jit(solution)/shard_map/dot_general | solution.py:192
  337.1 2.7 fusion.2
  340.7 6.8 %convolution_convert_fusion = bf16[1536,2688]{1,0:T(8,128)(2,1)} fusion(bf16[1536,304]{0,1:T(8,128)(2,1)S(1)} %fusion.2, bf16[304,2560]{1,0:T(8,128)(2,1)S(1)} %copy-done.4), kind=kOutput, calls=%fused_computation.6 | convolution fusion | flops 2514419712 | bytes 10747904 | tf_op jit(solution)/shard_map/dot_general | solution.py:215
  348.8 9.2 %all-to-all-start.3 = ((bf16[32,48,2688]{2,1,0:T(8,128)(2,1)}), bf16[32,48,2688]{2,1,0:T(8,128)(2,1)}, u32[]{:S(2)}, u32[]{:S(2)}) async-start(bf16[32,48,2688]{2,1,0:T(8,128)(2,1)} %constant_dynamic-update-slice_fusion), calls=%async_computation.3 | async-start | bytes 16515072 | tf_op jit(solution)/shard_map/all_to_all | solution.py:221
  359.0 129.2 %all-to-all-done.3 = bf16[32,48,2688]{2,1,0:T(8,128)(2,1)} async-done(((bf16[32,48,2688]{2,1,0:T(8,128)(2,1)}), bf16[32,48,2688]{2,1,0:T(8,128)(2,1)}, u32[]{:S(2)}, u32[]{:S(2)}) %all-to-all-start.3) | async-done | bytes 8257568 | tf_op jit(solution)/shard_map/all_to_all | solution.py:221
  488.2 5.0 convert_reduce_fusion
  494.1 6.6 %all-gather = bf16[4,6,80]{2,1,0:T(8,128)(2,1)S(1)} all-gather(bf16[1,6,80]{2,1,0:T(8,128)(2,1)S(1)} %reshape.686), channel_id=1, replica_groups=mesh['dp'=4,'ty'=4,'tx'=4,'tz'=2] {'dp'}, dimensions={0}, use_global_device_ids=true | all-gather | bytes 4800 | tf_op jit(solution)/shard_map/all_gather | solution.py:231
  (114 shorter events, 20.3 us)
Async XLA Ops:
  7.2 324.0 %copy-start = (bf16[2560,304]{0,1:T(8,128)(2,1)S(1)}, bf16[2560,304]{0,1:T(8,128)(2,1)}, u32[]{:S(2)}) copy-start(bf16[2560,304]{0,1:T(8,128)(2,1)} %param.25) | copy-start | bytes 4669444
  7.2 13.4 %copy-start.7 = (bf16[2560,64]{0,1:T(8,128)(2,1)S(1)}, bf16[2560,64]{0,1:T(8,128)(2,1)}, u32[]{:S(2)}) copy-start(bf16[2560,64]{0,1:T(8,128)(2,1)} %param.23) | copy-start | bytes 983044
  7.2 16.2 %copy-start.13 = (s32[1,6]{1,0:T(1,128)S(1)}, s32[1,6]{1,0:T(1,128)}, u32[]{:S(2)}) copy-start(s32[1,6]{1,0:T(1,128)} %param.15) | copy-start | bytes 76
  7.2 16.3 %copy-start.11 = (bf16[128]{0:T(256)(128)(2,1)S(1)}, bf16[128]{0:T(256)(128)(2,1)}, u32[]{:S(2)}) copy-start(bf16[128]{0:T(256)(128)(2,1)} %param.19) | copy-start | bytes 772
  7.2 16.3 %copy-start.12 = (bf16[128]{0:T(256)(128)(2,1)S(1)}, bf16[128]{0:T(256)(128)(2,1)}, u32[]{:S(2)}) copy-start(bf16[128]{0:T(256)(128)(2,1)} %param.20) | copy-start | bytes 772
  7.2 87.2 %copy-start.5 = (bf16[2560,128]{1,0:T(8,128)(2,1)S(1)}, bf16[2560,128]{1,0:T(8,128)(2,1)}, u32[]{:S(2)}) copy-start(bf16[2560,128]{1,0:T(8,128)(2,1)} %param.22) | copy-start | bytes 1966084
  7.2 87.2 %all-gather.4.cloned.1.call-start = ((), (), s32[]{:S(2)}) async-start(), calls=%async_computation.4 | async-start | bytes 8355840 | tf_op jit(solution)/shard_map/all_gather | solution.py:38
  10.3 9.3 %collective-permute-start = (bf16[48,2560]{1,0:T(8,128)(2,1)S(1)}, bf16[48,2560]{1,0:T(8,128)(2,1)S(1)}, u32[]{:S(2)}, u32[]{:S(2)}) collective-permute-start(bf16[48,2560]{1,0:T(8,128)(2,1)S(1)} %fusion.63), channel_id=1, source_target_pairs={{0,1},{1,0},{2,3},{3,2},{4,5},{5,4},{6,7},{7,6},{8,9},{9,8},{10,11... | collective-permute-start | bytes 737288 | tf_op jit(solution)/shard_map/ppermute | solution.py:32
  20.6 9.7 %collective-permute-start.1 = (bf16[2560,64]{0,1:T(8,128)(2,1)S(1)}, bf16[2560,64]{0,1:T(8,128)(2,1)}, u32[]{:S(2)}, u32[]{:S(2)}) collective-permute-start(bf16[2560,64]{0,1:T(8,128)(2,1)S(1)} %copy-done.7), channel_id=1, source_target_pairs={{0,1},{1,0},{2,3},{3,2},{4,5},{5,4},{6,7},{7,6},{8,9},{9,8},{10,11... | collective-permute-start | bytes 983048 | tf_op jit(solution)/shard_map/ppermute | solution.py:22
  31.5 69.0 %collective-permute-start.2 = (bf16[2560,128]{0,1:T(8,128)(2,1)S(1)}, bf16[2560,128]{0,1:T(8,128)(2,1)}, u32[]{:S(2)}, u32[]{:S(2)}) collective-permute-start(bf16[2560,128]{0,1:T(8,128)(2,1)S(1)} %maximum_select_fusion.2), channel_id=1, source_target_pairs={{0,2},{1,3},{2,0},{3,1},{4,6},{5,7},{6,4},{7,5},{8,10},{9,11},{10,... | collective-permute-start | bytes 1966088 | tf_op jit(solution)/shard_map/ppermute | solution.py:22
  94.4 6.1 %copy-start.2 = (bf16[1536,2560]{1,0:T(8,128)(2,1)S(1)}, bf16[1536,2560]{1,0:T(8,128)(2,1)}, u32[]{:S(2)}) copy-start(bf16[1536,2560]{1,0:T(8,128)(2,1)} %all-gather.4.cloned.1.call-done) | copy-start | bytes 23592964
  112.6 1.3 copy-start.6
  119.3 9.4 %copy-start.8 = (bf16[2560]{0:T(1024)(128)(2,1)S(1)}, bf16[2560]{0:T(1024)(128)(2,1)}, u32[]{:S(2)}) copy-start(bf16[2560]{0:T(1024)(128)(2,1)} %param.21) | copy-start | bytes 15364
  119.3 131.1 %all-to-all-start = ((bf16[32,48,2560]{2,1,0:T(8,128)(2,1)}), bf16[32,48,2560]{2,1,0:T(8,128)(2,1)}, u32[]{:S(2)}, u32[]{:S(2)}) async-start(bf16[32,48,2560]{2,1,0:T(8,128)(2,1)} %bitcast.123), calls=%async_computation | async-start | bytes 15728640 | tf_op jit(solution)/shard_map/all_to_all | solution.py:27
  128.6 202.5 %all-gather.6.cloned.1.call-start = ((), (), s32[]{:S(2)}) async-start(), calls=%async_computation.5 | async-start | bytes 8355840 | tf_op jit(solution)/shard_map/all_gather | solution.py:38
  128.7 126.2 %copy-start.3 = (bf16[48,2560]{1,0:T(8,128)(2,1)S(1)}, bf16[48,2560]{1,0:T(8,128)(2,1)}, u32[]{:S(2)}) copy-start(bf16[48,2560]{1,0:T(8,128)(2,1)} %param.14) | copy-start | bytes 737284
  255.0 8.8 %copy-start.14 = (s32[96]{0:T(128)S(1)}, s32[96]{0:T(128)}, u32[]{:S(2)}) copy-start(s32[96]{0:T(128)} %param.16) | copy-start | bytes 1156
  255.3 7.5 %collective-permute-start.3 = (bf16[48,2560]{1,0:T(8,128)(2,1)S(1)}, bf16[48,2560]{1,0:T(8,128)(2,1)S(1)}, u32[]{:S(2)}, u32[]{:S(2)}) collective-permute-start(bf16[48,2560]{1,0:T(8,128)(2,1)S(1)} %fusion.67), channel_id=1, source_target_pairs={{0,1},{1,0},{2,3},{3,2},{4,5},{5,4},{6,7},{7,6},{8,9},{9,8},{10,11... | collective-permute-start | bytes 737288 | tf_op jit(solution)/shard_map/ppermute | solution.py:32
  267.2 8.7 %all-to-all-start.1 = ((s32[4,1,24]{2,1,0:T(1,128)}), s32[4,1,24]{2,1,0:T(1,128)S(1)}, u32[]{:S(2)}, u32[]{:S(2)}) async-start(s32[4,1,24]{2,1,0:T(1,128)} %bitcast.30), calls=%async_computation.1 | async-start | bytes 4096 | tf_op jit(solution)/shard_map/all_to_all | solution.py:143
  279.2 8.5 %all-to-all-start.2 = ((bf16[4,2,12288]{2,1,0:T(2,128)(2,1)}), bf16[4,2,12288]{2,1,0:T(2,128)(2,1)S(1)}, u32[]{:S(2)}, u32[]{:S(2)}) async-start(bf16[4,2,12288]{2,1,0:T(2,128)(2,1)} %reshape.700), calls=%async_computation.2 | async-start | bytes 393216 | tf_op jit(solution)/shard_map/all_to_all | solution.py:142
  331.1 5.6 %copy-start.9 = (bf16[1536,2560]{1,0:T(8,128)(2,1)S(1)}, bf16[1536,2560]{1,0:T(8,128)(2,1)}, u32[]{:S(2)}) copy-start(bf16[1536,2560]{1,0:T(8,128)(2,1)} %all-gather.6.cloned.1.call-done) | copy-start | bytes 23592964
  331.1 5.9 %copy-start.10 = (bf16[2560,304]{0,1:T(8,128)(2,1)S(1)}, bf16[2560,304]{0,1:T(8,128)(2,1)}, u32[]{:S(2)}) copy-start(bf16[2560,304]{0,1:T(8,128)(2,1)} %param.26) | copy-start | bytes 4669444
  337.1 2.7 copy-start.4
  348.8 139.5 %all-to-all-start.3 = ((bf16[32,48,2688]{2,1,0:T(8,128)(2,1)}), bf16[32,48,2688]{2,1,0:T(8,128)(2,1)}, u32[]{:S(2)}, u32[]{:S(2)}) async-start(bf16[32,48,2688]{2,1,0:T(8,128)(2,1)} %constant_dynamic-update-slice_fusion), calls=%async_computation.3 | async-start | bytes 16515072 | tf_op jit(solution)/shard_map/all_to_all | solution.py:221
  359.0 141.8 %copy-start.15 = (s32[16]{0:T(128)S(1)}, s32[16]{0:T(128)}, u32[]{:S(2)}) copy-start(s32[16]{0:T(128)} %param.17) | copy-start | bytes 196
  488.2 13.4 %copy-start.1 = (bf16[2560,304]{0,1:T(8,128)(2,1)S(1)}, bf16[2560,304]{0,1:T(8,128)(2,1)}, u32[]{:S(2)}) copy-start(bf16[2560,304]{0,1:T(8,128)(2,1)} %param.25) | copy-start | bytes 4669444
Sparse Core Ops, SparseCore 0:
  20.7 73.6 all-gather.3
  263.8 67.2 all-gather.5

commit v14 on v12

--- a/solution.py
+++ b/solution.py
@@ -98,12 +98,10 @@
             jnp.concatenate([partner, head_weight], axis=1),
             jnp.concatenate([head_weight, partner], axis=1),
         )
-    joined = jnp.concatenate(
-        [
-            jnp.dot(portion, w_query, preferred_element_type=jnp.float32),
-            jnp.dot(portion, head_weight, preferred_element_type=jnp.float32),
-        ],
-        axis=1,
+    joined = jnp.dot(
+        portion,
+        jnp.concatenate([w_query, head_weight], axis=1),
+        preferred_element_type=jnp.float32,
     )
     queries = joined[:, :query_cols].reshape(token_count, heads_dev, HEAD_SIZE)
     kv_part = joined[:, query_cols:].astype(jnp.bfloat16)

time: 509 us -> 505 us (level)
    all_gather x2, waiting for transfers between devices: 102 us -> 79.8 us  [gather_rows(): return lax.all_gather(rows, ('ty', 'tx'), axis=0, tiled=True)]
    ppermute x2, waiting for transfers between devices: 4.94 us -> 23.2 us  [partner_2(): return lax.ppermute(value, axis, pairs)]
  transfers between devices with their start and end apart: 8 -> 8, of which waited for: 7 -> 8; matrix products, arithmetic and copies ran while one was open for 4% -> 4% of each run, Pallas kernels for 0% -> 0%
where the time goes in v14:
time: 505 us
  waiting for transfers between devices  361 us (71%)
  matrix products  32.7 us (6%)
  starting transfers between devices  31.6 us (6%)
  other arithmetic  25.7 us (5%)
  blocking collectives  24.8 us (5%)
  between operations  14.7 us (3%)
  local copies, waits for them, and re-layouts  14.2 us (3%)
    all_to_all x1, waiting for transfers between devices, per_device(): got = lax.all_to_all(payload, TENSOR, 0, 0, tiled=True)  129 us
    all_to_all x1, waiting for transfers between devices, scatter_sum(): got = lax.all_to_all(pieces, TENSOR, 0, 0, tiled=True)  122 us
    all_gather x2, waiting for transfers between devices, gather_rows(): return lax.all_gather(rows, ('ty', 'tx'), axis=0, tiled=True)  79.8 us
    ppermute x2, waiting for transfers between devices, partner_2(): return lax.ppermute(value, axis, pairs)  23.2 us
    all_gather x2, blocking collectives, gather_rows(): rows = lax.all_gather(rows, 'tz', axis=0, tiled=True)  18.2 us
  transfers between devices with their start and end apart: 8, of which 8 were waited for; matrix products, arithmetic and copies ran while one was open for 4% of the time, Pallas kernels for 0%

profile of v14, /device:TPU:27, one launch (start us, length us, event | category | flops | bytes accessed | tf_op | source)
XLA Modules:
  0.0 504.6 jit_solution(11761504074912077139)
XLA Ops:
  7.3 1.2 fusion.59
  9.2 1.1 fusion.61
  10.3 10.0 %all_gather.15 = bf16[96,2560]{1,0:T(8,128)(2,1)} all-gather(bf16[48,2560]{1,0:T(8,128)(2,1)S(1)} %fusion.61), channel_id=1, replica_groups=mesh['dp'=4,'ty'=4,'tx'=4,'tz'=2] {'tz'}, dimensions={0}, use_global_device_ids=true | all-gather | bytes 737280 | tf_op jit(solution)/shard_map/all_gather | solution.py:32
  20.3 2.8 collective-permute-start
  23.9 1.2 convert_element_type.136
  27.8 2.4 collective-permute-done
  32.3 20.8 %collective-permute-done.1 = bf16[2560,128]{0,1:T(8,128)(2,1)S(1)} collective-permute-done((bf16[2560,128]{0,1:T(8,128)(2,1)S(1)}, bf16[2560,128]{0,1:T(8,128)(2,1)S(1)}, u32[]{:S(2)}, u32[]{:S(2)}) %collective-permute-start.1) | collective-permute-done | bytes 655392 | tf_op jit(solution)/shard_map/ppermute | solution.py:22
  53.4 41.0 %all-gather.4.cloned.1.call-done = bf16[1536,2560]{1,0:T(8,128)(2,1)} async-done(((bf16[96,2560]{1,0:T(8,128)(2,1)}), bf16[1536,2560]{1,0:T(8,128)(2,1)}) %all-gather.4.cloned.1.call-update) | async-done | bytes 7864336 | tf_op jit(solution)/shard_map/all_gather | solution.py:33
  94.4 5.6 %fusion.124 = (bf16[1536,384]{0,1:T(8,128)(2,1)S(1)}, f32[1536,384]{0,1:T(8,128)S(1)}) fusion(bf16[1536,2560]{1,0:T(8,128)(2,1)} %all-gather.4.cloned.1.call-done, bf16[2560,256]{0,1:T(8,128)(2,1)S(1)} %maximum_select_fusion, bf16[2560,128]{0,1:T(8,128)(2,1)S(1)} %copy.29), kind=kOutput, calls=%fused_computation.194 | convolution fusion | flops 3024420864 | bytes 13369344 | tf_op jit(solution)/shard_map/dot_general | solution.py:101
  100.8 1.7 fusion.72
  107.4 1.3 fusion.6
  108.7 1.3 fusion.29
  110.1 5.4 %convolution_convert_fusion.1 = bf16[1536,2560]{1,0:T(8,128)(2,1)} fusion(bf16[1536,128]{1,0:T(8,128)(2,1)S(1)} %bitcast.123, bf16[128,2560]{1,0:T(8,128)(2,1)S(1)} %copy-done.5), kind=kOutput, calls=%fused_computation.7 | convolution fusion | flops 1010565120 | bytes 8912896 | tf_op jit(solution)/shard_map/dot_general | solution.py:179
  115.4 9.3 %all-to-all-start = ((bf16[32,48,2560]{2,1,0:T(8,128)(2,1)}), bf16[32,48,2560]{2,1,0:T(8,128)(2,1)}, u32[]{:S(2)}, u32[]{:S(2)}) async-start(bf16[32,48,2560]{2,1,0:T(8,128)(2,1)} %bitcast.121), calls=%async_computation | async-start | bytes 15728640 | tf_op jit(solution)/shard_map/all_to_all | solution.py:27
  125.0 121.7 %all-to-all-done = bf16[32,48,2560]{2,1,0:T(8,128)(2,1)} async-done(((bf16[32,48,2560]{2,1,0:T(8,128)(2,1)}), bf16[32,48,2560]{2,1,0:T(8,128)(2,1)}, u32[]{:S(2)}, u32[]{:S(2)}) %all-to-all-start) | async-done | bytes 7864352 | tf_op jit(solution)/shard_map/all_to_all | solution.py:27
  246.7 4.5 convert_reduce_fusion.1
  251.6 8.2 %all_gather.17 = bf16[96,2560]{1,0:T(8,128)(2,1)} all-gather(bf16[48,2560]{1,0:T(8,128)(2,1)S(1)} %fusion.65), channel_id=1, replica_groups=mesh['dp'=4,'ty'=4,'tx'=4,'tz'=2] {'tz'}, dimensions={0}, use_global_device_ids=true | all-gather | bytes 737280 | tf_op jit(solution)/shard_map/all_gather | solution.py:32
  261.2 1.2 gather_fusion
  263.0 5.6 %all-to-all-start.1 = ((s32[4,1,24]{2,1,0:T(1,128)}), s32[4,1,24]{2,1,0:T(1,128)S(1)}, u32[]{:S(2)}, u32[]{:S(2)}) async-start(s32[4,1,24]{2,1,0:T(1,128)} %bitcast.30), calls=%async_computation.1 | async-start | bytes 4096 | tf_op jit(solution)/shard_map/all_to_all | solution.py:136
  268.7 3.0 all-to-all-done.1
  276.1 4.0 all-to-all-start.2
  280.1 4.1 all-to-all-done.2
  284.6 3.5 scatter_fusion
  288.6 38.8 %all-gather.6.cloned.1.call-done = bf16[1536,2560]{1,0:T(8,128)(2,1)} async-done(((bf16[96,2560]{1,0:T(8,128)(2,1)}), bf16[1536,2560]{1,0:T(8,128)(2,1)}) %all-gather.6.cloned.1.call-update) | async-done | bytes 7864336 | tf_op jit(solution)/shard_map/all_gather | solution.py:33
  327.4 5.6 %fusion.125 = f32[1536,304]{0,1:T(8,128)S(1)} fusion(bf16[1536,2560]{1,0:T(8,128)(2,1)} %all-gather.6.cloned.1.call-done, bf16[2560,304]{0,1:T(8,128)(2,1)S(1)} %copy-done), kind=kOutput, calls=%fused_computation.195 | convolution fusion | flops 2390753280 | bytes 11288576 | tf_op jit(solution)/shard_map/dot_general | solution.py:185
  333.3 2.7 fusion.2
  336.9 6.8 %convolution_convert_fusion = bf16[1536,2688]{1,0:T(8,128)(2,1)} fusion(bf16[1536,304]{0,1:T(8,128)(2,1)S(1)} %fusion.2, bf16[304,2560]{1,0:T(8,128)(2,1)S(1)} %copy-done.3), kind=kOutput, calls=%fused_computation.6 | convolution fusion | flops 2514419712 | bytes 10747904 | tf_op jit(solution)/shard_map/dot_general | solution.py:208
  345.0 9.2 %all-to-all-start.3 = ((bf16[32,48,2688]{2,1,0:T(8,128)(2,1)}), bf16[32,48,2688]{2,1,0:T(8,128)(2,1)}, u32[]{:S(2)}, u32[]{:S(2)}) async-start(bf16[32,48,2688]{2,1,0:T(8,128)(2,1)} %constant_dynamic-update-slice_fusion), calls=%async_computation.3 | async-start | bytes 16515072 | tf_op jit(solution)/shard_map/all_to_all | solution.py:214
  354.2 1.1 copy.34
  355.2 129.2 %all-to-all-done.3 = bf16[32,48,2688]{2,1,0:T(8,128)(2,1)} async-done(((bf16[32,48,2688]{2,1,0:T(8,128)(2,1)}), bf16[32,48,2688]{2,1,0:T(8,128)(2,1)}, u32[]{:S(2)}, u32[]{:S(2)}) %all-to-all-start.3) | async-done | bytes 8257568 | tf_op jit(solution)/shard_map/all_to_all | solution.py:214
  484.4 5.0 convert_reduce_fusion
  490.3 6.6 %all-gather = bf16[4,6,80]{2,1,0:T(8,128)(2,1)S(1)} all-gather(bf16[1,6,80]{2,1,0:T(8,128)(2,1)S(1)} %reshape.686), channel_id=1, replica_groups=mesh['dp'=4,'ty'=4,'tx'=4,'tz'=2] {'dp'}, dimensions={0}, use_global_device_ids=true | all-gather | bytes 4800 | tf_op jit(solution)/shard_map/all_gather | solution.py:224
  (131 shorter events, 24.1 us)
Async XLA Ops:
  7.2 320.2 %copy-start = (bf16[2560,304]{0,1:T(8,128)(2,1)S(1)}, bf16[2560,304]{0,1:T(8,128)(2,1)}, u32[]{:S(2)}) copy-start(bf16[2560,304]{0,1:T(8,128)(2,1)} %param.25) | copy-start | bytes 4669444
  7.2 23.0 %copy-start.7 = (bf16[2560,64]{0,1:T(8,128)(2,1)S(1)}, bf16[2560,64]{0,1:T(8,128)(2,1)}, u32[]{:S(2)}) copy-start(bf16[2560,64]{0,1:T(8,128)(2,1)} %param.23) | copy-start | bytes 983044
  7.2 18.5 %copy-start.23 = (s32[1,6]{1,0:T(1,128)S(1)}, s32[1,6]{1,0:T(1,128)}, u32[]{:S(2)}) copy-start(s32[1,6]{1,0:T(1,128)} %param.15) | copy-start | bytes 76
  7.2 17.9 %copy-start.22 = (bf16[128]{0:T(256)(128)(2,1)S(1)}, bf16[128]{0:T(256)(128)(2,1)}, u32[]{:S(2)}) copy-start(bf16[128]{0:T(256)(128)(2,1)} %param.20) | copy-start | bytes 772
  7.2 18.6 %copy-start.6 = (bf16[2560,128]{1,0:T(8,128)(2,1)S(1)}, bf16[2560,128]{1,0:T(8,128)(2,1)}, u32[]{:S(2)}) copy-start(bf16[2560,128]{1,0:T(8,128)(2,1)} %param.22) | copy-start | bytes 1966084
  7.2 87.2 %all-gather.4.cloned.1.call-start = ((), (), s32[]{:S(2)}) async-start(), calls=%async_computation.4 | async-start | bytes 8355840 | tf_op jit(solution)/shard_map/all_gather | solution.py:33
  20.3 9.8 %collective-permute-start = (bf16[2560,64]{0,1:T(8,128)(2,1)}, bf16[2560,64]{0,1:T(8,128)(2,1)S(1)}, u32[]{:S(2)}, u32[]{:S(2)}) collective-permute-start(bf16[2560,64]{0,1:T(8,128)(2,1)} %param.23), channel_id=1, source_target_pairs={{0,1},{1,0},{2,3},{3,2},{4,5},{5,4},{6,7},{7,6},{8,9},{9,8},{10,11... | collective-permute-start | bytes 983048 | tf_op jit(solution)/shard_map/ppermute | solution.py:22
  23.9 1.8 copy-start.17
  30.3 22.9 %collective-permute-start.1 = (bf16[2560,128]{0,1:T(8,128)(2,1)S(1)}, bf16[2560,128]{0,1:T(8,128)(2,1)S(1)}, u32[]{:S(2)}, u32[]{:S(2)}) collective-permute-start(bf16[2560,128]{0,1:T(8,128)(2,1)S(1)} %maximum_select_fusion.1), channel_id=1, source_target_pairs={{0,2},{1,3},{2,0},{3,1},{4,6},{5,7},{6,4},{7,5},{8,10},{9,11},{10,... | collective-permute-start | bytes 1966088 | tf_op jit(solution)/shard_map/ppermute | solution.py:22
  53.4 46.8 %copy-start.16 = (f32[128]{0:T(128)S(1)}, f32[128]{0:T(128)}, u32[]{:S(2)}) copy-start(f32[128]{0:T(128)} %convert_element_type.136) | copy-start | bytes 1540
  100.0 8.7 %copy-start.4 = (bf16[1536,384]{0,1:T(8,128)(2,1)}, bf16[1536,384]{0,1:T(8,128)(2,1)S(1)}, u32[]{:S(2)}) copy-start(bf16[1536,384]{0,1:T(8,128)(2,1)S(1)} %get-tuple-element.31) | copy-start | bytes 3538948
  100.6 1.9 copy-start.10
  103.0 1.0 copy-start.8
  103.0 1.0 copy-start.12
  103.0 1.0 copy-start.13
  105.5 1.0 copy-start.9
  105.5 0.9 copy-start.11
  108.7 1.3 copy-start.5
  115.4 9.6 %copy-start.14 = (bf16[2560]{0:T(1024)(128)(2,1)S(1)}, bf16[2560]{0:T(1024)(128)(2,1)}, u32[]{:S(2)}) copy-start(bf16[2560]{0:T(1024)(128)(2,1)} %param.21) | copy-start | bytes 15364
  115.4 131.2 %all-to-all-start = ((bf16[32,48,2560]{2,1,0:T(8,128)(2,1)}), bf16[32,48,2560]{2,1,0:T(8,128)(2,1)}, u32[]{:S(2)}, u32[]{:S(2)}) async-start(bf16[32,48,2560]{2,1,0:T(8,128)(2,1)} %bitcast.121), calls=%async_computation | async-start | bytes 15728640 | tf_op jit(solution)/shard_map/all_to_all | solution.py:27
  124.8 202.6 %all-gather.6.cloned.1.call-start = ((), (), s32[]{:S(2)}) async-start(), calls=%async_computation.5 | async-start | bytes 8355840 | tf_op jit(solution)/shard_map/all_gather | solution.py:33
  125.0 126.2 %copy-start.2 = (bf16[48,2560]{1,0:T(8,128)(2,1)S(1)}, bf16[48,2560]{1,0:T(8,128)(2,1)}, u32[]{:S(2)}) copy-start(bf16[48,2560]{1,0:T(8,128)(2,1)} %param.14) | copy-start | bytes 737284
  251.2 8.6 %copy-start.24 = (s32[96]{0:T(128)S(1)}, s32[96]{0:T(128)}, u32[]{:S(2)}) copy-start(s32[96]{0:T(128)} %param.16) | copy-start | bytes 1156
  251.2 17.5 %copy-start.18 = (s32[6,1]{0,1:T(1,128)S(1)}, s32[6,1]{0,1:T(1,128)}, u32[]{:S(2)}) copy-start(s32[6,1]{0,1:T(1,128)} %copy-done.17) | copy-start | bytes 76
  263.0 8.7 %all-to-all-start.1 = ((s32[4,1,24]{2,1,0:T(1,128)}), s32[4,1,24]{2,1,0:T(1,128)S(1)}, u32[]{:S(2)}, u32[]{:S(2)}) async-start(s32[4,1,24]{2,1,0:T(1,128)} %bitcast.30), calls=%async_computation.1 | async-start | bytes 4096 | tf_op jit(solution)/shard_map/all_to_all | solution.py:136
  276.1 8.2 %all-to-all-start.2 = ((bf16[4,2,12288]{2,1,0:T(2,128)(2,1)}), bf16[4,2,12288]{2,1,0:T(2,128)(2,1)S(1)}, u32[]{:S(2)}, u32[]{:S(2)}) async-start(bf16[4,2,12288]{2,1,0:T(2,128)(2,1)} %reshape.700), calls=%async_computation.2 | async-start | bytes 393216 | tf_op jit(solution)/shard_map/all_to_all | solution.py:135
  327.4 5.6 %copy-start.20 = (bf16[1536,2560]{1,0:T(8,128)(2,1)S(1)}, bf16[1536,2560]{1,0:T(8,128)(2,1)}, u32[]{:S(2)}) copy-start(bf16[1536,2560]{1,0:T(8,128)(2,1)} %all-gather.6.cloned.1.call-done) | copy-start | bytes 23592964
  327.4 5.9 %copy-start.21 = (bf16[2560,304]{0,1:T(8,128)(2,1)S(1)}, bf16[2560,304]{0,1:T(8,128)(2,1)}, u32[]{:S(2)}) copy-start(bf16[2560,304]{0,1:T(8,128)(2,1)} %param.26) | copy-start | bytes 4669444
  333.3 2.7 copy-start.3
  345.0 139.4 %all-to-all-start.3 = ((bf16[32,48,2688]{2,1,0:T(8,128)(2,1)}), bf16[32,48,2688]{2,1,0:T(8,128)(2,1)}, u32[]{:S(2)}, u32[]{:S(2)}) async-start(bf16[32,48,2688]{2,1,0:T(8,128)(2,1)} %constant_dynamic-update-slice_fusion), calls=%async_computation.3 | async-start | bytes 16515072 | tf_op jit(solution)/shard_map/all_to_all | solution.py:214
  355.2 141.8 %copy-start.25 = (s32[16]{0:T(128)S(1)}, s32[16]{0:T(128)}, u32[]{:S(2)}) copy-start(s32[16]{0:T(128)} %param.17) | copy-start | bytes 196
  484.4 13.4 %copy-start.1 = (bf16[2560,304]{0,1:T(8,128)(2,1)S(1)}, bf16[2560,304]{0,1:T(8,128)(2,1)}, u32[]{:S(2)}) copy-start(bf16[2560,304]{0,1:T(8,128)(2,1)} %param.25) | copy-start | bytes 4669444
  (2 other events, 1.4 us)
Sparse Core Ops, SparseCore 0:
  20.5 73.9 all-gather.3
  259.9 67.3 all-gather.5

commit v15 on v14

--- a/solution.py
+++ b/solution.py
@@ -182,8 +182,11 @@
     resid = (stream.astype(jnp.float32) + attn_sum).astype(jnp.bfloat16)
     portion = gather_rows(row_norm(resid, mlp_gain).astype(jnp.bfloat16))
     paged_key_value_cache, portion = lax.optimization_barrier((paged_key_value_cache, portion))
-    gate_rows = jnp.dot(portion, w_gate, preferred_element_type=jnp.float32)
-    upward = jnp.dot(portion, w_up, preferred_element_type=jnp.float32)
+    both = jnp.dot(
+        portion, jnp.concatenate([w_gate, w_up], axis=1), preferred_element_type=jnp.float32
+    )
+    gate_rows = both[:, : w_gate.shape[1]]
+    upward = both[:, w_gate.shape[1] :]
     hidden = (jax.nn.silu(gate_rows) * upward).astype(jnp.bfloat16)
     width = w_down.shape[1]
     feat = width // tensor_element_count

time: 505 us -> 505 us (level)
  transfers between devices with their start and end apart: 8 -> 8, of which waited for: 8 -> 8; matrix products, arithmetic and copies ran while one was open for 4% -> 3% of each run, Pallas kernels for 0% -> 0%
where the time goes in v15:
time: 505 us; the launch traced here: 504 us
  waiting for transfers between devices  365 us (72%)
  matrix products  32.3 us (6%)
  starting transfers between devices  31.6 us (6%)
  blocking collectives  24.9 us (5%)
  other arithmetic  22.3 us (4%)
  between operations  14.5 us (3%)
  local copies, waits for them, and re-layouts  13.6 us (3%)
    all_to_all x1, waiting for transfers between devices, per_device(): got = lax.all_to_all(payload, TENSOR, 0, 0, tiled=True)  129 us
    all_to_all x1, waiting for transfers between devices, scatter_sum(): got = lax.all_to_all(pieces, TENSOR, 0, 0, tiled=True)  121 us
    all_gather x2, waiting for transfers between devices, gather_rows(): return lax.all_gather(rows, ('ty', 'tx'), axis=0, tiled=True)  80.5 us
    ppermute x2, waiting for transfers between devices, partner_2(): return lax.ppermute(value, axis, pairs)  26.7 us
    all_gather x2, blocking collectives, gather_rows(): rows = lax.all_gather(rows, 'tz', axis=0, tiled=True)  18.2 us
  transfers between devices with their start and end apart: 8, of which 8 were waited for; matrix products, arithmetic and copies ran while one was open for 3% of the time, Pallas kernels for 0%

profile of v15, /device:TPU:27, one launch (start us, length us, event | category | flops | bytes accessed | tf_op | source)
XLA Modules:
  0.0 504.4 jit_solution(18431551448405183028)
XLA Ops:
  7.3 1.2 fusion.63
  9.2 1.1 fusion.65
  10.3 10.0 %all_gather.15 = bf16[96,2560]{1,0:T(8,128)(2,1)} all-gather(bf16[48,2560]{1,0:T(8,128)(2,1)S(1)} %fusion.65), channel_id=1, replica_groups=mesh['dp'=4,'ty'=4,'tx'=4,'tz'=2] {'tz'}, dimensions={0}, use_global_device_ids=true | all-gather | bytes 737280 | tf_op jit(solution)/shard_map/all_gather | solution.py:32
  20.3 2.8 collective-permute-start
  24.7 1.1 copy.29
  25.9 4.3 collective-permute-done
  30.6 22.5 %collective-permute-done.1 = bf16[2560,128]{0,1:T(8,128)(2,1)S(1)} collective-permute-done((bf16[2560,128]{0,1:T(8,128)(2,1)S(1)}, bf16[2560,128]{0,1:T(8,128)(2,1)S(1)}, u32[]{:S(2)}, u32[]{:S(2)}) %collective-permute-start.1) | collective-permute-done | bytes 655392 | tf_op jit(solution)/shard_map/ppermute | solution.py:22
  53.4 41.0 %all-gather.4.cloned.1.call-done = bf16[1536,2560]{1,0:T(8,128)(2,1)} async-done(((bf16[96,2560]{1,0:T(8,128)(2,1)}), bf16[1536,2560]{1,0:T(8,128)(2,1)}) %all-gather.4.cloned.1.call-update) | async-done | bytes 7864336 | tf_op jit(solution)/shard_map/all_gather | solution.py:33
  94.4 5.7 %fusion.129 = (bf16[1536,384]{0,1:T(8,128)(2,1)S(1)}, f32[1536,384]{0,1:T(8,128)S(1)}) fusion(bf16[1536,2560]{1,0:T(8,128)(2,1)} %all-gather.4.cloned.1.call-done, bf16[2560,256]{0,1:T(8,128)(2,1)S(1)} %maximum_select_fusion, bf16[2560,128]{0,1:T(8,128)(2,1)} %copy.29), kind=kOutput, calls=%fused_computation.199 | convolution fusion | flops 3024420864 | bytes 13369344 | tf_op jit(solution)/shard_map/dot_general | solution.py:101
  100.6 1.7 fusion.76
  107.1 1.3 fusion.9
  108.4 1.3 fusion.33
  109.7 5.3 %convolution_convert_fusion.1 = bf16[1536,2560]{1,0:T(8,128)(2,1)} fusion(bf16[1536,128]{1,0:T(8,128)(2,1)S(1)} %bitcast.120, bf16[128,2560]{1,0:T(8,128)(2,1)S(1)} %copy-done), kind=kOutput, calls=%fused_computation.7 | convolution fusion | flops 1010565120 | bytes 8912896 | tf_op jit(solution)/shard_map/dot_general | solution.py:179
  115.1 9.4 %all-to-all-start = ((bf16[32,48,2560]{2,1,0:T(8,128)(2,1)}), bf16[32,48,2560]{2,1,0:T(8,128)(2,1)}, u32[]{:S(2)}, u32[]{:S(2)}) async-start(bf16[32,48,2560]{2,1,0:T(8,128)(2,1)} %bitcast.118), calls=%async_computation | async-start | bytes 15728640 | tf_op jit(solution)/shard_map/all_to_all | solution.py:27
  124.7 121.3 %all-to-all-done = bf16[32,48,2560]{2,1,0:T(8,128)(2,1)} async-done(((bf16[32,48,2560]{2,1,0:T(8,128)(2,1)}), bf16[32,48,2560]{2,1,0:T(8,128)(2,1)}, u32[]{:S(2)}, u32[]{:S(2)}) %all-to-all-start) | async-done | bytes 7864352 | tf_op jit(solution)/shard_map/all_to_all | solution.py:27
  246.0 4.5 convert_reduce_fusion.1
  250.9 8.2 %all_gather.17 = bf16[96,2560]{1,0:T(8,128)(2,1)} all-gather(bf16[48,2560]{1,0:T(8,128)(2,1)S(1)} %fusion.69), channel_id=1, replica_groups=mesh['dp'=4,'ty'=4,'tx'=4,'tz'=2] {'tz'}, dimensions={0}, use_global_device_ids=true | all-gather | bytes 737280 | tf_op jit(solution)/shard_map/all_gather | solution.py:32
  260.4 1.2 gather_fusion
  262.3 5.6 %all-to-all-start.1 = ((s32[4,1,24]{2,1,0:T(1,128)}), s32[4,1,24]{2,1,0:T(1,128)S(1)}, u32[]{:S(2)}, u32[]{:S(2)}) async-start(s32[4,1,24]{2,1,0:T(1,128)} %bitcast.30), calls=%async_computation.1 | async-start | bytes 4096 | tf_op jit(solution)/shard_map/all_to_all | solution.py:136
  268.0 3.0 all-to-all-done.1
  273.4 1.0 reshape.700
  274.4 4.0 all-to-all-start.2
  278.4 4.5 all-to-all-done.2
  283.2 3.5 scatter_fusion
  287.2 39.5 %all-gather.6.cloned.1.call-done = bf16[1536,2560]{1,0:T(8,128)(2,1)} async-done(((bf16[96,2560]{1,0:T(8,128)(2,1)}), bf16[1536,2560]{1,0:T(8,128)(2,1)}) %all-gather.6.cloned.1.call-update) | async-done | bytes 7864336 | tf_op jit(solution)/shard_map/all_gather | solution.py:33
  326.6 7.8 %fusion.2 = f32[1536,608]{0,1:T(8,128)S(1)} fusion(bf16[1536,2560]{1,0:T(8,128)(2,1)} %all-gather.6.cloned.1.call-done, bf16[2560,304]{0,1:T(8,128)(2,1)S(1)} %copy-done.7, bf16[2560,304]{0,1:T(8,128)(2,1)} %param.25), kind=kOutput, calls=%fused_computation.16 | convolution fusion | flops 4787732480 | bytes 14712832 | tf_op jit(solution)/shard_map/dot_general | solution.py:185
  336.8 6.8 %convolution_convert_fusion = bf16[1536,2688]{1,0:T(8,128)(2,1)} fusion(bf16[1536,304]{0,1:T(8,128)(2,1)S(1)} %fusion.15, bf16[304,2560]{1,0:T(8,128)(2,1)S(1)} %copy-done.3), kind=kOutput, calls=%fused_computation.6 | convolution fusion | flops 2514419712 | bytes 10747904 | tf_op jit(solution)/shard_map/dot_general | solution.py:211
  344.8 9.2 %all-to-all-start.3 = ((bf16[32,48,2688]{2,1,0:T(8,128)(2,1)}), bf16[32,48,2688]{2,1,0:T(8,128)(2,1)}, u32[]{:S(2)}, u32[]{:S(2)}) async-start(bf16[32,48,2688]{2,1,0:T(8,128)(2,1)} %constant_dynamic-update-slice_fusion), calls=%async_computation.3 | async-start | bytes 16515072 | tf_op jit(solution)/shard_map/all_to_all | solution.py:217
  354.0 1.1 copy.34
  355.1 129.1 %all-to-all-done.3 = bf16[32,48,2688]{2,1,0:T(8,128)(2,1)} async-done(((bf16[32,48,2688]{2,1,0:T(8,128)(2,1)}), bf16[32,48,2688]{2,1,0:T(8,128)(2,1)}, u32[]{:S(2)}, u32[]{:S(2)}) %all-to-all-start.3) | async-done | bytes 8257568 | tf_op jit(solution)/shard_map/all_to_all | solution.py:217
  484.2 5.0 convert_reduce_fusion
  490.1 6.7 %all-gather = bf16[4,6,80]{2,1,0:T(8,128)(2,1)S(1)} all-gather(bf16[1,6,80]{2,1,0:T(8,128)(2,1)S(1)} %reshape.686), channel_id=1, replica_groups=mesh['dp'=4,'ty'=4,'tx'=4,'tz'=2] {'dp'}, dimensions={0}, use_global_device_ids=true | all-gather | bytes 4800 | tf_op jit(solution)/shard_map/all_gather | solution.py:227
  (103 shorter events, 19.3 us)
Async XLA Ops:
  7.2 102.5 %copy-start = (bf16[128,2560]{1,0:T(8,128)(2,1)S(1)}, bf16[128,2560]{1,0:T(8,128)(2,1)}, u32[]{:S(2)}) copy-start(bf16[128,2560]{1,0:T(8,128)(2,1)} %param.24) | copy-start | bytes 1966084
  7.2 22.9 %copy-start.5 = (bf16[2560,64]{0,1:T(8,128)(2,1)S(1)}, bf16[2560,64]{0,1:T(8,128)(2,1)}, u32[]{:S(2)}) copy-start(bf16[2560,64]{0,1:T(8,128)(2,1)} %param.23) | copy-start | bytes 983044
  7.2 17.4 %copy-start.9 = (s32[1,6]{1,0:T(1,128)S(1)}, s32[1,6]{1,0:T(1,128)}, u32[]{:S(2)}) copy-start(s32[1,6]{1,0:T(1,128)} %param.15) | copy-start | bytes 76
  7.2 17.4 %copy-start.8 = (bf16[128]{0:T(256)(128)(2,1)S(1)}, bf16[128]{0:T(256)(128)(2,1)}, u32[]{:S(2)}) copy-start(bf16[128]{0:T(256)(128)(2,1)} %param.20) | copy-start | bytes 772
  7.2 17.5 %copy-start.4 = (bf16[2560,128]{1,0:T(8,128)(2,1)S(1)}, bf16[2560,128]{1,0:T(8,128)(2,1)}, u32[]{:S(2)}) copy-start(bf16[2560,128]{1,0:T(8,128)(2,1)} %param.22) | copy-start | bytes 1966084
  7.2 87.2 %all-gather.4.cloned.1.call-start = ((), (), s32[]{:S(2)}) async-start(), calls=%async_computation.4 | async-start | bytes 8355840 | tf_op jit(solution)/shard_map/all_gather | solution.py:33
  20.3 9.8 %collective-permute-start = (bf16[2560,64]{0,1:T(8,128)(2,1)}, bf16[2560,64]{0,1:T(8,128)(2,1)S(1)}, u32[]{:S(2)}, u32[]{:S(2)}) collective-permute-start(bf16[2560,64]{0,1:T(8,128)(2,1)} %param.23), channel_id=1, source_target_pairs={{0,1},{1,0},{2,3},{3,2},{4,5},{5,4},{6,7},{7,6},{8,9},{9,8},{10,11... | collective-permute-start | bytes 983048 | tf_op jit(solution)/shard_map/ppermute | solution.py:22
  30.2 22.9 %collective-permute-start.1 = (bf16[2560,128]{0,1:T(8,128)(2,1)S(1)}, bf16[2560,128]{0,1:T(8,128)(2,1)S(1)}, u32[]{:S(2)}, u32[]{:S(2)}) collective-permute-start(bf16[2560,128]{0,1:T(8,128)(2,1)S(1)} %maximum_select_fusion.1), channel_id=1, source_target_pairs={{0,2},{1,3},{2,0},{3,1},{4,6},{5,7},{6,4},{7,5},{8,10},{9,11},{10,... | collective-permute-start | bytes 1966088 | tf_op jit(solution)/shard_map/ppermute | solution.py:22
  115.1 9.6 %copy-start.6 = (bf16[2560]{0:T(1024)(128)(2,1)S(1)}, bf16[2560]{0:T(1024)(128)(2,1)}, u32[]{:S(2)}) copy-start(bf16[2560]{0:T(1024)(128)(2,1)} %param.21) | copy-start | bytes 15364
  115.1 130.9 %all-to-all-start = ((bf16[32,48,2560]{2,1,0:T(8,128)(2,1)}), bf16[32,48,2560]{2,1,0:T(8,128)(2,1)}, u32[]{:S(2)}, u32[]{:S(2)}) async-start(bf16[32,48,2560]{2,1,0:T(8,128)(2,1)} %bitcast.118), calls=%async_computation | async-start | bytes 15728640 | tf_op jit(solution)/shard_map/all_to_all | solution.py:27
  124.4 202.2 %all-gather.6.cloned.1.call-start = ((), (), s32[]{:S(2)}) async-start(), calls=%async_computation.5 | async-start | bytes 8355840 | tf_op jit(solution)/shard_map/all_gather | solution.py:33
  124.7 125.8 %copy-start.2 = (bf16[48,2560]{1,0:T(8,128)(2,1)S(1)}, bf16[48,2560]{1,0:T(8,128)(2,1)}, u32[]{:S(2)}) copy-start(bf16[48,2560]{1,0:T(8,128)(2,1)} %param.14) | copy-start | bytes 737284
  250.5 8.6 %copy-start.10 = (s32[96]{0:T(128)S(1)}, s32[96]{0:T(128)}, u32[]{:S(2)}) copy-start(s32[96]{0:T(128)} %param.16) | copy-start | bytes 1156
  262.3 8.7 %all-to-all-start.1 = ((s32[4,1,24]{2,1,0:T(1,128)}), s32[4,1,24]{2,1,0:T(1,128)S(1)}, u32[]{:S(2)}, u32[]{:S(2)}) async-start(s32[4,1,24]{2,1,0:T(1,128)} %bitcast.30), calls=%async_computation.1 | async-start | bytes 4096 | tf_op jit(solution)/shard_map/all_to_all | solution.py:136
  272.7 53.9 %copy-start.7 = (bf16[2560,304]{0,1:T(8,128)(2,1)S(1)}, bf16[2560,304]{0,1:T(8,128)(2,1)}, u32[]{:S(2)}) copy-start(bf16[2560,304]{0,1:T(8,128)(2,1)} %param.26) | copy-start | bytes 4669444
  274.4 8.5 %all-to-all-start.2 = ((bf16[4,2,12288]{2,1,0:T(2,128)(2,1)}), bf16[4,2,12288]{2,1,0:T(2,128)(2,1)S(1)}, u32[]{:S(2)}, u32[]{:S(2)}) async-start(bf16[4,2,12288]{2,1,0:T(2,128)(2,1)} %reshape.700), calls=%async_computation.2 | async-start | bytes 393216 | tf_op jit(solution)/shard_map/all_to_all | solution.py:135
  334.4 1.4 copy-start.3
  344.8 139.4 %all-to-all-start.3 = ((bf16[32,48,2688]{2,1,0:T(8,128)(2,1)}), bf16[32,48,2688]{2,1,0:T(8,128)(2,1)}, u32[]{:S(2)}, u32[]{:S(2)}) async-start(bf16[32,48,2688]{2,1,0:T(8,128)(2,1)} %constant_dynamic-update-slice_fusion), calls=%async_computation.3 | async-start | bytes 16515072 | tf_op jit(solution)/shard_map/all_to_all | solution.py:217
  355.1 141.6 %copy-start.11 = (s32[16]{0:T(128)S(1)}, s32[16]{0:T(128)}, u32[]{:S(2)}) copy-start(s32[16]{0:T(128)} %param.17) | copy-start | bytes 196
  484.2 13.3 %copy-start.1 = (bf16[128,2560]{1,0:T(8,128)(2,1)S(1)}, bf16[128,2560]{1,0:T(8,128)(2,1)}, u32[]{:S(2)}) copy-start(bf16[128,2560]{1,0:T(8,128)(2,1)} %param.24) | copy-start | bytes 1966084
Sparse Core Ops, SparseCore 0:
  20.4 73.9 all-gather.3
  259.2 67.3 all-gather.5

commit v16 on v15

--- a/solution.py
+++ b/solution.py
@@ -149,18 +149,22 @@
     def dense_block(block_index):
         first_row = block_index * block_rows
         key_count = first_row + block_rows
+        key_first = max(0, first_row - 768)
         q_block = q_rot[first_row:key_count]
         q_prompt = prompt[first_row:key_count]
         row_ids = first_row + local_ids
         scores = (
             jnp.einsum(
-                "qhd,kd->hqk", q_block, key_flat[:key_count], preferred_element_type=jnp.float32
+                "qhd,kd->hqk",
+                q_block,
+                key_flat[key_first:key_count],
+                preferred_element_type=jnp.float32,
             )
             / score_scale
         )
         allowed = (
-            (q_prompt[:, None] == prompt[None, :key_count])
-            & (row_ids[:, None] >= all_ids[None, :key_count])
+            (q_prompt[:, None] == prompt[None, key_first:key_count])
+            & (row_ids[:, None] >= all_ids[None, key_first:key_count])
         )[None]
         peak = jnp.max(jnp.where(allowed, scores, -jnp.inf), axis=2, keepdims=True)
         weight = jnp.where(allowed, jnp.exp(scores - peak), 0.0)
@@ -168,7 +172,7 @@
         running = jnp.einsum(
             "hqk,kd->hqd",
             weight.astype(jnp.bfloat16),
-            value_matrix_rows[:key_count],
+            value_matrix_rows[key_first:key_count],
             preferred_element_type=jnp.float32,
         )
         return (running / total_weight).astype(jnp.bfloat16)

time: 505 us -> 504 us (level)
  no operation moved by 1% of the time
where the time goes in v16:
time: 504 us; the launch traced here: 503 us
  waiting for transfers between devices  365 us (72%)
  matrix products  32 us (6%)
  starting transfers between devices  31.4 us (6%)
  blocking collectives  24.9 us (5%)
  other arithmetic  22 us (4%)
  between operations  14.6 us (3%)
  local copies, waits for them, and re-layouts  13.6 us (3%)
    all_to_all x1, waiting for transfers between devices, per_device(): got = lax.all_to_all(payload, TENSOR, 0, 0, tiled=True)  128 us
    all_to_all x1, waiting for transfers between devices, scatter_sum(): got = lax.all_to_all(pieces, TENSOR, 0, 0, tiled=True)  122 us
    all_gather x2, waiting for transfers between devices, gather_rows(): return lax.all_gather(rows, ('ty', 'tx'), axis=0, tiled=True)  80.6 us
    ppermute x2, waiting for transfers between devices, partner_2(): return lax.ppermute(value, axis, pairs)  26.7 us
    all_gather x2, blocking collectives, gather_rows(): rows = lax.all_gather(rows, 'tz', axis=0, tiled=True)  18.2 us
  transfers between devices with their start and end apart: 8, of which 8 were waited for; matrix products, arithmetic and copies ran while one was open for 3% of the time, Pallas kernels for 0%

profile of v16, /device:TPU:27, one launch (start us, length us, event | category | flops | bytes accessed | tf_op | source)
XLA Modules:
  0.0 503.3 jit_solution(10188079126482272437)
XLA Ops:
  7.3 1.2 fusion.62
  9.2 1.1 fusion.64
  10.3 10.0 %all_gather.15 = bf16[96,2560]{1,0:T(8,128)(2,1)} all-gather(bf16[48,2560]{1,0:T(8,128)(2,1)S(1)} %fusion.64), channel_id=1, replica_groups=mesh['dp'=4,'ty'=4,'tx'=4,'tz'=2] {'tz'}, dimensions={0}, use_global_device_ids=true | all-gather | bytes 737280 | tf_op jit(solution)/shard_map/all_gather | solution.py:32
  20.3 2.8 collective-permute-start
  24.8 1.1 copy.29
  25.9 4.2 collective-permute-done
  30.6 22.5 %collective-permute-done.1 = bf16[2560,128]{0,1:T(8,128)(2,1)S(1)} collective-permute-done((bf16[2560,128]{0,1:T(8,128)(2,1)S(1)}, bf16[2560,128]{0,1:T(8,128)(2,1)S(1)}, u32[]{:S(2)}, u32[]{:S(2)}) %collective-permute-start.1) | collective-permute-done | bytes 655392 | tf_op jit(solution)/shard_map/ppermute | solution.py:22
  53.4 41.0 %all-gather.4.cloned.1.call-done = bf16[1536,2560]{1,0:T(8,128)(2,1)} async-done(((bf16[96,2560]{1,0:T(8,128)(2,1)}), bf16[1536,2560]{1,0:T(8,128)(2,1)}) %all-gather.4.cloned.1.call-update) | async-done | bytes 7864336 | tf_op jit(solution)/shard_map/all_gather | solution.py:33
  94.4 5.7 %fusion.129 = (bf16[1536,384]{0,1:T(8,128)(2,1)S(1)}, f32[1536,384]{0,1:T(8,128)S(1)}) fusion(bf16[1536,2560]{1,0:T(8,128)(2,1)} %all-gather.4.cloned.1.call-done, bf16[2560,256]{0,1:T(8,128)(2,1)S(1)} %maximum_select_fusion, bf16[2560,128]{0,1:T(8,128)(2,1)} %copy.29), kind=kOutput, calls=%fused_computation.201 | convolution fusion | flops 3024420864 | bytes 13369344 | tf_op jit(solution)/shard_map/dot_general | solution.py:101
  100.6 1.7 fusion.75
  106.9 1.0 fusion.13
  107.9 1.1 fusion.32
  109.1 5.4 %convolution_convert_fusion.1 = bf16[1536,2560]{1,0:T(8,128)(2,1)} fusion(bf16[1536,128]{1,0:T(8,128)(2,1)S(1)} %bitcast.125, bf16[128,2560]{1,0:T(8,128)(2,1)S(1)} %copy-done), kind=kOutput, calls=%fused_computation.7 | convolution fusion | flops 1010565120 | bytes 8912896 | tf_op jit(solution)/shard_map/dot_general | solution.py:183
  114.4 9.3 %all-to-all-start = ((bf16[32,48,2560]{2,1,0:T(8,128)(2,1)}), bf16[32,48,2560]{2,1,0:T(8,128)(2,1)}, u32[]{:S(2)}, u32[]{:S(2)}) async-start(bf16[32,48,2560]{2,1,0:T(8,128)(2,1)} %bitcast.123), calls=%async_computation | async-start | bytes 15728640 | tf_op jit(solution)/shard_map/all_to_all | solution.py:27
  123.8 121.6 %all-to-all-done = bf16[32,48,2560]{2,1,0:T(8,128)(2,1)} async-done(((bf16[32,48,2560]{2,1,0:T(8,128)(2,1)}), bf16[32,48,2560]{2,1,0:T(8,128)(2,1)}, u32[]{:S(2)}, u32[]{:S(2)}) %all-to-all-start) | async-done | bytes 7864352 | tf_op jit(solution)/shard_map/all_to_all | solution.py:27
  245.4 4.5 convert_reduce_fusion.1
  250.3 8.2 %all_gather.17 = bf16[96,2560]{1,0:T(8,128)(2,1)} all-gather(bf16[48,2560]{1,0:T(8,128)(2,1)S(1)} %fusion.68), channel_id=1, replica_groups=mesh['dp'=4,'ty'=4,'tx'=4,'tz'=2] {'tz'}, dimensions={0}, use_global_device_ids=true | all-gather | bytes 737280 | tf_op jit(solution)/shard_map/all_gather | solution.py:32
  259.9 1.2 gather_fusion
  261.8 5.6 %all-to-all-start.1 = ((s32[4,1,24]{2,1,0:T(1,128)}), s32[4,1,24]{2,1,0:T(1,128)S(1)}, u32[]{:S(2)}, u32[]{:S(2)}) async-start(s32[4,1,24]{2,1,0:T(1,128)} %bitcast.29), calls=%async_computation.1 | async-start | bytes 4096 | tf_op jit(solution)/shard_map/all_to_all | solution.py:136
  267.4 3.0 all-to-all-done.1
  272.8 1.0 reshape.716
  273.8 4.0 all-to-all-start.2
  277.8 4.5 all-to-all-done.2
  282.7 3.5 scatter_fusion
  286.6 39.5 %all-gather.6.cloned.1.call-done = bf16[1536,2560]{1,0:T(8,128)(2,1)} async-done(((bf16[96,2560]{1,0:T(8,128)(2,1)}), bf16[1536,2560]{1,0:T(8,128)(2,1)}) %all-gather.6.cloned.1.call-update) | async-done | bytes 7864336 | tf_op jit(solution)/shard_map/all_gather | solution.py:33
  326.2 7.8 %fusion.1 = f32[1536,608]{0,1:T(8,128)S(1)} fusion(bf16[1536,2560]{1,0:T(8,128)(2,1)} %all-gather.6.cloned.1.call-done, bf16[2560,304]{0,1:T(8,128)(2,1)S(1)} %copy-done.7, bf16[2560,304]{0,1:T(8,128)(2,1)} %param.25), kind=kOutput, calls=%fused_computation.12 | convolution fusion | flops 4787732480 | bytes 14712832 | tf_op jit(solution)/shard_map/dot_general | solution.py:189
  336.3 6.8 %convolution_convert_fusion = bf16[1536,2688]{1,0:T(8,128)(2,1)} fusion(bf16[1536,304]{0,1:T(8,128)(2,1)S(1)} %fusion.12, bf16[304,2560]{1,0:T(8,128)(2,1)S(1)} %copy-done.3), kind=kOutput, calls=%fused_computation.6 | convolution fusion | flops 2514419712 | bytes 10747904 | tf_op jit(solution)/shard_map/dot_general | solution.py:215
  344.4 9.2 %all-to-all-start.3 = ((bf16[32,48,2688]{2,1,0:T(8,128)(2,1)}), bf16[32,48,2688]{2,1,0:T(8,128)(2,1)}, u32[]{:S(2)}, u32[]{:S(2)}) async-start(bf16[32,48,2688]{2,1,0:T(8,128)(2,1)} %constant_dynamic-update-slice_fusion), calls=%async_computation.3 | async-start | bytes 16515072 | tf_op jit(solution)/shard_map/all_to_all | solution.py:221
  353.6 1.1 copy.34
  354.6 128.5 %all-to-all-done.3 = bf16[32,48,2688]{2,1,0:T(8,128)(2,1)} async-done(((bf16[32,48,2688]{2,1,0:T(8,128)(2,1)}), bf16[32,48,2688]{2,1,0:T(8,128)(2,1)}, u32[]{:S(2)}, u32[]{:S(2)}) %all-to-all-start.3) | async-done | bytes 8257568 | tf_op jit(solution)/shard_map/all_to_all | solution.py:221
  483.1 5.0 convert_reduce_fusion
  489.0 6.7 %all-gather = bf16[4,6,80]{2,1,0:T(8,128)(2,1)S(1)} all-gather(bf16[1,6,80]{2,1,0:T(8,128)(2,1)S(1)} %reshape.702), channel_id=1, replica_groups=mesh['dp'=4,'ty'=4,'tx'=4,'tz'=2] {'dp'}, dimensions={0}, use_global_device_ids=true | all-gather | bytes 4800 | tf_op jit(solution)/shard_map/all_gather | solution.py:231
  (105 shorter events, 19.0 us)
Async XLA Ops:
  7.2 101.9 %copy-start = (bf16[128,2560]{1,0:T(8,128)(2,1)S(1)}, bf16[128,2560]{1,0:T(8,128)(2,1)}, u32[]{:S(2)}) copy-start(bf16[128,2560]{1,0:T(8,128)(2,1)} %param.24) | copy-start | bytes 1966084
  7.2 22.9 %copy-start.5 = (bf16[2560,64]{0,1:T(8,128)(2,1)S(1)}, bf16[2560,64]{0,1:T(8,128)(2,1)}, u32[]{:S(2)}) copy-start(bf16[2560,64]{0,1:T(8,128)(2,1)} %param.23) | copy-start | bytes 983044
  7.2 17.5 %copy-start.8 = (bf16[128]{0:T(256)(128)(2,1)S(1)}, bf16[128]{0:T(256)(128)(2,1)}, u32[]{:S(2)}) copy-start(bf16[128]{0:T(256)(128)(2,1)} %param.19) | copy-start | bytes 772
  7.2 17.5 %copy-start.9 = (bf16[128]{0:T(256)(128)(2,1)S(1)}, bf16[128]{0:T(256)(128)(2,1)}, u32[]{:S(2)}) copy-start(bf16[128]{0:T(256)(128)(2,1)} %param.20) | copy-start | bytes 772
  7.2 17.5 %copy-start.4 = (bf16[2560,128]{1,0:T(8,128)(2,1)S(1)}, bf16[2560,128]{1,0:T(8,128)(2,1)}, u32[]{:S(2)}) copy-start(bf16[2560,128]{1,0:T(8,128)(2,1)} %param.22) | copy-start | bytes 1966084
  7.2 87.2 %all-gather.4.cloned.1.call-start = ((), (), s32[]{:S(2)}) async-start(), calls=%async_computation.4 | async-start | bytes 8355840 | tf_op jit(solution)/shard_map/all_gather | solution.py:33
  20.3 9.8 %collective-permute-start = (bf16[2560,64]{0,1:T(8,128)(2,1)}, bf16[2560,64]{0,1:T(8,128)(2,1)S(1)}, u32[]{:S(2)}, u32[]{:S(2)}) collective-permute-start(bf16[2560,64]{0,1:T(8,128)(2,1)} %param.23), channel_id=1, source_target_pairs={{0,1},{1,0},{2,3},{3,2},{4,5},{5,4},{6,7},{7,6},{8,9},{9,8},{10,11... | collective-permute-start | bytes 983048 | tf_op jit(solution)/shard_map/ppermute | solution.py:22
  30.2 22.9 %collective-permute-start.1 = (bf16[2560,128]{0,1:T(8,128)(2,1)S(1)}, bf16[2560,128]{0,1:T(8,128)(2,1)S(1)}, u32[]{:S(2)}, u32[]{:S(2)}) collective-permute-start(bf16[2560,128]{0,1:T(8,128)(2,1)S(1)} %maximum_select_fusion.1), channel_id=1, source_target_pairs={{0,2},{1,3},{2,0},{3,1},{4,6},{5,7},{6,4},{7,5},{8,10},{9,11},{10,... | collective-permute-start | bytes 1966088 | tf_op jit(solution)/shard_map/ppermute | solution.py:22
  114.4 9.4 %copy-start.6 = (bf16[2560]{0:T(1024)(128)(2,1)S(1)}, bf16[2560]{0:T(1024)(128)(2,1)}, u32[]{:S(2)}) copy-start(bf16[2560]{0:T(1024)(128)(2,1)} %param.21) | copy-start | bytes 15364
  114.4 131.0 %all-to-all-start = ((bf16[32,48,2560]{2,1,0:T(8,128)(2,1)}), bf16[32,48,2560]{2,1,0:T(8,128)(2,1)}, u32[]{:S(2)}, u32[]{:S(2)}) async-start(bf16[32,48,2560]{2,1,0:T(8,128)(2,1)} %bitcast.123), calls=%async_computation | async-start | bytes 15728640 | tf_op jit(solution)/shard_map/all_to_all | solution.py:27
  123.7 202.4 %all-gather.6.cloned.1.call-start = ((), (), s32[]{:S(2)}) async-start(), calls=%async_computation.5 | async-start | bytes 8355840 | tf_op jit(solution)/shard_map/all_gather | solution.py:33
  123.8 126.1 %copy-start.2 = (bf16[48,2560]{1,0:T(8,128)(2,1)S(1)}, bf16[48,2560]{1,0:T(8,128)(2,1)}, u32[]{:S(2)}) copy-start(bf16[48,2560]{1,0:T(8,128)(2,1)} %param.14) | copy-start | bytes 737284
  250.0 8.6 %copy-start.10 = (s32[96]{0:T(128)S(1)}, s32[96]{0:T(128)}, u32[]{:S(2)}) copy-start(s32[96]{0:T(128)} %param.16) | copy-start | bytes 1156
  261.8 8.7 %all-to-all-start.1 = ((s32[4,1,24]{2,1,0:T(1,128)}), s32[4,1,24]{2,1,0:T(1,128)S(1)}, u32[]{:S(2)}, u32[]{:S(2)}) async-start(s32[4,1,24]{2,1,0:T(1,128)} %bitcast.29), calls=%async_computation.1 | async-start | bytes 4096 | tf_op jit(solution)/shard_map/all_to_all | solution.py:136
  272.1 54.0 %copy-start.7 = (bf16[2560,304]{0,1:T(8,128)(2,1)S(1)}, bf16[2560,304]{0,1:T(8,128)(2,1)}, u32[]{:S(2)}) copy-start(bf16[2560,304]{0,1:T(8,128)(2,1)} %param.26) | copy-start | bytes 4669444
  273.8 8.5 %all-to-all-start.2 = ((bf16[4,2,12288]{2,1,0:T(2,128)(2,1)}), bf16[4,2,12288]{2,1,0:T(2,128)(2,1)S(1)}, u32[]{:S(2)}, u32[]{:S(2)}) async-start(bf16[4,2,12288]{2,1,0:T(2,128)(2,1)} %reshape.716), calls=%async_computation.2 | async-start | bytes 393216 | tf_op jit(solution)/shard_map/all_to_all | solution.py:135
  334.0 1.4 copy-start.3
  344.4 138.7 %all-to-all-start.3 = ((bf16[32,48,2688]{2,1,0:T(8,128)(2,1)}), bf16[32,48,2688]{2,1,0:T(8,128)(2,1)}, u32[]{:S(2)}, u32[]{:S(2)}) async-start(bf16[32,48,2688]{2,1,0:T(8,128)(2,1)} %constant_dynamic-update-slice_fusion), calls=%async_computation.3 | async-start | bytes 16515072 | tf_op jit(solution)/shard_map/all_to_all | solution.py:221
  354.6 141.0 %copy-start.11 = (s32[16]{0:T(128)S(1)}, s32[16]{0:T(128)}, u32[]{:S(2)}) copy-start(s32[16]{0:T(128)} %param.17) | copy-start | bytes 196
  483.1 13.3 %copy-start.1 = (bf16[128,2560]{1,0:T(8,128)(2,1)S(1)}, bf16[128,2560]{1,0:T(8,128)(2,1)}, u32[]{:S(2)}) copy-start(bf16[128,2560]{1,0:T(8,128)(2,1)} %param.24) | copy-start | bytes 1966084
Sparse Core Ops, SparseCore 0:
  20.4 73.9 all-gather.3
  258.7 67.4 all-gather.5
